TPU v7x, 128 devices: a whole 4x4x4 slice. The times are simulated.
128 devices in a mesh: req: 64 (over z, y, x), blk: 2 (over core).
Axes of the slice: x: 4, y: 4, z: 4, core: 2. Of those that a mesh axis runs over, the one named last changes fastest.
Arguments:
- normed: bfloat16 [32768, 1536], P('req', 'blk'), may hold values from -6 to 6
- router: bfloat16 [1536, 64], P('blk'), may hold values from -0.15625 to 0.15625
- adapter_down: bfloat16 [1536, 256], P('blk'), may hold values from -0.15625 to 0.15625
- adapter_up: bfloat16 [256, 1536], P(None, 'blk'), may hold values from -1.5 to 1.5
- shared_gate_up: bfloat16 [1536, 2, 1024], P(None, None, 'blk'), may hold values from -0.15625 to 0.15625
- shared_down: bfloat16 [1024, 1536], P('blk'), may hold values from -0.1875 to 0.1875
- expert_gate_up: bfloat16 [64, 1536, 1024], P('req', 'blk'), may hold values from -0.15625 to 0.15625
- expert_down: bfloat16 [64, 512, 1536], P('req', None, 'blk'), may hold values from -0.25 to 0.25
- lengths: int32 [64, 4], P('req'), may hold values from 1 to 256, 512 in all within a row
- adapter_ids: int32 [64, 4], P('req'), may hold values from 0 to 15
- routes: int32 [32768, 6], P('req'), may hold values from 0 to 63, all different within a row; in each aligned block of 512 rows (0 to 511, 512 to 1023, ...) at most 52 rows name the same one
Outputs:
- mixed: bfloat16 [32768, 1536], P('req', 'blk')
Inputs may be any that keep to these rules, and one draw needn't show every extreme that they name: `lengths`: each row of an index of req lists its 4 prompts in token order; they sum to 512, the longest is 256. `routes`: each row names 6 different experts. Among the 512 rows of one index of req no expert is named more than 52 times, a bound that some block reaches.
All inputs are finite; a program needn't handle non-finite values.
Results may differ from a plain program's by a relative error of at most 0.013.
Values may be sent and summed in bfloat16 or wider, within the bound.
No kernel may reach another device: no remote copies, remote signals or barrier semaphores. Data moves between devices by JAX's collectives and lax.ppermute only.
A program may use at most 128 MiB of HBM per device.

v0:
```python
import jax
import jax.numpy as jnp
from jax import lax
from jax.sharding import PartitionSpec as P

RANK = 16


def slot_table(target, source_row, total_slots):
    source_slot = jnp.zeros((total_slots,), jnp.int32).at[target].set(source_row)
    filled = jnp.zeros((total_slots,), jnp.int32).at[target].set(1)
    return (source_slot, filled)


def body(
    normed,
    router,
    adapter_down,
    adapter_up,
    shared_gate_up,
    shared_down,
    expert_gate_up,
    expert_down,
    lengths,
    adapter_ids,
    routes,
):
    tok_rows = normed.shape[0]
    feat_local = normed.shape[1]
    top_count = routes.shape[1]
    req_count = lax.axis_size("req")
    expert_count = req_count * expert_gate_up.shape[0]
    most_rows = (
        tok_rows * top_count + expert_count - 1
    ) // expert_count + tok_rows * top_count // (12 * expert_count)
    slot_count = req_count * most_rows
    hidden_width = expert_down.shape[1]
    logit_part = jnp.dot(normed, router, preferred_element_type=jnp.float32)
    low_part = jnp.dot(normed, adapter_down, preferred_element_type=jnp.float32)
    logits, low_all = (
        lax.psum(logit_part.astype(jnp.bfloat16), "blk").astype(jnp.float32),
        lax.psum(low_part.astype(jnp.bfloat16), "blk").astype(jnp.float32),
    )
    ends = jnp.cumsum(lengths[0])
    position = jnp.arange(tok_rows, dtype=jnp.int32)
    request = jnp.sum((position[:, None] >= ends[None, :]).astype(jnp.int32), axis=1)
    slots_req = jnp.arange(lengths.shape[1], dtype=jnp.int32)
    adapter_token = jnp.sum(
        jnp.where(request[:, None] == slots_req[None, :], adapter_ids[0][None, :], 0), axis=1
    )
    column_owner = jnp.arange(low_all.shape[1], dtype=jnp.int32) // RANK
    low = jnp.where(column_owner[None, :] == adapter_token[:, None], low_all, 0.0).astype(
        jnp.bfloat16
    )
    delta = jnp.dot(low, adapter_up, preferred_element_type=jnp.float32)
    shared_local = shared_gate_up.shape[2]
    shared_flat = shared_gate_up.reshape(shared_gate_up.shape[0], 2 * shared_local)
    shared_pre = jnp.dot(
        lax.all_gather(normed, "blk", axis=1, tiled=True),
        shared_flat,
        preferred_element_type=jnp.float32,
    )
    shared_hidden = (
        jax.nn.silu(shared_pre[:, :shared_local]) * shared_pre[:, shared_local:]
    ).astype(jnp.bfloat16)
    shared_terms = jnp.dot(shared_hidden, shared_down, preferred_element_type=jnp.float32)
    shared_out = lax.psum_scatter(
        shared_terms.astype(jnp.bfloat16), "blk", scatter_dimension=1, tiled=True
    ).astype(jnp.float32)
    scores = jax.nn.sigmoid(logits)
    chosen = jnp.take_along_axis(scores, routes, axis=1)
    gate_weight = chosen / jnp.sum(chosen, axis=1, keepdims=True)
    flat_expert = routes.reshape(-1)
    one_hot = (flat_expert[:, None] == jnp.arange(expert_count, dtype=jnp.int32)[None, :]).astype(
        jnp.int32
    )
    earlier = jnp.cumsum(one_hot, axis=0) - one_hot
    slot_rank = jnp.sum(earlier * one_hot, axis=1)
    source_row = jnp.arange(tok_rows * top_count, dtype=jnp.int32) // top_count
    weight_gate_up = expert_gate_up[0]
    weight_down = expert_down[0]
    target = flat_expert * most_rows + slot_rank
    source_slot, filled = slot_table(target, source_row, expert_count * most_rows)
    send_rows = jnp.where(filled[:, None] > 0, normed[source_slot], jnp.zeros((), jnp.bfloat16))
    received = lax.all_to_all(
        send_rows.reshape(expert_count, most_rows, feat_local),
        "req",
        split_axis=0,
        concat_axis=0,
        tiled=True,
    )
    rows_in = received.reshape(slot_count, feat_local)
    gate_up = lax.psum_scatter(
        jnp.dot(rows_in, weight_gate_up, preferred_element_type=jnp.float32).astype(jnp.bfloat16),
        "blk",
        scatter_dimension=0,
        tiled=True,
    ).astype(jnp.float32)
    hidden = (jax.nn.silu(gate_up[:, :hidden_width]) * gate_up[:, hidden_width:]).astype(
        jnp.bfloat16
    )
    expert_out = jnp.dot(
        lax.all_gather(hidden, "blk", axis=0, tiled=True),
        weight_down,
        preferred_element_type=jnp.float32,
    ).astype(jnp.bfloat16)
    returned = lax.all_to_all(
        expert_out.reshape(req_count, most_rows, feat_local),
        "req",
        split_axis=0,
        concat_axis=0,
        tiled=True,
    )
    picked = returned.reshape(expert_count * most_rows, feat_local)[target].astype(jnp.float32)
    weighted = picked * gate_weight.reshape(-1)[:, None]
    routed = jnp.sum(weighted.reshape(tok_rows, top_count, feat_local), axis=1)
    return (shared_out + 0.5 * delta + routed).astype(jnp.bfloat16)


def solution(mesh):
    return jax.shard_map(
        body,
        mesh=mesh,
        in_specs=(
            P("req", "blk"),
            P("blk", None),
            P("blk", None),
            P(None, "blk"),
            P(None, None, "blk"),
            P("blk", None),
            P("req", "blk", None),
            P("req", None, "blk"),
            P("req", None),
            P("req", None),
            P("req", None),
        ),
        out_specs=P("req", "blk"),
        check_vma=False,
    )
```

profile of v0, /device:TPU:2, one launch (start us, length us, event | category | flops | bytes accessed | tf_op | source)
XLA Modules:
  0.0 381.9 jit_solution(10369042271794032363)
XLA Ops:
  9.5 32.0 %reduce-window.19 = s32[64,24,128]{2,1,0:T(8,128)S(1)} reduce-window(s32[64,24,128]{2,1,0:T(8,128)} %fusion.7, s32[]{:T(128)} %constant.58.clone.1), window={size=1x1x128 pad=0_0x0_0x127_0}, to_apply=%region_5.6 | reduce-window | flops 24969216 | bytes 1572868 | tf_op jit(solution)/shard_map/reduce-window.1
  47.3 11.8 %scatter_custom_fusion.1 = s32[3328]{0:T(1024)S(1)} fusion(s32[3072]{0:T(1024)S(1)} %bitcast.52, s32[3072]{0:T(1024)S(1)} %add_select_fusion, s32[]{:T(128)} %constant.58.clone.1), kind=kCustom, calls=%fused_computation.48 | custom fusion | bytes 13316 | tf_op jit(solution)/shard_map/scatter | solution.py:10
  59.1 10.8 %gather_fusion = bf16[3328,768]{1,0:T(8,128)(2,1)} fusion(bf16[512,768]{1,0:T(8,128)(2,1)S(1)} %copy-done.2, s32[4096]{0:T(1024)S(1)} %pad_clamp_fusion), kind=kCustom, calls=%fused_computation | custom fusion | bytes 10236928 | tf_op jit(solution)/shard_map/gather | solution.py:84
  70.0 7.4 %gather.13 = bf16[64,52,768]{2,1,0:T(8,128)(2,1)} reshape(bf16[3328,768]{1,0:T(8,128)(2,1)} %gather_fusion) | data formatting | bytes 10223616 | tf_op jit(solution)/shard_map/gather | solution.py:84
  77.3 11.8 %scatter_custom_fusion = s32[3328]{0:T(1024)S(1)} fusion(s32[3072]{0:T(1024)S(1)} %bitcast.53, s32[3072]{0:T(1024)S(1)} %broadcast.128, s32[]{:T(128)} %constant.58.clone.1), kind=kCustom, calls=%fused_computation.51 | custom fusion | bytes 13316 | tf_op jit(solution)/shard_map/scatter | solution.py:11
  89.3 3.6 broadcast_select_fusion
  92.9 77.0 %all_to_all.10 = bf16[64,52,768]{2,1,0:T(8,128)(2,1)} all-to-all(bf16[64,52,768]{2,1,0:T(8,128)(2,1)S(1)} %broadcast_select_fusion), channel_id=1, replica_groups=mesh['req'=64,'blk'=2] {'req'}, dimensions={0} | all-to-all | bytes 10223616 | tf_op jit(solution)/shard_map/all_to_all | solution.py:85
  169.9 7.4 %reshape.143 = bf16[3328,768]{1,0:T(8,128)(2,1)} reshape(bf16[64,52,768]{2,1,0:T(8,128)(2,1)} %all_to_all.10) | data formatting | bytes 10223616 | tf_op jit(solution)/shard_map/reshape | solution.py:92
  177.3 10.0 %convolution_convert_fusion = bf16[3328,1024]{1,0:T(8,128)(2,1)} fusion(bf16[3328,768]{1,0:T(8,128)(2,1)} %reshape.143, bf16[1,768,1024]{2,1,0:T(8,128)(2,1)S(1)} %copy-done), kind=kOutput, calls=%fused_computation.6 | convolution fusion | flops 5237899264 | bytes 13500416 | tf_op jit(solution)/shard_map/dot_general | solution.py:94
  187.5 15.8 %reduce-scatter.5.cloned.1.call-done = bf16[1664,1024]{1,0:T(8,128)(2,1)} async-done(((bf16[3328,1024]{1,0:T(8,128)(2,1)}), bf16[1664,1024]{1,0:T(8,128)(2,1)}) %reduce-scatter.5.cloned.1.call-update) | async-done | bytes 3407888 | tf_op jit(solution)/shard_map/reduce_scatter | solution.py:93
  203.3 2.8 convert_element_type.66
  208.5 16.7 %all-gather.5.cloned.1.call-done = bf16[3328,512]{1,0:T(8,128)(2,1)} async-done(((bf16[1664,512]{1,0:T(8,128)(2,1)}), bf16[3328,512]{1,0:T(8,128)(2,1)}) %all-gather.5.cloned.1.call-update) | async-done | bytes 3407888 | tf_op jit(solution)/shard_map/all_gather | solution.py:103
  225.2 7.0 %convolution_convert_fusion.1 = bf16[3328,768]{1,0:T(8,128)(2,1)} fusion(bf16[3328,512]{1,0:T(8,128)(2,1)} %all-gather.5.cloned.1.call-done, bf16[1,512,768]{2,1,0:T(8,128)(2,1)S(1)} %copy-done.9), kind=kOutput, calls=%fused_computation.7 | convolution fusion | flops 2619801600 | bytes 9306112 | tf_op jit(solution)/shard_map/dot_general | solution.py:102
  232.3 7.4 %reshape.144 = bf16[64,52,768]{2,1,0:T(8,128)(2,1)} reshape(bf16[3328,768]{1,0:T(8,128)(2,1)} %convolution_convert_fusion.1) | data formatting | bytes 10223616 | tf_op jit(solution)/shard_map/reshape | solution.py:108
  239.7 10.7 %all-to-all-start.1 = ((bf16[64,52,768]{2,1,0:T(8,128)(2,1)}), bf16[64,52,768]{2,1,0:T(8,128)(2,1)}, u32[]{:S(2)}, u32[]{:S(2)}) async-start(bf16[64,52,768]{2,1,0:T(8,128)(2,1)} %reshape.144), calls=%async_computation.3 | async-start | bytes 11010048 | tf_op jit(solution)/shard_map/all_to_all | solution.py:107
  253.6 4.5 %copy.42 = bf16[192,8,2,512]{3,1,2,0:T(8,128)(2,1)} copy(bf16[192,8,2,512]{3,2,1,0:T(2,128)(2,1)} %bitcast.47) | data formatting | bytes 6291456
  258.1 8.6 %all-gather.3.cloned.1.call-done = bf16[512,1536]{1,0:T(8,128)(2,1)} async-done(((bf16[512,768]{1,0:T(8,128)(2,1)}), bf16[512,1536]{1,0:T(8,128)(2,1)}) %all-gather.3.cloned.1.call-update) | async-done | bytes 1572880 | tf_op jit(solution)/shard_map/all_gather | solution.py:59
  266.7 4.3 %fusion.23 = f32[512,1024]{1,0:T(8,128)S(1)} fusion(bf16[512,1536]{1,0:T(8,128)(2,1)} %all-gather.3.cloned.1.call-done, bf16[1536,1024]{1,0:T(8,128)(2,1)} %bitcast.48), kind=kOutput, calls=%fused_computation.65 | convolution fusion | flops 1610612736 | bytes 6815744 | tf_op jit(solution)/shard_map/dot_general | solution.py:58
  274.0 20.4 %all-reduce.3.cloned.1.call-done = (bf16[512,64]{0,1:T(8,128)(2,1)}, bf16[512,256]{1,0:T(8,128)(2,1)}) async-done(((bf16[512,64]{0,1:T(8,128)(2,1)}, bf16[512,256]{1,0:T(8,128)(2,1)}), (bf16[512,64]{0,1:T(8,128)(2,1)}, bf16[512,256]{1,0:T(8,128)(2,1)})) %all-reduce.3.cloned.1.call-update) | async-done | bytes 327696 | tf_op jit(solution)/shard_map/psum | solution.py:41
  295.3 24.9 %gather_fusion.2 = f32[3072]{0:T(1024)S(1)} fusion(f32[512,64]{0,1:T(8,128)S(1)} %add_divide_fusion, s32[3072]{0:T(1024)S(1)} %reshape.164), kind=kCustom, calls=%fused_computation.2 | custom fusion | bytes 49152 | tf_op jit(solution)/shard_map/jit(take_along_axis)/gather | solution.py:71
  321.2 7.4 %reshape.145 = bf16[3328,768]{1,0:T(8,128)(2,1)} reshape(bf16[64,52,768]{2,1,0:T(8,128)(2,1)} %all-to-all-done.1) | data formatting | bytes 10223616 | tf_op jit(solution)/shard_map/reshape | solution.py:114
  328.6 17.7 %gather_fusion.1 = bf16[3072,768]{1,0:T(8,128)(2,1)} fusion(bf16[3328,768]{1,0:T(8,128)(2,1)} %reshape.145, s32[3072]{0:T(1024)S(1)} %broadcast_clamp_fusion), kind=kCustom, calls=%fused_computation.1 | custom fusion | bytes 9449472 | tf_op jit(solution)/shard_map/gather | solution.py:114
  346.3 9.2 %reshape.147 = f32[512,6,768]{2,1,0:T(8,128)} reshape(bf16[3072,768]{1,0:T(8,128)(2,1)} %gather_fusion.1) | data formatting | bytes 14155776 | tf_op jit(solution)/shard_map/convert_element_type | solution.py:114
  355.4 17.2 %multiply_reduce_fusion = f32[512,768]{1,0:T(8,128)S(1)} fusion(f32[512,6,768]{2,1,0:T(8,128)} %reshape.147, f32[512,6]{1,0:T(8,128)S(1)} %copy.40), kind=kLoop, calls=%fused_computation.5 | loop fusion | flops 4325376 | bytes 11022336 | tf_op jit(solution)/shard_map/reduce_sum | solution.py:116
  (72 shorter events, 22.1 us)
Async XLA Ops:
  6.5 170.7 %copy-start = (bf16[1,768,1024]{2,1,0:T(8,128)(2,1)S(1)}, bf16[1,768,1024]{2,1,0:T(8,128)(2,1)}, u32[]{:S(2)}) copy-start(bf16[1,768,1024]{2,1,0:T(8,128)(2,1)} %param.17) | copy-start | bytes 4718596
  6.5 196.8 %reduce-scatter.5.cloned.1.call-start = ((), (), s32[]{:S(2)}) async-start(), calls=%async_computation.6 | async-start | bytes 10223616 | tf_op jit(solution)/shard_map/reduce_scatter | solution.py:93
  9.5 49.6 %copy-start.2 = (bf16[512,768]{1,0:T(8,128)(2,1)S(1)}, bf16[512,768]{1,0:T(8,128)(2,1)}, u32[]{:S(2)}) copy-start(bf16[512,768]{1,0:T(8,128)(2,1)} %param.11) | copy-start | bytes 2359300
  187.3 37.9 %all-gather.5.cloned.1.call-start = ((), (), s32[]{:S(2)}) async-start(), calls=%async_computation.7 | async-start | bytes 5111808 | tf_op jit(solution)/shard_map/all_gather | solution.py:103
  206.1 19.1 %copy-start.9 = (bf16[1,512,768]{2,1,0:T(8,128)(2,1)S(1)}, bf16[1,512,768]{2,1,0:T(8,128)(2,1)}, u32[]{:S(2)}) copy-start(bf16[1,512,768]{2,1,0:T(8,128)(2,1)} %param.18) | copy-start | bytes 2359300
  239.7 11.5 %copy-start.3 = (bf16[512,768]{1,0:T(8,128)(2,1)S(1)}, bf16[512,768]{1,0:T(8,128)(2,1)}, u32[]{:S(2)}) copy-start(bf16[512,768]{1,0:T(8,128)(2,1)} %param.11) | copy-start | bytes 2359300
  239.7 11.5 %copy-start.6 = (bf16[768,64]{0,1:T(8,128)(2,1)S(1)}, bf16[768,64]{0,1:T(8,128)(2,1)}, u32[]{:S(2)}) copy-start(bf16[768,64]{0,1:T(8,128)(2,1)} %param.12) | copy-start | bytes 294916
  239.7 12.5 %copy-start.5 = (bf16[768,256]{1,0:T(8,128)(2,1)S(1)}, bf16[768,256]{1,0:T(8,128)(2,1)}, u32[]{:S(2)}) copy-start(bf16[768,256]{1,0:T(8,128)(2,1)} %param.13) | copy-start | bytes 1179652
  239.7 81.5 %all-to-all-start.1 = ((bf16[64,52,768]{2,1,0:T(8,128)(2,1)}), bf16[64,52,768]{2,1,0:T(8,128)(2,1)}, u32[]{:S(2)}, u32[]{:S(2)}) async-start(bf16[64,52,768]{2,1,0:T(8,128)(2,1)} %reshape.144), calls=%async_computation.3 | async-start | bytes 11010048 | tf_op jit(solution)/shard_map/all_to_all | solution.py:107
  250.4 16.3 %all-gather.3.cloned.1.call-start = ((), (), s32[]{:S(2)}) async-start(), calls=%async_computation.4 | async-start | bytes 2359296 | tf_op jit(solution)/shard_map/all_gather | solution.py:59
  251.1 43.3 %all-reduce.3.cloned.1.call-start = ((), (), s32[]{:S(2)}) async-start(), calls=%async_computation.8 | async-start | bytes 655360 | tf_op jit(solution)/shard_map/psum | solution.py:41
  253.3 119.4 %reduce-scatter.3.cloned.1.call-start = ((), (), s32[]{:S(2)}) async-start(), calls=%async_computation.5 | async-start | bytes 2359296 | tf_op jit(solution)/shard_map/reduce_scatter | solution.py:67
  266.7 4.3 %copy-start.8 = (bf16[512,1536]{1,0:T(8,128)(2,1)S(1)}, bf16[512,1536]{1,0:T(8,128)(2,1)}, u32[]{:S(2)}) copy-start(bf16[512,1536]{1,0:T(8,128)(2,1)} %param.16) | copy-start | bytes 4718596
  271.0 2.3 copy-start.4
  271.0 2.6 copy-start.10
  271.0 2.9 copy-start.7
  355.4 19.9 %copy-start.1 = (bf16[1,768,1024]{2,1,0:T(8,128)(2,1)S(1)}, bf16[1,768,1024]{2,1,0:T(8,128)(2,1)}, u32[]{:S(2)}) copy-start(bf16[1,768,1024]{2,1,0:T(8,128)(2,1)} %param.17) | copy-start | bytes 4718596
Sparse Core Ops, SparseCore 0:
  187.4 15.8 reduce-scatter.4
  208.6 16.5 all-gather.4
  252.9 13.7 all-gather.2
  269.0 25.3 all-reduce.2
  296.6 13.0 reduce-scatter.2
where the time goes:
time: 388 us; the launch traced here: 382 us
  local copies, waits for them, and re-layouts  126 us (32%)
  blocking collectives  77 us (20%)
  other arithmetic  63.6 us (16%)
  waiting for transfers between devices  62.8 us (16%)
  matrix products  28.2 us (7%)
  between operations  13.4 us (3%)
  starting transfers between devices  11.3 us (3%)
    all_to_all x1, blocking collectives, body(): lax.all_to_all(send_rows.reshape(expert_count, most_rows, feat_local), 'r...  77 us
    another operation x4, other arithmetic  33.5 us
    gather x5, local copies, waits for them, and re-layouts, body(): chosen = jnp.take_along_axis(scores, routes, axis=1)  25.5 us
    psum x1, waiting for transfers between devices, body(): lax.psum(logit_part.astype(jnp.bfloat16), 'blk').astype(jnp.float32)  20.4 us
    gather x2, local copies, waits for them, and re-layouts, body(): normed[source_slot]  18.2 us
    gather x1, local copies, waits for them, and re-layouts, body(): returned.reshape(expert_count * most_rows, feat_local)[target]  17.7 us
    reduce_sum x1, other arithmetic, body(): routed = jnp.sum(weighted.reshape(tok_rows, top_count, feat_local), axis=1)  17.2 us
    all_gather x1, waiting for transfers between devices, body(): lax.all_gather(hidden, 'blk', axis=0, tiled=True)  16.7 us
  transfers between devices with their start and end apart: 6, of which 5 were waited for; matrix products, arithmetic and copies ran while one was open for 24% of the time, Pallas kernels for 0%

commit v1 on v0

v1 whole, which is shorter than its diff:
```python
import jax
import jax.numpy as jnp
from jax import lax
from jax.sharding import PartitionSpec as P

RANK = 16


def body(
    normed,
    router,
    adapter_down,
    adapter_up,
    shared_gate_up,
    shared_down,
    expert_gate_up,
    expert_down,
    lengths,
    adapter_ids,
    routes,
):
    tok_rows = normed.shape[0]
    feat_local = normed.shape[1]
    top_count = routes.shape[1]
    req_count = lax.axis_size("req")
    blk_count = lax.axis_size("blk")
    expert_count = req_count * expert_gate_up.shape[0]
    most_rows = (
        tok_rows * top_count + expert_count - 1
    ) // expert_count + tok_rows * top_count // (12 * expert_count)
    part_rows = -(-most_rows // blk_count)
    most_rows = part_rows * blk_count
    hidden_width = expert_down.shape[1]

    expert_iota = jnp.arange(expert_count, dtype=jnp.int32)
    has = jnp.zeros((tok_rows, expert_count), jnp.float32)
    for k in range(top_count):
        has = has + (routes[:, k][:, None] == expert_iota[None, :]).astype(jnp.float32)
    tok_iota = jnp.arange(tok_rows, dtype=jnp.int32)
    earlier = (tok_iota[None, :] < tok_iota[:, None]).astype(jnp.bfloat16)
    rank = jnp.dot(earlier, has.astype(jnp.bfloat16), preferred_element_type=jnp.float32)
    rank = jnp.where(has > 0, rank, -1.0).astype(jnp.int32)
    slot_iota = jnp.arange(most_rows, dtype=jnp.int32)
    pick = rank.T[:, None, :] == slot_iota[None, :, None]

    send_rows = jnp.dot(
        pick.reshape(expert_count * most_rows, tok_rows).astype(jnp.bfloat16),
        normed,
        preferred_element_type=jnp.float32,
    ).astype(jnp.bfloat16)
    both = ("req", "blk")
    received = lax.all_to_all(
        send_rows.reshape(expert_count * blk_count, part_rows, feat_local),
        both,
        split_axis=0,
        concat_axis=0,
        tiled=True,
    )
    rows_in = received.reshape(req_count, blk_count, part_rows, feat_local)

    weight_gate_up = lax.all_gather(expert_gate_up[0], "blk", axis=0, tiled=True)
    weight_down = lax.all_gather(expert_down[0], "blk", axis=1, tiled=True)
    gate_up = jnp.einsum(
        "gcsd,cdf->gsf",
        rows_in,
        weight_gate_up.reshape(blk_count, feat_local, 2 * hidden_width),
        preferred_element_type=jnp.float32,
    )
    hidden = (jax.nn.silu(gate_up[..., :hidden_width]) * gate_up[..., hidden_width:]).astype(
        jnp.bfloat16
    )
    expert_out = jnp.einsum(
        "gsh,hcd->gcsd",
        hidden,
        weight_down.reshape(hidden_width, blk_count, feat_local),
        preferred_element_type=jnp.float32,
    ).astype(jnp.bfloat16)
    returned = lax.all_to_all(
        expert_out.reshape(req_count * blk_count, part_rows, feat_local),
        both,
        split_axis=0,
        concat_axis=0,
        tiled=True,
    )

    normed_full = lax.all_gather(normed, "blk", axis=1, tiled=True)
    small_w = lax.all_gather(
        jnp.concatenate([router, adapter_down], axis=1), "blk", axis=0, tiled=True
    )
    small = jnp.dot(normed_full, small_w, preferred_element_type=jnp.float32)
    logits = small[:, :expert_count]
    low_all = small[:, expert_count:]
    ends = jnp.cumsum(lengths[0])
    request = jnp.sum((tok_iota[:, None] >= ends[None, :]).astype(jnp.int32), axis=1)
    slots_req = jnp.arange(lengths.shape[1], dtype=jnp.int32)
    adapter_token = jnp.sum(
        jnp.where(request[:, None] == slots_req[None, :], adapter_ids[0][None, :], 0), axis=1
    )
    column_owner = jnp.arange(low_all.shape[1], dtype=jnp.int32) // RANK
    low = jnp.where(column_owner[None, :] == adapter_token[:, None], low_all, 0.0).astype(
        jnp.bfloat16
    )
    delta = jnp.dot(low, adapter_up, preferred_element_type=jnp.float32)
    shared_local = shared_gate_up.shape[2]
    shared_flat = shared_gate_up.reshape(shared_gate_up.shape[0], 2 * shared_local)
    shared_pre = jnp.dot(normed_full, shared_flat, preferred_element_type=jnp.float32)
    shared_hidden = (
        jax.nn.silu(shared_pre[:, :shared_local]) * shared_pre[:, shared_local:]
    ).astype(jnp.bfloat16)
    shared_terms = jnp.dot(shared_hidden, shared_down, preferred_element_type=jnp.float32)
    shared_out = lax.psum_scatter(
        shared_terms.astype(jnp.bfloat16), "blk", scatter_dimension=1, tiled=True
    ).astype(jnp.float32)

    chosen = jnp.where(has > 0, jax.nn.sigmoid(logits), 0.0)
    gate = chosen / jnp.sum(chosen, axis=1, keepdims=True)
    weights = jnp.where(pick, gate.T[:, None, :], 0.0).reshape(expert_count * most_rows, tok_rows)
    weights_hi = weights.astype(jnp.bfloat16)
    weights_lo = (weights - weights_hi.astype(jnp.float32)).astype(jnp.bfloat16)
    back = returned.reshape(expert_count * most_rows, feat_local)
    contract = (((0,), (0,)), ((), ()))
    routed = lax.dot_general(
        weights_hi, back, contract, preferred_element_type=jnp.float32
    ) + lax.dot_general(weights_lo, back, contract, preferred_element_type=jnp.float32)
    return (shared_out + 0.5 * delta + routed).astype(jnp.bfloat16)


def solution(mesh):
    return jax.shard_map(
        body,
        mesh=mesh,
        in_specs=(
            P("req", "blk"),
            P("blk", None),
            P("blk", None),
            P(None, "blk"),
            P(None, None, "blk"),
            P("blk", None),
            P("req", "blk", None),
            P("req", None, "blk"),
            P("req", None),
            P("req", None),
            P("req", None),
        ),
        out_specs=P("req", "blk"),
        check_vma=False,
    )
```

time: 388 us -> 261 us (0.67); the launches traced: 382 us -> 259 us
  blocking collectives: 77 us -> 2.87 us
  local copies, waits for them, and re-layouts: 126 us -> 55.8 us
  other arithmetic: 63.6 us -> 7.76 us
  waiting for transfers between devices: 62.8 us -> 114 us
  matrix products: 28.2 us -> 49.6 us
  starting transfers between devices: 11.3 us -> 16.5 us
    all_to_all x1 -> x2, waiting for transfers between devices: 0.42 us -> 87.5 us  [the longest x1 57.1 us: body(): lax.all_to_all(send_rows.reshape(expert_count * blk_count, part_rows, fea...]
    all_to_all x1 -> x0, blocking collectives: 77 us -> none  [body(): lax.all_to_all(send_rows.reshape(expert_count, most_rows, feat_local), 'r...]
    gather x8 -> x0, local copies, waits for them, and re-layouts: 61.4 us -> none  [the longest x5 25.5 us: body(): chosen = jnp.take_along_axis(scores, routes, axis=1)]
    another operation x4 -> x1, other arithmetic: 33.5 us -> 0.18 us
    scatter x2 -> x0, local copies, waits for them, and re-layouts: 23.6 us -> none  [the longest x1 11.8 us: slot_table(): jnp.zeros((total_slots,), jnp.int32).at[target].set(source_row)]
    dot_general x5 -> x8, matrix products: 23.3 us -> 44.2 us  [the longest x1 13.5 us: body(): jnp.einsum('gcsd,cdf->gsf', rows_in, weight_gate_up.reshape(blk_count, fe...]
    psum x1 -> x0, waiting for transfers between devices: 20.4 us -> none  [body(): lax.psum(logit_part.astype(jnp.bfloat16), 'blk').astype(jnp.float32)]
    reduce_sum x4 -> x2, other arithmetic: 18.6 us -> 0.22 us  [the longest x1 0.13 us: body(): gate = chosen / jnp.sum(chosen, axis=1, keepdims=True)]
  transfers between devices with their start and end apart: 6 -> 6, of which waited for: 5 -> 4; matrix products, arithmetic and copies ran while one was open for 24% -> 26% of each run, Pallas kernels for 0% -> 0%
where the time goes in v1:
time: 261 us; the launch traced here: 259 us
  waiting for transfers between devices  114 us (44%)
  local copies, waits for them, and re-layouts  55.8 us (21%)
  matrix products  49.6 us (19%)
  starting transfers between devices  16.5 us (6%)
  between operations  13.3 us (5%)
  other arithmetic  7.76 us (3%)
  blocking collectives  2.87 us (1%)
    all_to_all x1, waiting for transfers between devices, body(): lax.all_to_all(send_rows.reshape(expert_count * blk_count, part_rows, fea...  57.1 us
    all_to_all x1, waiting for transfers between devices, body(): lax.all_to_all(expert_out.reshape(req_count * blk_count, part_rows, feat_...  30.4 us
    all_gather x1, waiting for transfers between devices, body(): lax.all_gather(expert_gate_up[0], 'blk', axis=0, tiled=True)  16.8 us
    dot_general x1, matrix products, body(): jnp.einsum('gcsd,cdf->gsf', rows_in, weight_gate_up.reshape(blk_count, fe...  13.5 us
    eq x4, local copies, waits for them, and re-layouts, body(): pick = rank.T[:, None, :] == slot_iota[None, :, None]  12.1 us
    all_to_all x1, starting transfers between devices, body(): lax.all_to_all(send_rows.reshape(expert_count * blk_count, part_rows, fea...  10.9 us
    reshape x1, local copies, waits for them, and re-layouts, body(): back = returned.reshape(expert_count * most_rows, feat_local)  9.15 us
    reshape x1, local copies, waits for them, and re-layouts, body(): send_rows.reshape(expert_count * blk_count, part_rows, feat_local)  9.08 us
  transfers between devices with their start and end apart: 6, of which 4 were waited for; matrix products, arithmetic and copies ran while one was open for 26% of the time, Pallas kernels for 0%

profile of v1, /device:TPU:2, one launch (start us, length us, event | category | flops | bytes accessed | tf_op | source)
XLA Modules:
  0.0 259.5 jit_solution(9073780814427026285)
XLA Ops:
  7.8 3.9 %eq.245 = s32[64,52,512]{2,1,0:T(8,128)} broadcast(s32[64,512]{1,0:T(8,128)S(1)} %fusion.15), dimensions={0,2} | broadcast | bytes 6946816 | tf_op jit(solution)/shard_map/eq | solution.py:44
  11.7 8.1 %eq.248 = s32[3328,512]{1,0:T(8,128)} reshape(s32[64,52,512]{2,1,0:T(8,128)} %eq.245) | data formatting | bytes 13631488 | tf_op jit(solution)/shard_map/eq | solution.py:44
  19.9 7.1 %fusion.3 = bf16[3328,768]{1,0:T(8,128)(2,1)} fusion(bf16[512,768]{1,0:T(8,128)(2,1)S(1)} %copy-done.4, s32[3328,512]{1,0:T(8,128)} %eq.248, s32[3328]{0:T(1024)S(1)} %eq.250), kind=kOutput, calls=%fused_computation.6 | convolution fusion | flops 2621505536 | bytes 12727296 | tf_op jit(solution)/shard_map/dot_general | solution.py:46
  26.9 9.1 %reshape.139 = bf16[128,26,768]{2,1,0:T(8,128)(2,1)} reshape(bf16[3328,768]{1,0:T(8,128)(2,1)} %fusion.3) | data formatting | bytes 10223616 | tf_op jit(solution)/shard_map/reshape | solution.py:53
  36.0 10.9 %all-to-all-start = ((bf16[128,26,768]{2,1,0:T(8,128)(2,1)}), bf16[128,26,768]{2,1,0:T(8,128)(2,1)}, u32[]{:S(2)}, u32[]{:S(2)}) async-start(bf16[128,26,768]{2,1,0:T(8,128)(2,1)} %reshape.139), calls=%async_computation.1 | async-start | bytes 12582912 | tf_op jit(solution)/shard_map/all_to_all | solution.py:52
  49.1 16.8 %all-gather.8.cloned.1.call-done = bf16[1,1536,1024]{2,1,0:T(8,128)(2,1)} async-done(((bf16[1,768,1024]{2,1,0:T(8,128)(2,1)}), bf16[1,1536,1024]{2,1,0:T(8,128)(2,1)}) %all-gather.8.cloned.1.call-update) | async-done | bytes 3145744 | tf_op jit(solution)/shard_map/all_gather | solution.py:61
  66.0 57.1 %all-to-all-done = bf16[128,26,768]{2,1,0:T(8,128)(2,1)} async-done(((bf16[128,26,768]{2,1,0:T(8,128)(2,1)}), bf16[128,26,768]{2,1,0:T(8,128)(2,1)}, u32[]{:S(2)}, u32[]{:S(2)}) %all-to-all-start) | async-done | bytes 5111840 | tf_op jit(solution)/shard_map/all_to_all | solution.py:52
  123.0 13.5 %fusion.10 = f32[64,26,1024]{2,0,1:T(8,128)} fusion(bf16[2,768,1024,1]{2,1,0,3:T(8,128)(2,1)} %bitcast.63, bf16[64,2,26,768]{3,2,1,0:T(8,128)(2,1)} %bitcast.11), kind=kOutput, calls=%fused_computation.14 | convolution fusion | flops 5234491392 | bytes 15073280 | tf_op jit(solution)/shard_map/gcsd,cdf->gsf/dot_general | solution.py:63
  136.5 6.3 %convert_bitcast_fusion = bf16[64,2,26,768]{3,0,1,2:T(8,128)(2,1)S(1)} fusion(bf16[512,2,768,1]{0,2,1,3:T(8,128)(2,1)} %bitcast.64, f32[64,26,1024]{2,0,1:T(8,128)} %fusion.10), kind=kOutput, calls=%fused_computation.9 | convolution fusion | flops 2624913408 | bytes 13500416 | tf_op jit(solution)/shard_map/gsh,hcd->gcsd/dot_general | solution.py:72
  142.9 5.7 %copy.40 = bf16[64,2,26,768]{3,2,1,0:T(8,128)(2,1)} copy(bf16[64,2,26,768]{3,0,1,2:T(8,128)(2,1)S(1)} %convert_bitcast_fusion) | data formatting | bytes 10223616 | tf_op jit(solution)/shard_map/reshape | solution.py:79
  148.6 5.3 %all-to-all-start.1 = ((bf16[128,26,768]{2,1,0:T(8,128)(2,1)}), bf16[128,26,768]{2,1,0:T(8,128)(2,1)}, u32[]{:S(2)}, u32[]{:S(2)}) async-start(bf16[128,26,768]{2,1,0:T(8,128)(2,1)} %bitcast.46), calls=%async_computation.2 | async-start | bytes 12582912 | tf_op jit(solution)/shard_map/all_to_all | solution.py:78
  154.8 4.4 %copy.42 = bf16[192,8,2,512]{3,1,2,0:T(8,128)(2,1)} copy(bf16[192,8,2,512]{3,2,1,0:T(2,128)(2,1)} %bitcast.47) | data formatting | bytes 6291456
  159.8 2.9 %all_gather.13 = bf16[1536,320]{1,0:T(8,128)(2,1)S(1)} all-gather(bf16[768,320]{1,0:T(8,128)(2,1)S(1)} %pad_maximum_fusion), channel_id=1, replica_groups=mesh['req'=64,'blk'=2] {'blk'}, dimensions={0}, use_global_device_ids=true | all-gather | bytes 1474560 | tf_op jit(solution)/shard_map/all_gather | solution.py:87
  162.6 7.9 %all-gather.6.cloned.1.call-done = bf16[512,1536]{1,0:T(8,128)(2,1)} async-done(((bf16[512,768]{1,0:T(8,128)(2,1)}), bf16[512,1536]{1,0:T(8,128)(2,1)}) %all-gather.6.cloned.1.call-update) | async-done | bytes 1572880 | tf_op jit(solution)/shard_map/all_gather | solution.py:86
  170.5 4.2 %fusion.42 = f32[512,1024]{1,0:T(8,128)S(1)} fusion(bf16[512,1536]{1,0:T(8,128)(2,1)} %all-gather.6.cloned.1.call-done, bf16[1536,1024]{1,0:T(8,128)(2,1)} %bitcast.48), kind=kOutput, calls=%fused_computation.70 | convolution fusion | flops 1610612736 | bytes 6815744 | tf_op jit(solution)/shard_map/dot_general | solution.py:106
  180.3 3.4 %fusion = bf16[64,52,512]{2,1,0:T(8,128)(2,1)} fusion(f32[64,512]{1,0:T(8,128)S(1)} %divide_bitcast_fusion, s32[64,512]{1,0:T(8,128)S(1)} %fusion.15), kind=kLoop, calls=%fused_computation.2 | loop fusion | flops 10223616 | bytes 3670016 | tf_op jit(solution)/shard_map/convert_element_type | solution.py:119
  183.7 6.2 %convert_element_type.143 = bf16[3328,512]{1,0:T(8,128)(2,1)} reshape(bf16[64,52,512]{2,1,0:T(8,128)(2,1)} %fusion) | data formatting | bytes 6815744 | tf_op jit(solution)/shard_map/convert_element_type | solution.py:119
  189.9 3.6 %select_convert_fusion = bf16[64,52,512]{2,1,0:T(8,128)(2,1)} fusion(f32[64,512]{1,0:T(8,128)S(1)} %divide_bitcast_fusion, s32[64,512]{1,0:T(8,128)S(1)} %fusion.15), kind=kLoop, calls=%fused_computation.1 | loop fusion | flops 3407872 | bytes 3670016 | tf_op jit(solution)/shard_map/convert_element_type | solution.py:118
  193.5 6.1 %convert_element_type.136 = bf16[3328,512]{1,0:T(8,128)(2,1)} reshape(bf16[64,52,512]{2,1,0:T(8,128)(2,1)} %select_convert_fusion) | data formatting | bytes 6815744 | tf_op jit(solution)/shard_map/convert_element_type | solution.py:118
  199.5 30.4 %all-to-all-done.1 = bf16[128,26,768]{2,1,0:T(8,128)(2,1)} async-done(((bf16[128,26,768]{2,1,0:T(8,128)(2,1)}), bf16[128,26,768]{2,1,0:T(8,128)(2,1)}, u32[]{:S(2)}, u32[]{:S(2)}) %all-to-all-start.1) | async-done | bytes 5111840 | tf_op jit(solution)/shard_map/all_to_all | solution.py:78
  229.9 9.2 %reshape.144 = bf16[3328,768]{1,0:T(8,128)(2,1)} reshape(bf16[128,26,768]{2,1,0:T(8,128)(2,1)} %all-to-all-done.1) | data formatting | bytes 10223616 | tf_op jit(solution)/shard_map/reshape | solution.py:120
  239.1 6.5 %fusion.44 = f32[512,768]{1,0:T(8,128)S(1)} fusion(bf16[3328,512]{1,0:T(8,128)(2,1)} %convert_element_type.143, bf16[3328,768]{1,0:T(8,128)(2,1)} %reshape.144), kind=kOutput, calls=%fused_computation.72 | convolution fusion | flops 2617245696 | bytes 10092544 | tf_op jit(solution)/shard_map/dot_general | solution.py:124
  245.6 4.1 %fusion.43 = f32[512,768]{1,0:T(8,128)} fusion(bf16[3328,512]{1,0:T(8,128)(2,1)S(1)} %copy-done.2, bf16[3328,768]{1,0:T(8,128)(2,1)S(1)} %copy-done.1), kind=kOutput, calls=%fused_computation.71 | convolution fusion | flops 2617245696 | bytes 10092544 | tf_op jit(solution)/shard_map/dot_general | solution.py:122
  249.7 3.3 %add_convert_fusion = bf16[512,768]{1,0:T(8,128)(2,1)} fusion(f32[512,768]{1,0:T(8,128)} %fusion.43, f32[512,768]{1,0:T(8,128)S(1)} %fusion.44, bf16[512,768]{1,0:T(8,128)(2,1)} %reduce-scatter.2.cloned.1.call-done, bf16[256,768]{1,0:T(8,128)(2,1)S(1)} %copy-done.6, f32[512,320]{0,1:T(8,128)} %copy-done.5, s32[512]{0:T(512)S(1)} %select_reduce_fusion, ...), kind=kOutput, calls=%fused_computation.16 | convolution fusion | flops 203948032 | bytes 5377024 | tf_op jit(solution)/shard_map/dot_general | solution.py:103
  (47 shorter events, 10.5 us)
Async XLA Ops:
  6.5 168.1 %copy-start = (bf16[512,1536]{1,0:T(8,128)(2,1)S(1)}, bf16[512,1536]{1,0:T(8,128)(2,1)}, u32[]{:S(2)}) copy-start(bf16[512,1536]{1,0:T(8,128)(2,1)} %param.16) | copy-start | bytes 4718596
  11.7 8.2 %copy-start.4 = (bf16[512,768]{1,0:T(8,128)(2,1)S(1)}, bf16[512,768]{1,0:T(8,128)(2,1)}, u32[]{:S(2)}) copy-start(bf16[512,768]{1,0:T(8,128)(2,1)} %param.11) | copy-start | bytes 2359300
  36.0 11.9 %copy-start.3 = (bf16[1,512,768]{2,1,0:T(8,128)(2,1)S(1)}, bf16[1,512,768]{2,1,0:T(8,128)(2,1)}, u32[]{:S(2)}) copy-start(bf16[1,512,768]{2,1,0:T(8,128)(2,1)} %param.18) | copy-start | bytes 2359300
  36.0 87.0 %all-to-all-start = ((bf16[128,26,768]{2,1,0:T(8,128)(2,1)}), bf16[128,26,768]{2,1,0:T(8,128)(2,1)}, u32[]{:S(2)}, u32[]{:S(2)}) async-start(bf16[128,26,768]{2,1,0:T(8,128)(2,1)} %reshape.139), calls=%async_computation.1 | async-start | bytes 12582912 | tf_op jit(solution)/shard_map/all_to_all | solution.py:52
  47.0 19.0 %all-gather.8.cloned.1.call-start = ((), (), s32[]{:S(2)}) async-start(), calls=%async_computation.5 | async-start | bytes 4718592 | tf_op jit(solution)/shard_map/all_gather | solution.py:61
  47.7 88.8 %all-gather.10.cloned.1.call-start = ((), (), s32[]{:S(2)}) async-start(), calls=%async_computation.6 | async-start | bytes 2359296 | tf_op jit(solution)/shard_map/all_gather | solution.py:62
  148.6 6.1 %copy-start.8 = (bf16[768,64]{0,1:T(8,128)(2,1)S(1)}, bf16[768,64]{0,1:T(8,128)(2,1)}, u32[]{:S(2)}) copy-start(bf16[768,64]{0,1:T(8,128)(2,1)} %param.12) | copy-start | bytes 294916
  148.6 81.4 %all-to-all-start.1 = ((bf16[128,26,768]{2,1,0:T(8,128)(2,1)}), bf16[128,26,768]{2,1,0:T(8,128)(2,1)}, u32[]{:S(2)}, u32[]{:S(2)}) async-start(bf16[128,26,768]{2,1,0:T(8,128)(2,1)} %bitcast.46), calls=%async_computation.2 | async-start | bytes 12582912 | tf_op jit(solution)/shard_map/all_to_all | solution.py:78
  153.8 16.7 %all-gather.6.cloned.1.call-start = ((), (), s32[]{:S(2)}) async-start(), calls=%async_computation.3 | async-start | bytes 2359296 | tf_op jit(solution)/shard_map/all_gather | solution.py:86
  154.6 4.6 %copy-start.10 = (s32[1,4]{1,0:T(1,128)S(1)}, s32[1,4]{1,0:T(1,128)}, u32[]{:S(2)}) copy-start(s32[1,4]{1,0:T(1,128)} %param.19) | copy-start | bytes 52
  154.6 4.9 %copy-start.7 = (bf16[768,256]{1,0:T(8,128)(2,1)S(1)}, bf16[768,256]{1,0:T(8,128)(2,1)}, u32[]{:S(2)}) copy-start(bf16[768,256]{1,0:T(8,128)(2,1)} %param.13) | copy-start | bytes 1179652
  154.6 95.1 %reduce-scatter.2.cloned.1.call-start = ((), (), s32[]{:S(2)}) async-start(), calls=%async_computation.4 | async-start | bytes 2359296 | tf_op jit(solution)/shard_map/reduce_scatter | solution.py:111
  174.7 2.3 copy-start.9
  179.4 0.9 copy-start.5
  239.1 6.5 %copy-start.1 = (bf16[3328,768]{1,0:T(8,128)(2,1)S(1)}, bf16[3328,768]{1,0:T(8,128)(2,1)}, u32[]{:S(2)}) copy-start(bf16[3328,768]{1,0:T(8,128)(2,1)} %reshape.144) | copy-start | bytes 15335428
  239.1 6.5 %copy-start.2 = (bf16[3328,512]{1,0:T(8,128)(2,1)S(1)}, bf16[3328,512]{1,0:T(8,128)(2,1)}, u32[]{:S(2)}) copy-start(bf16[3328,512]{1,0:T(8,128)(2,1)} %convert_element_type.136) | copy-start | bytes 10223620
  245.6 4.1 %copy-start.6 = (bf16[256,768]{1,0:T(8,128)(2,1)S(1)}, bf16[256,768]{1,0:T(8,128)(2,1)}, u32[]{:S(2)}) copy-start(bf16[256,768]{1,0:T(8,128)(2,1)} %param.14) | copy-start | bytes 1179652
Sparse Core Ops, SparseCore 0:
  49.4 16.4 all-gather.7
  67.6 13.8 all-gather.9
  156.3 14.1 all-gather.5
  177.0 13.0 reduce-scatter.1

commit v2 on v1

--- a/solution.py
+++ b/solution.py
@@ -40,23 +40,28 @@
     earlier = (tok_iota[None, :] < tok_iota[:, None]).astype(jnp.bfloat16)
     rank = jnp.dot(earlier, has.astype(jnp.bfloat16), preferred_element_type=jnp.float32)
     rank = jnp.where(has > 0, rank, -1.0).astype(jnp.int32)
-    slot_iota = jnp.arange(most_rows, dtype=jnp.int32)
-    pick = rank.T[:, None, :] == slot_iota[None, :, None]
+    pad_rows = -(-part_rows // 16) * 16
+    chunk_count = expert_count * blk_count
+    row_iota = jnp.arange(chunk_count * pad_rows, dtype=jnp.int32)
+    row_slot = (row_iota // pad_rows) % blk_count * part_rows + row_iota % pad_rows
+    row_slot = jnp.where(row_iota % pad_rows < part_rows, row_slot, -2)
+    rank_rows = jnp.broadcast_to(
+        rank.T[:, None, :], (expert_count, blk_count * pad_rows, tok_rows)
+    ).reshape(chunk_count * pad_rows, tok_rows)
+    pick = rank_rows == row_slot[:, None]
 
     send_rows = jnp.dot(
-        pick.reshape(expert_count * most_rows, tok_rows).astype(jnp.bfloat16),
-        normed,
-        preferred_element_type=jnp.float32,
+        pick.astype(jnp.bfloat16), normed, preferred_element_type=jnp.float32
     ).astype(jnp.bfloat16)
     both = ("req", "blk")
     received = lax.all_to_all(
-        send_rows.reshape(expert_count * blk_count, part_rows, feat_local),
+        send_rows.reshape(chunk_count, pad_rows, feat_local),
         both,
         split_axis=0,
         concat_axis=0,
         tiled=True,
     )
-    rows_in = received.reshape(req_count, blk_count, part_rows, feat_local)
+    rows_in = received.reshape(req_count, blk_count, pad_rows, feat_local)
 
     weight_gate_up = lax.all_gather(expert_gate_up[0], "blk", axis=0, tiled=True)
     weight_down = lax.all_gather(expert_down[0], "blk", axis=1, tiled=True)
@@ -76,7 +81,7 @@
         preferred_element_type=jnp.float32,
     ).astype(jnp.bfloat16)
     returned = lax.all_to_all(
-        expert_out.reshape(req_count * blk_count, part_rows, feat_local),
+        expert_out.reshape(req_count * blk_count, pad_rows, feat_local),
         both,
         split_axis=0,
         concat_axis=0,
@@ -114,10 +119,13 @@
 
     chosen = jnp.where(has > 0, jax.nn.sigmoid(logits), 0.0)
     gate = chosen / jnp.sum(chosen, axis=1, keepdims=True)
-    weights = jnp.where(pick, gate.T[:, None, :], 0.0).reshape(expert_count * most_rows, tok_rows)
+    gate_rows = jnp.broadcast_to(
+        gate.T[:, None, :], (expert_count, blk_count * pad_rows, tok_rows)
+    ).reshape(chunk_count * pad_rows, tok_rows)
+    weights = jnp.where(pick, gate_rows, 0.0)
     weights_hi = weights.astype(jnp.bfloat16)
     weights_lo = (weights - weights_hi.astype(jnp.float32)).astype(jnp.bfloat16)
-    back = returned.reshape(expert_count * most_rows, feat_local)
+    back = returned.reshape(chunk_count * pad_rows, feat_local)
     contract = (((0,), (0,)), ((), ()))
     routed = lax.dot_general(
         weights_hi, back, contract, preferred_element_type=jnp.float32

time: 261 us -> 229 us (0.88)
  local copies, waits for them, and re-layouts: 55.8 us -> 7.54 us
  waiting for transfers between devices: 114 us -> 128 us
  matrix products: 49.6 us -> 53.3 us
    reshape x3 -> x0, local copies, waits for them, and re-layouts: 23.9 us -> none  [the longest x1 9.15 us: body(): back = returned.reshape(expert_count * most_rows, feat_local)]
    all_to_all x2, waiting for transfers between devices: 87.5 us -> 101 us  [the longest x1 57.1 us: body(): lax.all_to_all(send_rows.reshape(chunk_count, pad_rows, feat_local), both...]
    convert_element_type x2 -> x0, local copies, waits for them, and re-layouts: 12.3 us -> none  [the longest x1 6.21 us: body(): weights_lo = (weights - weights_hi.astype(jnp.float32)).astype(jnp.bfloat16)]
    eq x4 -> x0, local copies, waits for them, and re-layouts: 12.1 us -> none  [body(): pick = rank.T[:, None, :] == slot_iota[None, :, None]]
    dot_general x1, matrix products: 6.32 us -> 10.1 us  [body(): jnp.einsum('gsh,hcd->gcsd', hidden, weight_down.reshape(hidden_width, blk...]
    dot_general x1, matrix products: 4.06 us -> 6.83 us  [body(): lax.dot_general(weights_hi, back, contract, preferred_element_type=jnp.fl...]
    unnamed x25 -> x23, local copies, waits for them, and re-layouts: 6.54 us -> 6.58 us
  transfers between devices with their start and end apart: 6 -> 6, of which waited for: 4 -> 4; matrix products, arithmetic and copies ran while one was open for 26% -> 20% of each run, Pallas kernels for 0% -> 0%
where the time goes in v2:
time: 229 us; the launch traced here: 228 us
  waiting for transfers between devices  128 us (56%)
  matrix products  53.3 us (23%)
  starting transfers between devices  16.4 us (7%)
  between operations  13.3 us (6%)
  other arithmetic  7.56 us (3%)
  local copies, waits for them, and re-layouts  7.54 us (3%)
  blocking collectives  2.83 us (1%)
    all_to_all x1, waiting for transfers between devices, body(): lax.all_to_all(send_rows.reshape(chunk_count, pad_rows, feat_local), both...  57.1 us
    all_to_all x1, waiting for transfers between devices, body(): lax.all_to_all(expert_out.reshape(req_count * blk_count, pad_rows, feat_l...  44.4 us
    all_gather x1, waiting for transfers between devices, body(): lax.all_gather(expert_gate_up[0], 'blk', axis=0, tiled=True)  17 us
    dot_general x1, matrix products, body(): jnp.einsum('gcsd,cdf->gsf', rows_in, weight_gate_up.reshape(blk_count, fe...  11.7 us
    all_to_all x1, starting transfers between devices, body(): lax.all_to_all(send_rows.reshape(chunk_count, pad_rows, feat_local), both...  10.9 us
    dot_general x1, matrix products, body(): jnp.einsum('gsh,hcd->gcsd', hidden, weight_down.reshape(hidden_width, blk...  10.1 us
    all_gather x1, waiting for transfers between devices, body(): normed_full = lax.all_gather(normed, 'blk', axis=1, tiled=True)  7.68 us
    dot_general x1, matrix products, body(): lax.dot_general(weights_lo, back, contract, preferred_element_type=jnp.fl...  7.23 us
  transfers between devices with their start and end apart: 6, of which 4 were waited for; matrix products, arithmetic and copies ran while one was open for 20% of the time, Pallas kernels for 0%

profile of v2, /device:TPU:2, one launch (start us, length us, event | category | flops | bytes accessed | tf_op | source)
XLA Modules:
  0.0 228.5 jit_solution(2046526554508976750)
XLA Ops:
  6.6 1.0 fusion.52
  7.8 1.3 bitcast_compare_fusion
  9.2 5.2 %convolution_convert_fusion = bf16[4096,768]{1,0:T(8,128)(2,1)} fusion(pred[4096,512]{1,0:T(32,128)(4,1)S(1)} %bitcast_compare_fusion, bf16[512,768]{1,0:T(8,128)(2,1)S(1)} %copy-done.3), kind=kOutput, calls=%fused_computation.4 | convolution fusion | flops 3224371200 | bytes 9175040 | tf_op jit(solution)/shard_map/dot_general | solution.py:53
  14.4 10.9 %all-to-all-start = ((bf16[128,32,768]{2,1,0:T(8,128)(2,1)}), bf16[128,32,768]{2,1,0:T(8,128)(2,1)}, u32[]{:S(2)}, u32[]{:S(2)}) async-start(bf16[128,32,768]{2,1,0:T(8,128)(2,1)} %bitcast.55), calls=%async_computation.1 | async-start | bytes 12582912 | tf_op jit(solution)/shard_map/all_to_all | solution.py:57
  26.2 1.2 copy.17
  27.3 17.0 %all-gather.8.cloned.1.call-done = bf16[1,1536,1024]{2,1,0:T(8,128)(2,1)} async-done(((bf16[1,768,1024]{2,1,0:T(8,128)(2,1)}), bf16[1,1536,1024]{2,1,0:T(8,128)(2,1)}) %all-gather.8.cloned.1.call-update) | async-done | bytes 3145744 | tf_op jit(solution)/shard_map/all_gather | solution.py:66
  44.4 57.1 %all-to-all-done = bf16[128,32,768]{2,1,0:T(8,128)(2,1)} async-done(((bf16[128,32,768]{2,1,0:T(8,128)(2,1)}), bf16[128,32,768]{2,1,0:T(8,128)(2,1)}, u32[]{:S(2)}, u32[]{:S(2)}) %all-to-all-start) | async-done | bytes 6291488 | tf_op jit(solution)/shard_map/all_to_all | solution.py:57
  101.4 11.7 %convolution_bitcast_fusion = f32[64,32,1024]{2,1,0:T(8,128)} fusion(bf16[64,2,32,768]{3,2,1,0:T(8,128)(2,1)} %bitcast.14, bf16[2,768,1024,1]{2,1,0,3:T(8,128)(2,1)} %bitcast.74), kind=kOutput, calls=%fused_computation.8 | convolution fusion | flops 6442450944 | bytes 17825792 | tf_op jit(solution)/shard_map/gcsd,cdf->gsf/dot_general | solution.py:68
  113.1 10.1 %convolution_convert_fusion.1 = bf16[64,32,2,768]{3,1,2,0:T(8,128)(2,1)} fusion(bf16[512,2,768,1]{0,2,1,3:T(8,128)(2,1)} %bitcast.75, f32[64,32,1024]{2,1,0:T(8,128)} %convolution_bitcast_fusion), kind=kOutput, calls=%fused_computation.7 | convolution fusion | flops 3230662656 | bytes 16252928 | tf_op jit(solution)/shard_map/gsh,hcd->gcsd/dot_general | solution.py:77
  123.2 5.3 %all-to-all-start.1 = ((bf16[128,32,768]{2,1,0:T(8,128)(2,1)}), bf16[128,32,768]{2,1,0:T(8,128)(2,1)}, u32[]{:S(2)}, u32[]{:S(2)}) async-start(bf16[128,32,768]{2,1,0:T(8,128)(2,1)} %bitcast.54), calls=%async_computation.2 | async-start | bytes 12582912 | tf_op jit(solution)/shard_map/all_to_all | solution.py:83
  128.5 0.7 all-gather.6.cloned.1.call-update
  129.5 4.5 %copy.23 = bf16[192,8,2,512]{3,1,2,0:T(8,128)(2,1)} copy(bf16[192,8,2,512]{3,2,1,0:T(2,128)(2,1)} %bitcast.58) | data formatting | bytes 6291456
  134.7 2.8 %all_gather.13 = bf16[1536,320]{1,0:T(8,128)(2,1)S(1)} all-gather(bf16[768,320]{1,0:T(8,128)(2,1)S(1)} %pad_maximum_fusion), channel_id=1, replica_groups=mesh['req'=64,'blk'=2] {'blk'}, dimensions={0}, use_global_device_ids=true | all-gather | bytes 1474560 | tf_op jit(solution)/shard_map/all_gather | solution.py:92
  137.5 7.7 %all-gather.6.cloned.1.call-done = bf16[512,1536]{1,0:T(8,128)(2,1)} async-done(((bf16[512,768]{1,0:T(8,128)(2,1)}), bf16[512,1536]{1,0:T(8,128)(2,1)}) %all-gather.6.cloned.1.call-update) | async-done | bytes 1572880 | tf_op jit(solution)/shard_map/all_gather | solution.py:91
  145.2 4.2 %fusion.53 = f32[512,1024]{1,0:T(8,128)S(1)} fusion(bf16[512,1536]{1,0:T(8,128)(2,1)} %all-gather.6.cloned.1.call-done, bf16[1536,1024]{1,0:T(8,128)(2,1)} %bitcast.59), kind=kOutput, calls=%fused_computation.101 | convolution fusion | flops 1610612736 | bytes 6815744 | tf_op jit(solution)/shard_map/dot_general | solution.py:111
  149.3 2.2 convolution_convert_fusion.2
  151.6 2.3 %convolution_bitcast_fusion.1 = f32[512,320]{0,1:T(8,128)S(1)} fusion(bf16[1536,320]{1,0:T(8,128)(2,1)S(1)} %all_gather.13, bf16[512,1536]{1,0:T(8,128)(2,1)} %all-gather.6.cloned.1.call-done), kind=kOutput, calls=%fused_computation.12 | convolution fusion | flops 503316480 | bytes 3211264 | tf_op jit(solution)/shard_map/dot_general | solution.py:95
  154.1 0.7 copy-done.4
  154.8 2.7 %select_convert_fusion = bf16[64,64,512]{2,1,0:T(8,128)(2,1)} fusion(f32[64,512]{1,0:T(8,128)S(1)} %divide_bitcast_fusion, s32[64,64]{1,0:T(8,128)S(1)} %fusion.28, s32[64,512]{1,0:T(8,128)S(1)} %fusion.4), kind=kLoop, calls=%fused_computation.1 | loop fusion | flops 4194304 | bytes 4472832 | tf_op jit(solution)/shard_map/convert_element_type | solution.py:126
  157.5 2.7 %fusion = bf16[64,64,512]{2,1,0:T(8,128)(2,1)} fusion(f32[64,512]{1,0:T(8,128)S(1)} %divide_bitcast_fusion, s32[64,64]{1,0:T(8,128)S(1)} %fusion.28, s32[64,512]{1,0:T(8,128)S(1)} %fusion.4), kind=kLoop, calls=%fused_computation.2 | loop fusion | flops 12582912 | bytes 4472832 | tf_op jit(solution)/shard_map/convert_element_type | solution.py:127
  160.2 44.4 %all-to-all-done.1 = bf16[128,32,768]{2,1,0:T(8,128)(2,1)} async-done(((bf16[128,32,768]{2,1,0:T(8,128)(2,1)}), bf16[128,32,768]{2,1,0:T(8,128)(2,1)}, u32[]{:S(2)}, u32[]{:S(2)}) %all-to-all-start.1) | async-done | bytes 6291488 | tf_op jit(solution)/shard_map/all_to_all | solution.py:83
  204.6 7.2 %fusion.55 = f32[512,768]{1,0:T(8,128)S(1)} fusion(bf16[4096,512]{1,0:T(8,128)(2,1)} %bitcast.57, bf16[4096,768]{1,0:T(8,128)(2,1)} %bitcast.25), kind=kOutput, calls=%fused_computation.103 | convolution fusion | flops 3221225472 | bytes 12058624 | tf_op jit(solution)/shard_map/dot_general | solution.py:132
  211.8 6.8 %fusion.54 = f32[512,768]{1,0:T(8,128)} fusion(bf16[4096,512]{1,0:T(8,128)(2,1)S(1)} %bitcast.56, bf16[4096,768]{1,0:T(8,128)(2,1)} %bitcast.25), kind=kOutput, calls=%fused_computation.102 | convolution fusion | flops 3221225472 | bytes 12058624 | tf_op jit(solution)/shard_map/dot_general | solution.py:130
  218.7 3.3 %add_convert_fusion = bf16[512,768]{1,0:T(8,128)(2,1)} fusion(f32[512,768]{1,0:T(8,128)} %fusion.54, f32[512,768]{1,0:T(8,128)S(1)} %fusion.55, bf16[512,768]{1,0:T(8,128)(2,1)} %reduce-scatter.2.cloned.1.call-done, bf16[256,768]{1,0:T(8,128)(2,1)S(1)} %copy-done.5, f32[512,320]{0,1:T(8,128)} %copy-done.4, s32[512]{0:T(512)S(1)} %select_reduce_fusion, ...), kind=kOutput, calls=%fused_computation.11 | convolution fusion | flops 203948032 | bytes 5377024 | tf_op jit(solution)/shard_map/dot_general | solution.py:108
  (39 shorter events, 2.2 us)
Async XLA Ops:
  6.5 142.8 %copy-start = (bf16[512,1536]{1,0:T(8,128)(2,1)S(1)}, bf16[512,1536]{1,0:T(8,128)(2,1)}, u32[]{:S(2)}) copy-start(bf16[512,1536]{1,0:T(8,128)(2,1)} %param.16) | copy-start | bytes 4718596
  6.5 2.6 %copy-start.3 = (bf16[512,768]{1,0:T(8,128)(2,1)S(1)}, bf16[512,768]{1,0:T(8,128)(2,1)}, u32[]{:S(2)}) copy-start(bf16[512,768]{1,0:T(8,128)(2,1)} %param.11) | copy-start | bytes 2359300
  14.4 11.7 %copy-start.2 = (bf16[1,512,768]{2,1,0:T(8,128)(2,1)S(1)}, bf16[1,512,768]{2,1,0:T(8,128)(2,1)}, u32[]{:S(2)}) copy-start(bf16[1,512,768]{2,1,0:T(8,128)(2,1)} %param.18) | copy-start | bytes 2359300
  14.4 87.0 %all-to-all-start = ((bf16[128,32,768]{2,1,0:T(8,128)(2,1)}), bf16[128,32,768]{2,1,0:T(8,128)(2,1)}, u32[]{:S(2)}, u32[]{:S(2)}) async-start(bf16[128,32,768]{2,1,0:T(8,128)(2,1)} %bitcast.55), calls=%async_computation.1 | async-start | bytes 12582912 | tf_op jit(solution)/shard_map/all_to_all | solution.py:57
  25.4 19.0 %all-gather.8.cloned.1.call-start = ((), (), s32[]{:S(2)}) async-start(), calls=%async_computation.5 | async-start | bytes 4718592 | tf_op jit(solution)/shard_map/all_gather | solution.py:66
  26.1 87.0 %all-gather.10.cloned.1.call-start = ((), (), s32[]{:S(2)}) async-start(), calls=%async_computation.6 | async-start | bytes 2359296 | tf_op jit(solution)/shard_map/all_gather | solution.py:67
  123.2 6.1 %copy-start.7 = (bf16[768,64]{0,1:T(8,128)(2,1)S(1)}, bf16[768,64]{0,1:T(8,128)(2,1)}, u32[]{:S(2)}) copy-start(bf16[768,64]{0,1:T(8,128)(2,1)} %param.12) | copy-start | bytes 294916
  123.2 81.4 %all-to-all-start.1 = ((bf16[128,32,768]{2,1,0:T(8,128)(2,1)}), bf16[128,32,768]{2,1,0:T(8,128)(2,1)}, u32[]{:S(2)}, u32[]{:S(2)}) async-start(bf16[128,32,768]{2,1,0:T(8,128)(2,1)} %bitcast.54), calls=%async_computation.2 | async-start | bytes 12582912 | tf_op jit(solution)/shard_map/all_to_all | solution.py:83
  128.5 16.7 %all-gather.6.cloned.1.call-start = ((), (), s32[]{:S(2)}) async-start(), calls=%async_computation.3 | async-start | bytes 2359296 | tf_op jit(solution)/shard_map/all_gather | solution.py:91
  129.2 89.4 %reduce-scatter.2.cloned.1.call-start = ((), (), s32[]{:S(2)}) async-start(), calls=%async_computation.4 | async-start | bytes 2359296 | tf_op jit(solution)/shard_map/reduce_scatter | solution.py:116
  129.5 4.5 %copy-start.9 = (s32[1,4]{1,0:T(1,128)S(1)}, s32[1,4]{1,0:T(1,128)}, u32[]{:S(2)}) copy-start(s32[1,4]{1,0:T(1,128)} %param.19) | copy-start | bytes 52
  129.5 4.8 %copy-start.8 = (s32[1,4]{1,0:T(1,128)S(1)}, s32[1,4]{1,0:T(1,128)}, u32[]{:S(2)}) copy-start(s32[1,4]{1,0:T(1,128)} %param.20) | copy-start | bytes 52
  129.5 4.9 %copy-start.6 = (bf16[768,256]{1,0:T(8,128)(2,1)S(1)}, bf16[768,256]{1,0:T(8,128)(2,1)}, u32[]{:S(2)}) copy-start(bf16[768,256]{1,0:T(8,128)(2,1)} %param.13) | copy-start | bytes 1179652
  153.9 0.9 copy-start.4
  204.6 7.2 %copy-start.1 = (bf16[64,64,512]{2,1,0:T(8,128)(2,1)S(1)}, bf16[64,64,512]{2,1,0:T(8,128)(2,1)}, u32[]{:S(2)}) copy-start(bf16[64,64,512]{2,1,0:T(8,128)(2,1)} %select_convert_fusion) | copy-start | bytes 12582916
  211.8 6.8 %copy-start.5 = (bf16[256,768]{1,0:T(8,128)(2,1)S(1)}, bf16[256,768]{1,0:T(8,128)(2,1)}, u32[]{:S(2)}) copy-start(bf16[256,768]{1,0:T(8,128)(2,1)} %param.14) | copy-start | bytes 1179652
Sparse Core Ops, SparseCore 0:
  27.8 16.4 all-gather.7
  46.0 13.8 all-gather.9
  131.0 14.1 all-gather.5
  151.7 13.0 reduce-scatter.1

commit v3 on v1

--- a/solution.py
+++ b/solution.py
@@ -40,48 +40,70 @@
     earlier = (tok_iota[None, :] < tok_iota[:, None]).astype(jnp.bfloat16)
     rank = jnp.dot(earlier, has.astype(jnp.bfloat16), preferred_element_type=jnp.float32)
     rank = jnp.where(has > 0, rank, -1.0).astype(jnp.int32)
-    slot_iota = jnp.arange(most_rows, dtype=jnp.int32)
-    pick = rank.T[:, None, :] == slot_iota[None, :, None]
+    wave_rows = 16
+    waves = -(-part_rows // wave_rows)
+    chunk_count = expert_count * blk_count
+    row_iota = jnp.arange(chunk_count * wave_rows, dtype=jnp.int32)
+    rank_rows = jnp.broadcast_to(
+        rank.T[:, None, :], (expert_count, blk_count * wave_rows, tok_rows)
+    ).reshape(chunk_count * wave_rows, tok_rows)
+    both = ("req", "blk")
 
-    send_rows = jnp.dot(
-        pick.reshape(expert_count * most_rows, tok_rows).astype(jnp.bfloat16),
-        normed,
-        preferred_element_type=jnp.float32,
-    ).astype(jnp.bfloat16)
-    both = ("req", "blk")
-    received = lax.all_to_all(
-        send_rows.reshape(expert_count * blk_count, part_rows, feat_local),
-        both,
-        split_axis=0,
-        concat_axis=0,
-        tiled=True,
-    )
-    rows_in = received.reshape(req_count, blk_count, part_rows, feat_local)
+    def wave_pick(w):
+        inner = w * wave_rows + row_iota % wave_rows
+        slot = (row_iota // wave_rows) % blk_count * part_rows + inner
+        slot = jnp.where(inner < part_rows, slot, -2)
+        return rank_rows == slot[:, None]
+
+    def exchange(rows):
+        return lax.all_to_all(
+            rows.reshape(chunk_count, wave_rows, feat_local),
+            both,
+            split_axis=0,
+            concat_axis=0,
+            tiled=True,
+        )
 
     weight_gate_up = lax.all_gather(expert_gate_up[0], "blk", axis=0, tiled=True)
     weight_down = lax.all_gather(expert_down[0], "blk", axis=1, tiled=True)
-    gate_up = jnp.einsum(
-        "gcsd,cdf->gsf",
-        rows_in,
-        weight_gate_up.reshape(blk_count, feat_local, 2 * hidden_width),
-        preferred_element_type=jnp.float32,
-    )
-    hidden = (jax.nn.silu(gate_up[..., :hidden_width]) * gate_up[..., hidden_width:]).astype(
-        jnp.bfloat16
-    )
-    expert_out = jnp.einsum(
-        "gsh,hcd->gcsd",
-        hidden,
-        weight_down.reshape(hidden_width, blk_count, feat_local),
-        preferred_element_type=jnp.float32,
-    ).astype(jnp.bfloat16)
-    returned = lax.all_to_all(
-        expert_out.reshape(req_count * blk_count, part_rows, feat_local),
-        both,
-        split_axis=0,
-        concat_axis=0,
-        tiled=True,
-    )
+
+    def expert(received):
+        rows_in = received.reshape(req_count, blk_count, wave_rows, feat_local)
+        gate_up = jnp.einsum(
+            "gcsd,cdf->gsf",
+            rows_in,
+            weight_gate_up.reshape(blk_count, feat_local, 2 * hidden_width),
+            preferred_element_type=jnp.float32,
+        )
+        hidden = (
+            jax.nn.silu(gate_up[..., :hidden_width]) * gate_up[..., hidden_width:]
+        ).astype(jnp.bfloat16)
+        return jnp.einsum(
+            "gsh,hcd->gcsd",
+            hidden,
+            weight_down.reshape(hidden_width, blk_count, feat_local),
+            preferred_element_type=jnp.float32,
+        ).astype(jnp.bfloat16)
+
+    picks = [wave_pick(w) for w in range(waves)]
+    received, last = [], None
+    for w in range(waves):
+        rows = jnp.dot(
+            picks[w].astype(jnp.bfloat16), normed, preferred_element_type=jnp.float32
+        ).astype(jnp.bfloat16)
+        if last is not None:
+            last, rows = lax.optimization_barrier((last, rows))
+            received[-1] = last
+        last = exchange(rows)
+        received.append(last)
+    results = [expert(r) for r in received]
+    returned = []
+    for w in range(waves):
+        last, rows = lax.optimization_barrier((last, results[w]))
+        if w > 0:
+            returned[-1] = last
+        last = exchange(rows)
+        returned.append(last)
 
     normed_full = lax.all_gather(normed, "blk", axis=1, tiled=True)
     small_w = lax.all_gather(
@@ -114,14 +136,19 @@
 
     chosen = jnp.where(has > 0, jax.nn.sigmoid(logits), 0.0)
     gate = chosen / jnp.sum(chosen, axis=1, keepdims=True)
-    weights = jnp.where(pick, gate.T[:, None, :], 0.0).reshape(expert_count * most_rows, tok_rows)
-    weights_hi = weights.astype(jnp.bfloat16)
-    weights_lo = (weights - weights_hi.astype(jnp.float32)).astype(jnp.bfloat16)
-    back = returned.reshape(expert_count * most_rows, feat_local)
+    gate_rows = jnp.broadcast_to(
+        gate.T[:, None, :], (expert_count, blk_count * wave_rows, tok_rows)
+    ).reshape(chunk_count * wave_rows, tok_rows)
     contract = (((0,), (0,)), ((), ()))
-    routed = lax.dot_general(
-        weights_hi, back, contract, preferred_element_type=jnp.float32
-    ) + lax.dot_general(weights_lo, back, contract, preferred_element_type=jnp.float32)
+    routed = jnp.zeros((tok_rows, feat_local), jnp.float32)
+    for w in range(waves):
+        weights = jnp.where(picks[w], gate_rows, 0.0)
+        weights_hi = weights.astype(jnp.bfloat16)
+        weights_lo = (weights - weights_hi.astype(jnp.float32)).astype(jnp.bfloat16)
+        back = returned[w].reshape(chunk_count * wave_rows, feat_local)
+        routed = routed + lax.dot_general(
+            weights_hi, back, contract, preferred_element_type=jnp.float32
+        ) + lax.dot_general(weights_lo, back, contract, preferred_element_type=jnp.float32)
     return (shared_out + 0.5 * delta + routed).astype(jnp.bfloat16)
 
 

time: 261 us -> 230 us (0.88)
  local copies, waits for them, and re-layouts: 55.8 us -> 7.18 us
  matrix products: 49.6 us -> 63.1 us
  starting transfers between devices: 16.5 us -> 29.2 us
  waiting for transfers between devices: 114 us -> 104 us
    reshape x3 -> x0, local copies, waits for them, and re-layouts: 23.9 us -> none  [the longest x1 9.15 us: body(): back = returned.reshape(expert_count * most_rows, feat_local)]
    all_gather x1, waiting for transfers between devices: 16.8 us -> 0.02 us  [body(): lax.all_gather(expert_gate_up[0], 'blk', axis=0, tiled=True)]
    all_to_all x2 -> x4, starting transfers between devices: 16.2 us -> 29 us  [exchange(): lax.all_to_all(rows.reshape(chunk_count, wave_rows, feat_local), both, sp...]
    convert_element_type x2 -> x0, local copies, waits for them, and re-layouts: 12.3 us -> none  [the longest x1 6.21 us: body(): weights_lo = (weights - weights_hi.astype(jnp.float32)).astype(jnp.bfloat16)]
    eq x4 -> x0, local copies, waits for them, and re-layouts: 12.1 us -> none  [body(): pick = rank.T[:, None, :] == slot_iota[None, :, None]]
    all_gather x1, waiting for transfers between devices: 7.88 us -> 0.02 us  [body(): normed_full = lax.all_gather(normed, 'blk', axis=1, tiled=True)]
    all_gather x1, waiting for transfers between devices: 0.01 us -> 7.32 us  [body(): weight_down = lax.all_gather(expert_down[0], 'blk', axis=1, tiled=True)]
    all_to_all x2 -> x4, waiting for transfers between devices: 87.5 us -> 94.8 us  [exchange(): lax.all_to_all(rows.reshape(chunk_count, wave_rows, feat_local), both, sp...]
  transfers between devices with their start and end apart: 6 -> 8, of which waited for: 4 -> 5; matrix products, arithmetic and copies ran while one was open for 26% -> 30% of each run, Pallas kernels for 0% -> 0%
where the time goes in v3:
time: 230 us; the launch traced here: 228 us
  waiting for transfers between devices  104 us (45%)
  matrix products  63.1 us (27%)
  starting transfers between devices  29.2 us (13%)
  between operations  13.4 us (6%)
  other arithmetic  8.77 us (4%)
  local copies, waits for them, and re-layouts  7.18 us (3%)
  blocking collectives  2.83 us (1%)
    all_to_all x4, waiting for transfers between devices, exchange(): lax.all_to_all(rows.reshape(chunk_count, wave_rows, feat_local), both, sp...  94.8 us
    all_to_all x4, starting transfers between devices, exchange(): lax.all_to_all(rows.reshape(chunk_count, wave_rows, feat_local), both, sp...  29 us
    dot_general x2, matrix products, expert(): jnp.einsum('gcsd,cdf->gsf', rows_in, weight_gate_up.reshape(blk_count, fe...  13.6 us
    dot_general x2, matrix products, body(): lax.dot_general(weights_hi, back, contract, preferred_element_type=jnp.fl...  9.97 us
    dot_general x2, matrix products, expert(): jnp.einsum('gsh,hcd->gcsd', hidden, weight_down.reshape(hidden_width, blk...  9.81 us
    dot_general x2, matrix products, body(): lax.dot_general(weights_lo, back, contract, preferred_element_type=jnp.fl...  9.45 us
    all_gather x1, waiting for transfers between devices, body(): weight_down = lax.all_gather(expert_down[0], 'blk', axis=1, tiled=True)  7.32 us
    dot_general x2, matrix products, body(): jnp.dot(picks[w].astype(jnp.bfloat16), normed, preferred_element_type=jnp...  6.98 us
  transfers between devices with their start and end apart: 8, of which 5 were waited for; matrix products, arithmetic and copies ran while one was open for 30% of the time, Pallas kernels for 0%

profile of v3, /device:TPU:2, one launch (start us, length us, event | category | flops | bytes accessed | tf_op | source)
XLA Modules:
  0.0 227.9 jit_solution(12520434062349154233)
XLA Ops:
  9.8 3.5 %convolution_convert_fusion.1 = bf16[2048,768]{1,0:T(8,128)(2,1)} fusion(pred[2048,512]{1,0:T(32,128)(4,1)S(1)} %get-tuple-element.22, bf16[512,768]{1,0:T(8,128)(2,1)S(1)} %copy-done.3), kind=kOutput, calls=%fused_computation.9 | convolution fusion | flops 1612185600 | bytes 4980736 | tf_op jit(solution)/shard_map/dot_general | solution.py:91
  13.3 10.9 %all-to-all-start = ((bf16[128,16,768]{2,1,0:T(8,128)(2,1)}), bf16[128,16,768]{2,1,0:T(8,128)(2,1)}, u32[]{:S(2)}, u32[]{:S(2)}) async-start(bf16[128,16,768]{2,1,0:T(8,128)(2,1)} %bitcast.86), calls=%async_computation.1 | async-start | bytes 6291456 | tf_op jit(solution)/shard_map/all_to_all | solution.py:59
  25.0 3.4 %convolution_convert_fusion = bf16[2048,768]{1,0:T(8,128)(2,1)} fusion(pred[2048,512]{1,0:T(32,128)(4,1)S(1)} %get-tuple-element.21, bf16[512,768]{1,0:T(8,128)(2,1)S(1)} %copy-done.3), kind=kOutput, calls=%fused_computation.8 | convolution fusion | flops 1612185600 | bytes 4980736 | tf_op jit(solution)/shard_map/dot_general | solution.py:91
  28.4 36.7 %all-to-all-done = bf16[128,16,768]{2,1,0:T(8,128)(2,1)} async-done(((bf16[128,16,768]{2,1,0:T(8,128)(2,1)}), bf16[128,16,768]{2,1,0:T(8,128)(2,1)}, u32[]{:S(2)}, u32[]{:S(2)}) %all-to-all-start) | async-done | bytes 3145760 | tf_op jit(solution)/shard_map/all_to_all | solution.py:59
  65.2 6.1 %all-to-all-start.1 = ((bf16[128,16,768]{2,1,0:T(8,128)(2,1)}), bf16[128,16,768]{2,1,0:T(8,128)(2,1)}, u32[]{:S(2)}, u32[]{:S(2)}) async-start(bf16[128,16,768]{2,1,0:T(8,128)(2,1)} %bitcast.84), calls=%async_computation.2 | async-start | bytes 6291456 | tf_op jit(solution)/shard_map/all_to_all | solution.py:59
  72.5 8.2 %convolution_bitcast_fusion.1 = f32[64,16,1024]{2,1,0:T(8,128)} fusion(bf16[64,2,16,768]{3,2,1,0:T(8,128)(2,1)} %bitcast.15, bf16[2,768,1024,1]{2,1,0,3:T(8,128)(2,1)} %bitcast.105), kind=kOutput, calls=%fused_computation.14 | convolution fusion | flops 3221225472 | bytes 10485760 | tf_op jit(solution)/shard_map/gcsd,cdf->gsf/dot_general | solution.py:72
  80.7 7.3 %all-gather.10.cloned.1.call-done = bf16[1,512,1536]{1,2,0:T(8,128)(2,1)} async-done(((bf16[1,512,768]{1,2,0:T(8,128)(2,1)}), bf16[1,512,1536]{1,2,0:T(8,128)(2,1)}) %all-gather.10.cloned.1.call-update) | async-done | bytes 1572880 | tf_op jit(solution)/shard_map/all_gather | solution.py:68
  88.0 6.3 %convert_bitcast_fusion.1 = bf16[64,2,16,768]{3,2,1,0:T(8,128)(2,1)} fusion(bf16[512,2,768,1]{0,2,1,3:T(8,128)(2,1)} %bitcast.107, f32[64,16,1024]{2,1,0:T(8,128)} %convolution_bitcast_fusion.1), kind=kOutput, calls=%fused_computation.11 | convolution fusion | flops 1615331328 | bytes 8912896 | tf_op jit(solution)/shard_map/gsh,hcd->gcsd/dot_general | solution.py:81
  94.3 18.0 %all-to-all-done.1 = bf16[128,16,768]{2,1,0:T(8,128)(2,1)} async-done(((bf16[128,16,768]{2,1,0:T(8,128)(2,1)}), bf16[128,16,768]{2,1,0:T(8,128)(2,1)}, u32[]{:S(2)}, u32[]{:S(2)}) %all-to-all-start.1) | async-done | bytes 3145760 | tf_op jit(solution)/shard_map/all_to_all | solution.py:59
  112.3 6.1 %all-to-all-start.2 = ((bf16[128,16,768]{2,1,0:T(8,128)(2,1)}), bf16[128,16,768]{2,1,0:T(8,128)(2,1)}, u32[]{:S(2)}, u32[]{:S(2)}) async-start(bf16[128,16,768]{2,1,0:T(8,128)(2,1)} %bitcast.83), calls=%async_computation.3 | async-start | bytes 6291456 | tf_op jit(solution)/shard_map/all_to_all | solution.py:59
  120.5 2.8 %all_gather.13 = bf16[1536,320]{1,0:T(8,128)(2,1)S(1)} all-gather(bf16[768,320]{1,0:T(8,128)(2,1)S(1)} %pad_maximum_fusion), channel_id=1, replica_groups=mesh['req'=64,'blk'=2] {'blk'}, dimensions={0}, use_global_device_ids=true | all-gather | bytes 1474560 | tf_op jit(solution)/shard_map/all_gather | solution.py:109
  123.9 4.5 %copy.29 = bf16[192,8,2,512]{3,1,2,0:T(8,128)(2,1)} copy(bf16[192,8,2,512]{3,2,1,0:T(2,128)(2,1)} %bitcast.81) | data formatting | bytes 6291456
  128.5 5.4 %convolution_bitcast_fusion = f32[64,16,1024]{2,1,0:T(8,128)S(1)} fusion(bf16[64,2,16,768]{3,2,1,0:T(8,128)(2,1)} %bitcast.26, bf16[2,768,1024,1]{2,1,0,3:T(8,128)(2,1)S(1)} %bitcast.106), kind=kOutput, calls=%fused_computation.13 | convolution fusion | flops 3221225472 | bytes 10485760 | tf_op jit(solution)/shard_map/gcsd,cdf->gsf/dot_general | solution.py:72
  134.0 3.5 %convert_bitcast_fusion = bf16[64,2,16,768]{3,2,1,0:T(8,128)(2,1)} fusion(bf16[512,2,768,1]{0,2,1,3:T(8,128)(2,1)S(1)} %bitcast.108, f32[64,16,1024]{2,1,0:T(8,128)S(1)} %convolution_bitcast_fusion), kind=kOutput, calls=%fused_computation.10 | convolution fusion | flops 1615331328 | bytes 8912896 | tf_op jit(solution)/shard_map/gsh,hcd->gcsd/dot_general | solution.py:81
  137.5 21.9 %all-to-all-done.2 = bf16[128,16,768]{2,1,0:T(8,128)(2,1)} async-done(((bf16[128,16,768]{2,1,0:T(8,128)(2,1)}), bf16[128,16,768]{2,1,0:T(8,128)(2,1)}, u32[]{:S(2)}, u32[]{:S(2)}) %all-to-all-start.2) | async-done | bytes 3145760 | tf_op jit(solution)/shard_map/all_to_all | solution.py:59
  159.4 5.9 %all-to-all-start.3 = ((bf16[128,16,768]{2,1,0:T(8,128)(2,1)}), bf16[128,16,768]{2,1,0:T(8,128)(2,1)}, u32[]{:S(2)}, u32[]{:S(2)}) async-start(bf16[128,16,768]{2,1,0:T(8,128)(2,1)} %bitcast.82), calls=%async_computation.4 | async-start | bytes 6291456 | tf_op jit(solution)/shard_map/all_to_all | solution.py:59
  165.4 4.2 %fusion.62 = f32[512,1024]{1,0:T(8,128)S(1)} fusion(bf16[512,1536]{1,0:T(8,128)(2,1)} %all-gather.6.cloned.1.call-done, bf16[1536,1024]{1,0:T(8,128)(2,1)} %bitcast.85), kind=kOutput, calls=%fused_computation.118 | convolution fusion | flops 1610612736 | bytes 6815744 | tf_op jit(solution)/shard_map/dot_general | solution.py:128
  176.9 2.6 %fusion = (bf16[64,32,512]{2,1,0:T(8,128)(2,1)S(1)}, bf16[64,32,512]{2,1,0:T(8,128)(2,1)}) fusion(f32[64,512]{1,0:T(8,128)S(1)} %divide_bitcast_fusion, s32[64,32]{1,0:T(8,128)S(1)} %get-tuple-element.30, s32[64,512]{1,0:T(8,128)S(1)} %fusion.4, s32[64,32]{1,0:T(8,128)S(1)} %get-tuple-element.29), kind=kLoop, calls=%fused_computation.6 | loop fusion | flops 12582912 | bytes 4472832 | tf_op jit(solution)/shard_map/convert_element_type | solution.py:147
  179.5 3.7 %fusion.64 = f32[512,768]{1,0:T(8,128)S(1)} fusion(bf16[2048,512]{1,0:T(8,128)(2,1)S(1)} %bitcast.90, bf16[2048,768]{1,0:T(8,128)(2,1)} %bitcast.34), kind=kOutput, calls=%fused_computation.120 | convolution fusion | flops 1610612736 | bytes 6815744 | tf_op jit(solution)/shard_map/dot_general | solution.py:151
  183.3 5.0 %fusion.63 = f32[512,768]{1,0:T(8,128)} fusion(bf16[2048,512]{1,0:T(8,128)(2,1)S(1)} %bitcast.89, bf16[2048,768]{1,0:T(8,128)(2,1)} %bitcast.34), kind=kOutput, calls=%fused_computation.119 | convolution fusion | flops 1610612736 | bytes 6815744 | tf_op jit(solution)/shard_map/dot_general | solution.py:149
  188.3 18.1 %all-to-all-done.3 = bf16[128,16,768]{2,1,0:T(8,128)(2,1)} async-done(((bf16[128,16,768]{2,1,0:T(8,128)(2,1)}), bf16[128,16,768]{2,1,0:T(8,128)(2,1)}, u32[]{:S(2)}, u32[]{:S(2)}) %all-to-all-start.3) | async-done | bytes 3145760 | tf_op jit(solution)/shard_map/all_to_all | solution.py:59
  206.4 5.7 %fusion.66 = f32[512,768]{1,0:T(8,128)} fusion(bf16[2048,512]{1,0:T(8,128)(2,1)} %bitcast.88, bf16[2048,768]{1,0:T(8,128)(2,1)} %bitcast.38), kind=kOutput, calls=%fused_computation.122 | convolution fusion | flops 1610612736 | bytes 6815744 | tf_op jit(solution)/shard_map/dot_general | solution.py:151
  212.1 4.9 %fusion.65 = f32[512,768]{1,0:T(8,128)} fusion(bf16[2048,512]{1,0:T(8,128)(2,1)S(1)} %bitcast.87, bf16[2048,768]{1,0:T(8,128)(2,1)} %bitcast.38), kind=kOutput, calls=%fused_computation.121 | convolution fusion | flops 1610612736 | bytes 6815744 | tf_op jit(solution)/shard_map/dot_general | solution.py:149
  217.1 4.3 %add_convert_fusion = bf16[512,768]{1,0:T(8,128)(2,1)} fusion(f32[512,768]{1,0:T(8,128)} %fusion.66, f32[512,768]{1,0:T(8,128)} %fusion.65, f32[512,768]{1,0:T(8,128)} %fusion.63, f32[512,768]{1,0:T(8,128)S(1)} %fusion.64, bf16[512,768]{1,0:T(8,128)(2,1)} %reduce-scatter.2.cloned.1.call-done, bf16[256,768]{1,0:T(8,128)(2,1)S(1)} %copy-done.5, ...), kind=kOutput, calls=%fused_computation.19 | convolution fusion | flops 204734464 | bytes 8522752 | tf_op jit(solution)/shard_map/dot_general | solution.py:125
  (64 shorter events, 15.2 us)
Async XLA Ops:
  6.5 163.1 %copy-start = (bf16[512,1536]{1,0:T(8,128)(2,1)S(1)}, bf16[512,1536]{1,0:T(8,128)(2,1)}, u32[]{:S(2)}) copy-start(bf16[512,1536]{1,0:T(8,128)(2,1)} %param.16) | copy-start | bytes 4718596
  6.5 3.2 %copy-start.3 = (bf16[512,768]{1,0:T(8,128)(2,1)S(1)}, bf16[512,768]{1,0:T(8,128)(2,1)}, u32[]{:S(2)}) copy-start(bf16[512,768]{1,0:T(8,128)(2,1)} %param.11) | copy-start | bytes 2359300
  13.3 51.9 %all-to-all-start = ((bf16[128,16,768]{2,1,0:T(8,128)(2,1)}), bf16[128,16,768]{2,1,0:T(8,128)(2,1)}, u32[]{:S(2)}, u32[]{:S(2)}) async-start(bf16[128,16,768]{2,1,0:T(8,128)(2,1)} %bitcast.86), calls=%async_computation.1 | async-start | bytes 6291456 | tf_op jit(solution)/shard_map/all_to_all | solution.py:59
  24.3 48.3 %all-gather.8.cloned.1.call-start = ((), (), s32[]{:S(2)}) async-start(), calls=%async_computation.7 | async-start | bytes 4718592 | tf_op jit(solution)/shard_map/all_gather | solution.py:67
  65.2 6.1 %copy-start.2 = (bf16[1,512,768]{2,1,0:T(8,128)(2,1)S(1)}, bf16[1,512,768]{2,1,0:T(8,128)(2,1)}, u32[]{:S(2)}) copy-start(bf16[1,512,768]{2,1,0:T(8,128)(2,1)} %param.18) | copy-start | bytes 2359300
  65.2 47.1 %all-to-all-start.1 = ((bf16[128,16,768]{2,1,0:T(8,128)(2,1)}), bf16[128,16,768]{2,1,0:T(8,128)(2,1)}, u32[]{:S(2)}, u32[]{:S(2)}) async-start(bf16[128,16,768]{2,1,0:T(8,128)(2,1)} %bitcast.84), calls=%async_computation.2 | async-start | bytes 6291456 | tf_op jit(solution)/shard_map/all_to_all | solution.py:59
  71.2 16.8 %all-gather.10.cloned.1.call-start = ((), (), s32[]{:S(2)}) async-start(), calls=%async_computation.8 | async-start | bytes 2359296 | tf_op jit(solution)/shard_map/all_gather | solution.py:68
  112.3 6.8 %copy-start.7 = (bf16[768,64]{0,1:T(8,128)(2,1)S(1)}, bf16[768,64]{0,1:T(8,128)(2,1)}, u32[]{:S(2)}) copy-start(bf16[768,64]{0,1:T(8,128)(2,1)} %param.12) | copy-start | bytes 294916
  112.3 7.0 %copy-start.17 = (s32[1,4]{1,0:T(1,128)S(1)}, s32[1,4]{1,0:T(1,128)}, u32[]{:S(2)}) copy-start(s32[1,4]{1,0:T(1,128)} %param.19) | copy-start | bytes 52
  112.3 7.3 %copy-start.14 = (s32[1,4]{1,0:T(1,128)S(1)}, s32[1,4]{1,0:T(1,128)}, u32[]{:S(2)}) copy-start(s32[1,4]{1,0:T(1,128)} %param.20) | copy-start | bytes 52
  112.3 7.9 %copy-start.6 = (bf16[768,256]{1,0:T(8,128)(2,1)S(1)}, bf16[768,256]{1,0:T(8,128)(2,1)}, u32[]{:S(2)}) copy-start(bf16[768,256]{1,0:T(8,128)(2,1)} %param.13) | copy-start | bytes 1179652
  112.3 47.1 %all-to-all-start.2 = ((bf16[128,16,768]{2,1,0:T(8,128)(2,1)}), bf16[128,16,768]{2,1,0:T(8,128)(2,1)}, u32[]{:S(2)}, u32[]{:S(2)}) async-start(bf16[128,16,768]{2,1,0:T(8,128)(2,1)} %bitcast.83), calls=%async_computation.3 | async-start | bytes 6291456 | tf_op jit(solution)/shard_map/all_to_all | solution.py:59
  118.4 47.1 %all-gather.6.cloned.1.call-start = ((), (), s32[]{:S(2)}) async-start(), calls=%async_computation.5 | async-start | bytes 2359296 | tf_op jit(solution)/shard_map/all_gather | solution.py:108
  123.9 4.6 %copy-start.15 = (bf16[1,1536,1024]{2,1,0:T(8,128)(2,1)S(1)}, bf16[1,1536,1024]{2,1,0:T(8,128)(2,1)}, u32[]{:S(2)}) copy-start(bf16[1,1536,1024]{2,1,0:T(8,128)(2,1)} %all-gather.8.cloned.1.call-done) | copy-start | bytes 9437188
  128.5 5.4 %copy-start.16 = (bf16[1,512,1536]{1,2,0:T(8,128)(2,1)S(1)}, bf16[1,512,1536]{1,2,0:T(8,128)(2,1)}, u32[]{:S(2)}) copy-start(bf16[1,512,1536]{1,2,0:T(8,128)(2,1)} %all-gather.10.cloned.1.call-done) | copy-start | bytes 4718596
  159.4 47.0 %all-to-all-start.3 = ((bf16[128,16,768]{2,1,0:T(8,128)(2,1)}), bf16[128,16,768]{2,1,0:T(8,128)(2,1)}, u32[]{:S(2)}, u32[]{:S(2)}) async-start(bf16[128,16,768]{2,1,0:T(8,128)(2,1)} %bitcast.82), calls=%async_computation.4 | async-start | bytes 6291456 | tf_op jit(solution)/shard_map/all_to_all | solution.py:59
  165.4 51.7 %reduce-scatter.2.cloned.1.call-start = ((), (), s32[]{:S(2)}) async-start(), calls=%async_computation.6 | async-start | bytes 2359296 | tf_op jit(solution)/shard_map/reduce_scatter | solution.py:133
  171.8 2.4 %copy-start.9 = (s32[512,1]{0,1:T(1,128)S(1)}, s32[512,1]{0,1:T(1,128)}, u32[]{:S(2)}) copy-start(s32[512,1]{0,1:T(1,128)} %copy-done.8) | copy-start | bytes 6148
  171.8 2.4 %copy-start.11 = (s32[512,1]{0,1:T(1,128)S(1)}, s32[512,1]{0,1:T(1,128)}, u32[]{:S(2)}) copy-start(s32[512,1]{0,1:T(1,128)} %copy-done.10) | copy-start | bytes 6148
  174.2 2.7 %copy-start.4 = (f32[512,320]{0,1:T(8,128)}, f32[512,320]{0,1:T(8,128)S(1)}, u32[]{:S(2)}) copy-start(f32[512,320]{0,1:T(8,128)S(1)} %convolution_bitcast_fusion.2) | copy-start | bytes 1966084
  206.4 5.7 %copy-start.1 = (bf16[64,32,512]{2,1,0:T(8,128)(2,1)S(1)}, bf16[64,32,512]{2,1,0:T(8,128)(2,1)}, u32[]{:S(2)}) copy-start(bf16[64,32,512]{2,1,0:T(8,128)(2,1)} %get-tuple-element.20) | copy-start | bytes 6291460
  212.1 4.9 %copy-start.5 = (bf16[256,768]{1,0:T(8,128)(2,1)S(1)}, bf16[256,768]{1,0:T(8,128)(2,1)}, u32[]{:S(2)}) copy-start(bf16[256,768]{1,0:T(8,128)(2,1)} %param.14) | copy-start | bytes 1179652
  212.1 4.9 %copy-start.12 = (s32[512]{0:T(512)S(1)}, s32[512]{0:T(512)}, u32[]{:S(2)}) copy-start(s32[512]{0:T(512)} %select_reduce_fusion) | copy-start | bytes 6148
  212.1 4.9 %copy-start.13 = (s32[256]{0:T(256)S(1)}, s32[256]{0:T(256)}, u32[]{:S(2)}) copy-start(s32[256]{0:T(256)} %and_select_fusion) | copy-start | bytes 3076
  (2 other events, 1.2 us)
Sparse Core Ops, SparseCore 0:
  26.7 16.4 all-gather.7
  73.7 14.2 all-gather.9
  120.8 14.2 all-gather.5
  171.9 13.5 reduce-scatter.1

commit v4 on v2

--- a/solution.py
+++ b/solution.py
@@ -4,6 +4,20 @@
 from jax.sharding import PartitionSpec as P
 
 RANK = 16
+
+
+def partner(x):
+    return lax.ppermute(x, "blk", [(0, 1), (1, 0)])
+
+
+def gather_blk(x, axis, stack=False):
+    other = partner(x)
+    mine = lax.axis_index("blk")
+    first = jnp.where(mine == 0, x, other)
+    second = jnp.where(mine == 0, other, x)
+    if stack:
+        return jnp.stack([first, second], axis=axis)
+    return jnp.concatenate([first, second], axis=axis)
 
 
 def body(
@@ -63,12 +77,12 @@
     )
     rows_in = received.reshape(req_count, blk_count, pad_rows, feat_local)
 
-    weight_gate_up = lax.all_gather(expert_gate_up[0], "blk", axis=0, tiled=True)
-    weight_down = lax.all_gather(expert_down[0], "blk", axis=1, tiled=True)
+    weight_gate_up = gather_blk(expert_gate_up[0], 0, stack=True)
+    weight_down = gather_blk(expert_down[0], 1, stack=True)
     gate_up = jnp.einsum(
         "gcsd,cdf->gsf",
         rows_in,
-        weight_gate_up.reshape(blk_count, feat_local, 2 * hidden_width),
+        weight_gate_up,
         preferred_element_type=jnp.float32,
     )
     hidden = (jax.nn.silu(gate_up[..., :hidden_width]) * gate_up[..., hidden_width:]).astype(
@@ -77,7 +91,7 @@
     expert_out = jnp.einsum(
         "gsh,hcd->gcsd",
         hidden,
-        weight_down.reshape(hidden_width, blk_count, feat_local),
+        weight_down,
         preferred_element_type=jnp.float32,
     ).astype(jnp.bfloat16)
     returned = lax.all_to_all(
@@ -88,10 +102,8 @@
         tiled=True,
     )
 
-    normed_full = lax.all_gather(normed, "blk", axis=1, tiled=True)
-    small_w = lax.all_gather(
-        jnp.concatenate([router, adapter_down], axis=1), "blk", axis=0, tiled=True
-    )
+    normed_full = gather_blk(normed, 1)
+    small_w = gather_blk(jnp.concatenate([router, adapter_down], axis=1), 0)
     small = jnp.dot(normed_full, small_w, preferred_element_type=jnp.float32)
     logits = small[:, :expert_count]
     low_all = small[:, expert_count:]
@@ -113,23 +125,28 @@
         jax.nn.silu(shared_pre[:, :shared_local]) * shared_pre[:, shared_local:]
     ).astype(jnp.bfloat16)
     shared_terms = jnp.dot(shared_hidden, shared_down, preferred_element_type=jnp.float32)
-    shared_out = lax.psum_scatter(
-        shared_terms.astype(jnp.bfloat16), "blk", scatter_dimension=1, tiled=True
-    ).astype(jnp.float32)
+    terms = shared_terms.astype(jnp.bfloat16).reshape(tok_rows, blk_count, feat_local)
+    mine = lax.axis_index("blk")
+    keep = jnp.where(mine == 0, terms[:, 0], terms[:, 1])
+    give = jnp.where(mine == 0, terms[:, 1], terms[:, 0])
+    shared_out = (keep + partner(give)).astype(jnp.float32)
 
     chosen = jnp.where(has > 0, jax.nn.sigmoid(logits), 0.0)
     gate = chosen / jnp.sum(chosen, axis=1, keepdims=True)
-    gate_rows = jnp.broadcast_to(
-        gate.T[:, None, :], (expert_count, blk_count * pad_rows, tok_rows)
-    ).reshape(chunk_count * pad_rows, tok_rows)
-    weights = jnp.where(pick, gate_rows, 0.0)
+    rows_per_expert = blk_count * pad_rows
+    rank_cols = jnp.broadcast_to(
+        rank[:, :, None], (tok_rows, expert_count, rows_per_expert)
+    ).reshape(tok_rows, chunk_count * pad_rows)
+    gate_cols = jnp.broadcast_to(
+        gate[:, :, None], (tok_rows, expert_count, rows_per_expert)
+    ).reshape(tok_rows, chunk_count * pad_rows)
+    weights = jnp.where(rank_cols == row_slot[None, :], gate_cols, 0.0)
     weights_hi = weights.astype(jnp.bfloat16)
     weights_lo = (weights - weights_hi.astype(jnp.float32)).astype(jnp.bfloat16)
     back = returned.reshape(chunk_count * pad_rows, feat_local)
-    contract = (((0,), (0,)), ((), ()))
-    routed = lax.dot_general(
-        weights_hi, back, contract, preferred_element_type=jnp.float32
-    ) + lax.dot_general(weights_lo, back, contract, preferred_element_type=jnp.float32)
+    routed = jnp.dot(weights_hi, back, preferred_element_type=jnp.float32) + jnp.dot(
+        weights_lo, back, preferred_element_type=jnp.float32
+    )
     return (shared_out + 0.5 * delta + routed).astype(jnp.bfloat16)
 
 

time: 229 us -> 220 us (0.961)
  matrix products: 53.3 us -> 40.4 us
  between operations: 13.3 us -> 0.42 us
  local copies, waits for them, and re-layouts: 7.54 us -> 20.2 us
  other arithmetic: 7.56 us -> 17.4 us
  waiting for transfers between devices: 128 us -> 124 us
  blocking collectives: 2.83 us -> 0 us
    all_gather x3 -> x0, waiting for transfers between devices: 24.7 us -> none  [the longest x1 17 us: body(): lax.all_gather(expert_gate_up[0], 'blk', axis=0, tiled=True)]
    all_to_all x1, waiting for transfers between devices: 57.1 us -> 67 us  [body(): lax.all_to_all(send_rows.reshape(chunk_count, pad_rows, feat_local), both...]
    dot_general x4, matrix products: 35.8 us -> 26.5 us  [the longest x1 9.69 us: body(): jnp.einsum('gcsd,cdf->gsf', rows_in, weight_gate_up, preferred_element_ty...]
    all_to_all x1, waiting for transfers between devices: 44.4 us -> 52.2 us  [body(): lax.all_to_all(expert_out.reshape(req_count * blk_count, pad_rows, feat_l...]
    convert_element_type x0 -> x1, local copies, waits for them, and re-layouts: none -> 6.16 us  [body(): expert_out = jnp.einsum('gsh,hcd->gcsd', hidden, weight_down, preferred_e...]
    ppermute x0 -> x5, waiting for transfers between devices: none -> 4.88 us  [partner(): return lax.ppermute(x, 'blk', [(0, 1), (1, 0)])]
    another operation x1 -> x3, other arithmetic: 0.18 us -> 4.64 us  [the longest x2 4.46 us: gather_blk(): return jnp.stack([first, second], axis=axis)]
    reshape x0 -> x1, local copies, waits for them, and re-layouts: none -> 3.63 us  [body(): shared_terms.astype(jnp.bfloat16).reshape(tok_rows, blk_count, feat_local)]
  transfers between devices with their start and end apart: 6 -> 7, of which waited for: 4 -> 4; matrix products, arithmetic and copies ran while one was open for 20% -> 21% of each run, Pallas kernels for 0% -> 0%
where the time goes in v4:
time: 220 us
  waiting for transfers between devices  124 us (56%)
  matrix products  40.4 us (18%)
  local copies, waits for them, and re-layouts  20.2 us (9%)
  starting transfers between devices  17.4 us (8%)
  other arithmetic  17.4 us (8%)
    all_to_all x1, waiting for transfers between devices, body(): lax.all_to_all(send_rows.reshape(chunk_count, pad_rows, feat_local), both...  67 us
    all_to_all x1, waiting for transfers between devices, body(): lax.all_to_all(expert_out.reshape(req_count * blk_count, pad_rows, feat_l...  52.2 us
    all_to_all x1, starting transfers between devices, body(): lax.all_to_all(send_rows.reshape(chunk_count, pad_rows, feat_local), both...  10.9 us
    dot_general x1, matrix products, body(): jnp.einsum('gcsd,cdf->gsf', rows_in, weight_gate_up, preferred_element_ty...  9.69 us
    dot_general x1, matrix products, body(): jnp.dot(weights_lo, back, preferred_element_type=jnp.float32)  7.23 us
    unnamed x48, local copies, waits for them, and re-layouts  7.2 us
    convert_element_type x1, local copies, waits for them, and re-layouts, body(): expert_out = jnp.einsum('gsh,hcd->gcsd', hidden, weight_down, preferred_e...  6.16 us
    dot_general x1, matrix products, body(): jnp.dot(weights_hi, back, preferred_element_type=jnp.float32)  5.82 us
  transfers between devices with their start and end apart: 7, of which 4 were waited for; matrix products, arithmetic and copies ran while one was open for 21% of the time, Pallas kernels for 0%

profile of v4, /device:TPU:2, one launch (start us, length us, event | category | flops | bytes accessed | tf_op | source)
XLA Modules:
  0.0 219.8 jit_solution(10057823721026798920)
XLA Ops:
  1.3 1.7 pad_maximum_fusion.3
  8.7 1.3 bitcast_compare_fusion
  10.1 5.3 %convolution_convert_fusion = bf16[4096,768]{1,0:T(8,128)(2,1)} fusion(pred[4096,512]{1,0:T(32,128)(4,1)S(1)} %bitcast_compare_fusion, bf16[512,768]{1,0:T(8,128)(2,1)S(1)} %copy-done.7), kind=kOutput, calls=%fused_computation.4 | convolution fusion | flops 3224371200 | bytes 9175040 | tf_op jit(solution)/shard_map/dot_general | solution.py:67
  15.4 10.9 %all-to-all-start = ((bf16[128,32,768]{2,1,0:T(8,128)(2,1)}), bf16[128,32,768]{2,1,0:T(8,128)(2,1)}, u32[]{:S(2)}, u32[]{:S(2)}) async-start(bf16[128,32,768]{2,1,0:T(8,128)(2,1)} %bitcast.70), calls=%async_computation | async-start | bytes 12582912 | tf_op jit(solution)/shard_map/all_to_all | solution.py:71
  26.9 4.0 %collective-permute-done.3 = bf16[512,768]{1,0:T(8,128)(2,1)S(1)} collective-permute-done((bf16[512,768]{1,0:T(8,128)(2,1)}, bf16[512,768]{1,0:T(8,128)(2,1)S(1)}, u32[]{:S(2)}, u32[]{:S(2)}) %collective-permute-start.3) | collective-permute-done | bytes 786464 | tf_op jit(solution)/shard_map/ppermute | solution.py:10
  30.9 2.4 %select_bitcast_fusion.3 = (bf16[512,1,768]{2,0,1:T(8,128)(2,1)}, bf16[512,1,768]{2,0,1:T(8,128)(2,1)}) fusion(bf16[512,768]{1,0:T(8,128)(2,1)S(1)} %collective-permute-done.3, pred[]{:T(512)S(6)} %eq.204, bf16[1,512,768]{2,1,0:T(8,128)(2,1)} %param.18), kind=kLoop, calls=%fused_computation.33 | loop fusion | flops 786432 | bytes 3145729 | tf_op jit(solution)/shard_map/stack | solution.py:19
  33.3 2.1 select_bitcast_fusion.1
  35.4 67.0 %all-to-all-done = bf16[128,32,768]{2,1,0:T(8,128)(2,1)} async-done(((bf16[128,32,768]{2,1,0:T(8,128)(2,1)}), bf16[128,32,768]{2,1,0:T(8,128)(2,1)}, u32[]{:S(2)}, u32[]{:S(2)}) %all-to-all-start) | async-done | bytes 6291488 | tf_op jit(solution)/shard_map/all_to_all | solution.py:71
  102.4 9.7 %convolution_bitcast_fusion = f32[64,32,1024]{2,1,0:T(8,128)S(1)} fusion(bf16[64,2,32,768]{3,2,1,0:T(8,128)(2,1)} %bitcast.20, bf16[1,768,1024]{2,1,0:T(8,128)(2,1)} %get-tuple-element.6, bf16[1,768,1024]{2,1,0:T(8,128)(2,1)} %get-tuple-element.5), kind=kOutput, calls=%fused_computation.8 | convolution fusion | flops 6444023808 | bytes 17825792 | tf_op jit(solution)/shard_map/gcsd,cdf->gsf/dot_general | solution.py:82
  112.1 1.5 fusion.1
  113.6 3.8 %convert_bitcast_fusion = bf16[64,2,32,768]{3,0,2,1:T(8,128)(2,1)S(1)} fusion(bf16[64,32,512]{2,1,0:T(8,128)(2,1)S(1)} %fusion.1, bf16[512,1,768]{2,0,1:T(8,128)(2,1)S(1)} %copy-done.13, bf16[512,1,768]{2,0,1:T(8,128)(2,1)S(1)} %copy-done.12), kind=kOutput, calls=%fused_computation.5 | convolution fusion | flops 3227516928 | bytes 9961472 | tf_op jit(solution)/shard_map/gsh,hcd->gcsd/dot_general | solution.py:91
  117.4 6.2 %copy.32 = bf16[64,2,32,768]{3,2,1,0:T(8,128)(2,1)} copy(bf16[64,2,32,768]{3,0,2,1:T(8,128)(2,1)S(1)} %convert_bitcast_fusion) | data formatting | bytes 12582912 | tf_op jit(solution)/shard_map/convert_element_type | solution.py:96
  123.5 5.3 %all-to-all-start.1 = ((bf16[128,32,768]{2,1,0:T(8,128)(2,1)}), bf16[128,32,768]{2,1,0:T(8,128)(2,1)}, u32[]{:S(2)}, u32[]{:S(2)}) async-start(bf16[128,32,768]{2,1,0:T(8,128)(2,1)} %bitcast.69), calls=%async_computation.1 | async-start | bytes 12582912 | tf_op jit(solution)/shard_map/all_to_all | solution.py:97
  128.9 4.5 %copy.37 = bf16[192,8,2,512]{3,1,2,0:T(8,128)(2,1)} copy(bf16[192,8,2,512]{3,2,1,0:T(2,128)(2,1)} %bitcast.73) | data formatting | bytes 6291456
  133.8 3.7 %fusion.11 = f32[512,1024]{1,0:T(8,128)S(1)} fusion(bf16[1536,1024]{1,0:T(8,128)(2,1)} %bitcast.74, bf16[512,768]{1,0:T(8,128)(2,1)S(1)} %copy-done.11, bf16[512,768]{1,0:T(8,128)(2,1)S(1)} %copy-done.9), kind=kOutput, calls=%fused_computation.27 | convolution fusion | flops 1613758464 | bytes 6815744 | tf_op jit(solution)/shard_map/dot_general | solution.py:123
  137.5 2.2 convolution_convert_fusion.1
  139.7 3.6 %reshape.210 = bf16[512,2,768]{2,1,0:T(2,128)(2,1)S(1)} reshape(bf16[512,1536]{1,0:T(8,128)(2,1)} %convolution_convert_fusion.1) | data formatting | bytes 3145728 | tf_op jit(solution)/shard_map/reshape | solution.py:128
  143.3 2.2 %fusion.68 = (bf16[512,1,768]{2,1,0:T(2,128)(2,1)S(1)}, bf16[512,1,768]{2,1,0:T(2,128)(2,1)S(1)}) fusion(bf16[512,2,768]{2,1,0:T(2,128)(2,1)S(1)} %reshape.210), kind=kLoop, calls=%fused_computation.129 | loop fusion | bytes 3145728 | tf_op jit(solution)/shard_map/slice | solution.py:130
  147.5 2.6 %select_convert_fusion = bf16[512,64,64]{0,2,1:T(8,128)(2,1)} fusion(f32[512,64]{0,1:T(8,128)S(1)} %broadcast_divide_fusion, s32[64,64]{1,0:T(8,128)S(1)} %fusion.42, s32[512,64]{0,1:T(8,128)S(1)} %get-tuple-element.21), kind=kLoop, calls=%fused_computation.1 | loop fusion | flops 4194304 | bytes 4472832 | tf_op jit(solution)/shard_map/convert_element_type | solution.py:144
  150.1 2.6 %fusion = bf16[512,64,64]{0,2,1:T(8,128)(2,1)} fusion(f32[512,64]{0,1:T(8,128)S(1)} %broadcast_divide_fusion, s32[64,64]{1,0:T(8,128)S(1)} %fusion.42, s32[512,64]{0,1:T(8,128)S(1)} %get-tuple-element.21), kind=kLoop, calls=%fused_computation.2 | loop fusion | flops 12582912 | bytes 4472832 | tf_op jit(solution)/shard_map/convert_element_type | solution.py:145
  152.7 52.2 %all-to-all-done.1 = bf16[128,32,768]{2,1,0:T(8,128)(2,1)} async-done(((bf16[128,32,768]{2,1,0:T(8,128)(2,1)}), bf16[128,32,768]{2,1,0:T(8,128)(2,1)}, u32[]{:S(2)}, u32[]{:S(2)}) %all-to-all-start.1) | async-done | bytes 6291488 | tf_op jit(solution)/shard_map/all_to_all | solution.py:97
  204.9 7.2 %fusion.71 = f32[512,768]{1,0:T(8,128)S(1)} fusion(bf16[512,4096]{0,1:T(8,128)(2,1)} %bitcast.72, bf16[4096,768]{1,0:T(8,128)(2,1)} %bitcast.30), kind=kOutput, calls=%fused_computation.132 | convolution fusion | flops 3221225472 | bytes 12058624 | tf_op jit(solution)/shard_map/dot_general | solution.py:147
  212.2 5.8 %fusion.70 = f32[512,768]{1,0:T(8,128)S(1)} fusion(bf16[512,4096]{0,1:T(8,128)(2,1)S(1)} %bitcast.71, bf16[4096,768]{1,0:T(8,128)(2,1)} %bitcast.30), kind=kOutput, calls=%fused_computation.131 | convolution fusion | flops 3221225472 | bytes 12058624 | tf_op jit(solution)/shard_map/dot_general | solution.py:147
  218.1 1.7 add_convert_fusion
  (70 shorter events, 9.8 us)
Async XLA Ops:
  0.0 137.5 %copy-start = (bf16[512,1536]{1,0:T(8,128)(2,1)S(1)}, bf16[512,1536]{1,0:T(8,128)(2,1)}, u32[]{:S(2)}) copy-start(bf16[512,1536]{1,0:T(8,128)(2,1)} %param.16) | copy-start | bytes 4718596
  0.0 6.5 %copy-start.7 = (bf16[512,768]{1,0:T(8,128)(2,1)S(1)}, bf16[512,768]{1,0:T(8,128)(2,1)}, u32[]{:S(2)}) copy-start(bf16[512,768]{1,0:T(8,128)(2,1)} %param.11) | copy-start | bytes 2359300
  0.0 6.5 %collective-permute-start = (bf16[512,768]{1,0:T(8,128)(2,1)}, bf16[512,768]{1,0:T(8,128)(2,1)S(1)}, u32[]{:S(2)}, u32[]{:S(2)}) collective-permute-start(bf16[512,768]{1,0:T(8,128)(2,1)} %param.11), channel_id=1, source_target_pairs={{0,1},{1,0},{2,3},{3,2},{4,5},{5,4},{6,7},{7,6},{8,9},{9,8},{10,11... | collective-permute-start | bytes 2359304 | tf_op jit(solution)/shard_map/ppermute | solution.py:10
  3.0 2.2 %collective-permute-start.2 = (bf16[768,320]{0,1:T(8,128)(2,1)}, bf16[768,320]{0,1:T(8,128)(2,1)}, u32[]{:S(2)}, u32[]{:S(2)}) collective-permute-start(bf16[768,320]{0,1:T(8,128)(2,1)} %pad_maximum_fusion.3), channel_id=1, source_target_pairs={{0,1},{1,0},{2,3},{3,2},{4,5},{5,4},{6,7},{7,6},{8,9},{9,8},{10,11... | collective-permute-start | bytes 1474568 | tf_op jit(solution)/shard_map/ppermute | solution.py:10
  4.4 3.7 %copy-start.17 = (s32[512,1]{0,1:T(1,128)}, s32[512,1]{0,1:T(1,128)S(1)}, u32[]{:S(2)}) copy-start(s32[512,1]{0,1:T(1,128)S(1)} %get-tuple-element.19) | copy-start | bytes 6148
  4.4 3.7 %copy-start.19 = (s32[512,1]{0,1:T(1,128)}, s32[512,1]{0,1:T(1,128)S(1)}, u32[]{:S(2)}) copy-start(s32[512,1]{0,1:T(1,128)S(1)} %get-tuple-element.20) | copy-start | bytes 6148
  15.4 10.9 %copy-start.6 = (bf16[1,768,1024]{2,1,0:T(8,128)(2,1)S(1)}, bf16[1,768,1024]{2,1,0:T(8,128)(2,1)}, u32[]{:S(2)}) copy-start(bf16[1,768,1024]{2,1,0:T(8,128)(2,1)} %param.17) | copy-start | bytes 4718596
  15.4 87.0 %all-to-all-start = ((bf16[128,32,768]{2,1,0:T(8,128)(2,1)}), bf16[128,32,768]{2,1,0:T(8,128)(2,1)}, u32[]{:S(2)}, u32[]{:S(2)}) async-start(bf16[128,32,768]{2,1,0:T(8,128)(2,1)} %bitcast.70), calls=%async_computation | async-start | bytes 12582912 | tf_op jit(solution)/shard_map/all_to_all | solution.py:71
  26.3 7.0 %collective-permute-start.4 = (bf16[768,1024]{1,0:T(8,128)(2,1)S(1)}, bf16[768,1024]{1,0:T(8,128)(2,1)S(1)}, u32[]{:S(2)}, u32[]{:S(2)}) collective-permute-start(bf16[768,1024]{1,0:T(8,128)(2,1)S(1)} %bitcast.75), channel_id=1, source_target_pairs={{0,1},{1,0},{2,3},{3,2},{4,5},{5,4},{6,7},{7,6},{8,9},{9,8},{10,11... | collective-permute-start | bytes 4718600 | tf_op jit(solution)/shard_map/ppermute | solution.py:10
  26.5 4.4 %collective-permute-start.3 = (bf16[512,768]{1,0:T(8,128)(2,1)}, bf16[512,768]{1,0:T(8,128)(2,1)S(1)}, u32[]{:S(2)}, u32[]{:S(2)}) collective-permute-start(bf16[512,768]{1,0:T(8,128)(2,1)} %bitcast.76), channel_id=1, source_target_pairs={{0,1},{1,0},{2,3},{3,2},{4,5},{5,4},{6,7},{7,6},{8,9},{9,8},{10,11... | collective-permute-start | bytes 2359304 | tf_op jit(solution)/shard_map/ppermute | solution.py:10
  112.1 1.5 copy-start.12
  123.5 81.4 %all-to-all-start.1 = ((bf16[128,32,768]{2,1,0:T(8,128)(2,1)}), bf16[128,32,768]{2,1,0:T(8,128)(2,1)}, u32[]{:S(2)}, u32[]{:S(2)}) async-start(bf16[128,32,768]{2,1,0:T(8,128)(2,1)} %bitcast.69), calls=%async_computation.1 | async-start | bytes 12582912 | tf_op jit(solution)/shard_map/all_to_all | solution.py:97
  128.8 4.6 %copy-start.22 = (s32[1,4]{1,0:T(1,128)S(1)}, s32[1,4]{1,0:T(1,128)}, u32[]{:S(2)}) copy-start(s32[1,4]{1,0:T(1,128)} %param.19) | copy-start | bytes 52
  128.8 4.9 %copy-start.21 = (s32[1,4]{1,0:T(1,128)S(1)}, s32[1,4]{1,0:T(1,128)}, u32[]{:S(2)}) copy-start(s32[1,4]{1,0:T(1,128)} %param.20) | copy-start | bytes 52
  128.9 4.9 %copy-start.9 = (bf16[512,768]{1,0:T(8,128)(2,1)S(1)}, bf16[512,768]{1,0:T(8,128)(2,1)}, u32[]{:S(2)}) copy-start(bf16[512,768]{1,0:T(8,128)(2,1)} %copy-done.8) | copy-start | bytes 2359300
  128.9 4.9 %copy-start.11 = (bf16[512,768]{1,0:T(8,128)(2,1)S(1)}, bf16[512,768]{1,0:T(8,128)(2,1)}, u32[]{:S(2)}) copy-start(bf16[512,768]{1,0:T(8,128)(2,1)} %copy-done.10) | copy-start | bytes 2359300
  145.6 1.9 copy-start.1
  145.6 1.9 copy-start.3
  145.8 72.2 %collective-permute-start.1 = (bf16[512,768]{1,0:T(8,128)(2,1)S(1)}, bf16[512,768]{1,0:T(8,128)(2,1)S(1)}, u32[]{:S(2)}, u32[]{:S(2)}) collective-permute-start(bf16[512,768]{1,0:T(8,128)(2,1)S(1)} %select_bitcast_fusion.4), channel_id=1, source_target_pairs={{0,1},{1,0},{2,3},{3,2},{4,5},{5,4},{6,7},{7,6},{8,9},{9,8},{10,11... | collective-permute-start | bytes 2359304 | tf_op jit(solution)/shard_map/ppermute | solution.py:10
  204.9 7.2 %copy-start.5 = (bf16[512,64,64]{0,2,1:T(8,128)(2,1)S(1)}, bf16[512,64,64]{0,2,1:T(8,128)(2,1)}, u32[]{:S(2)}) copy-start(bf16[512,64,64]{0,2,1:T(8,128)(2,1)} %select_convert_fusion) | copy-start | bytes 12582916
  212.2 5.9 %copy-start.2 = (bf16[512,1,768]{2,1,0:T(2,128)(2,1)S(1)}, bf16[512,1,768]{2,1,0:T(2,128)(2,1)}, u32[]{:S(2)}) copy-start(bf16[512,1,768]{2,1,0:T(2,128)(2,1)} %copy-done.1) | copy-start | bytes 2359300
  212.2 5.9 %copy-start.4 = (bf16[512,1,768]{2,1,0:T(2,128)(2,1)S(1)}, bf16[512,1,768]{2,1,0:T(2,128)(2,1)}, u32[]{:S(2)}) copy-start(bf16[512,1,768]{2,1,0:T(2,128)(2,1)} %copy-done.3) | copy-start | bytes 2359300
  212.2 5.9 %copy-start.15 = (f32[512,320]{0,1:T(8,128)S(1)}, f32[512,320]{0,1:T(8,128)}, u32[]{:S(2)}) copy-start(f32[512,320]{0,1:T(8,128)} %copy-done.14) | copy-start | bytes 1966084
  212.2 5.9 %copy-start.16 = (bf16[256,768]{1,0:T(8,128)(2,1)S(1)}, bf16[256,768]{1,0:T(8,128)(2,1)}, u32[]{:S(2)}) copy-start(bf16[256,768]{1,0:T(8,128)(2,1)} %param.14) | copy-start | bytes 1179652
  (6 other events, 5.8 us)

commit v5 on v4

--- a/solution.py
+++ b/solution.py
@@ -78,7 +78,7 @@
     rows_in = received.reshape(req_count, blk_count, pad_rows, feat_local)
 
     weight_gate_up = gather_blk(expert_gate_up[0], 0, stack=True)
-    weight_down = gather_blk(expert_down[0], 1, stack=True)
+    weight_down = gather_blk(expert_down[0].T, 0, stack=True)
     gate_up = jnp.einsum(
         "gcsd,cdf->gsf",
         rows_in,
@@ -89,7 +89,7 @@
         jnp.bfloat16
     )
     expert_out = jnp.einsum(
-        "gsh,hcd->gcsd",
+        "gsh,cdh->gcsd",
         hidden,
         weight_down,
         preferred_element_type=jnp.float32,
@@ -102,7 +102,10 @@
         tiled=True,
     )
 
-    normed_full = gather_blk(normed, 1)
+    send_rows, router, adapter_down, normed_late = lax.optimization_barrier(
+        (send_rows, router, adapter_down, normed)
+    )
+    normed_full = gather_blk(normed_late, 1)
     small_w = gather_blk(jnp.concatenate([router, adapter_down], axis=1), 0)
     small = jnp.dot(normed_full, small_w, preferred_element_type=jnp.float32)
     logits = small[:, :expert_count]

time: 220 us -> 213 us (0.968)
  waiting for transfers between devices: 124 us -> 115 us
  other arithmetic: 17.4 us -> 21.3 us
    all_to_all x1, waiting for transfers between devices: 52.2 us -> 44.7 us  [body(): lax.all_to_all(expert_out.reshape(req_count * blk_count, pad_rows, feat_l...]
    unnamed x48 -> x60, local copies, waits for them, and re-layouts: 7.2 us -> 5.1 us
  transfers between devices with their start and end apart: 7 -> 7, of which waited for: 4 -> 3; matrix products, arithmetic and copies ran while one was open for 21% -> 22% of each run, Pallas kernels for 0% -> 0%
where the time goes in v5:
time: 213 us
  waiting for transfers between devices  115 us (54%)
  matrix products  38.8 us (18%)
  other arithmetic  21.3 us (10%)
  local copies, waits for them, and re-layouts  19.3 us (9%)
  starting transfers between devices  17.8 us (8%)
    all_to_all x1, waiting for transfers between devices, body(): lax.all_to_all(send_rows.reshape(chunk_count, pad_rows, feat_local), both...  66.7 us
    all_to_all x1, waiting for transfers between devices, body(): lax.all_to_all(expert_out.reshape(req_count * blk_count, pad_rows, feat_l...  44.7 us
    all_to_all x1, starting transfers between devices, body(): lax.all_to_all(send_rows.reshape(chunk_count, pad_rows, feat_local), both...  10.9 us
    dot_general x1, matrix products, body(): jnp.einsum('gcsd,cdf->gsf', rows_in, weight_gate_up, preferred_element_ty...  9.21 us
    dot_general x1, matrix products, body(): jnp.dot(weights_lo, back, preferred_element_type=jnp.float32)  7.23 us
    convert_element_type x1, local copies, waits for them, and re-layouts, body(): expert_out = jnp.einsum('gsh,cdh->gcsd', hidden, weight_down, preferred_e...  6.18 us
    dot_general x1, matrix products, body(): jnp.dot(weights_hi, back, preferred_element_type=jnp.float32)  5.82 us
    dot_general x1, matrix products, body(): jnp.dot(pick.astype(jnp.bfloat16), normed, preferred_element_type=jnp.flo...  5.31 us
  transfers between devices with their start and end apart: 7, of which 3 were waited for; matrix products, arithmetic and copies ran while one was open for 22% of the time, Pallas kernels for 0%

profile of v5, /device:TPU:2, one launch (start us, length us, event | category | flops | bytes accessed | tf_op | source)
XLA Modules:
  0.0 212.8 jit_solution(7026132313352574712)
XLA Ops:
  3.3 5.3 %convolution_convert_fusion = bf16[4096,768]{1,0:T(8,128)(2,1)} fusion(pred[4096,512]{1,0:T(32,128)(4,1)S(1)} %bitcast_compare_fusion, bf16[512,768]{1,0:T(8,128)(2,1)S(1)} %copy-done.7), kind=kOutput, calls=%fused_computation.4 | convolution fusion | flops 3224371200 | bytes 9175040 | tf_op jit(solution)/shard_map/dot_general | solution.py:67
  8.6 10.9 %all-to-all-start = ((bf16[128,32,768]{2,1,0:T(8,128)(2,1)}), bf16[128,32,768]{2,1,0:T(8,128)(2,1)}, u32[]{:S(2)}, u32[]{:S(2)}) async-start(bf16[128,32,768]{2,1,0:T(8,128)(2,1)} %bitcast.72), calls=%async_computation | async-start | bytes 12582912 | tf_op jit(solution)/shard_map/all_to_all | solution.py:71
  20.7 3.7 %collective-permute-done.3 = bf16[768,512]{1,0:T(8,128)(2,1)S(1)} collective-permute-done((bf16[768,512]{1,0:T(8,128)(2,1)S(1)}, bf16[768,512]{1,0:T(8,128)(2,1)S(1)}, u32[]{:S(2)}, u32[]{:S(2)}) %collective-permute-start.3) | collective-permute-done | bytes 786464 | tf_op jit(solution)/shard_map/ppermute | solution.py:10
  25.6 3.2 %select_bitcast_fusion.1 = (bf16[1,768,1024]{2,1,0:T(8,128)(2,1)S(1)}, bf16[1,768,1024]{2,1,0:T(8,128)(2,1)}) fusion(bf16[768,1024]{1,0:T(8,128)(2,1)} %collective-permute-done.4, pred[]{:T(512)S(6)} %eq.204, bf16[1,768,1024]{2,1,0:T(8,128)(2,1)} %param.17), kind=kLoop, calls=%fused_computation.21 | loop fusion | flops 1572864 | bytes 6291457 | tf_op jit(solution)/shard_map/stack | solution.py:19
  28.9 66.7 %all-to-all-done = bf16[128,32,768]{2,1,0:T(8,128)(2,1)} async-done(((bf16[128,32,768]{2,1,0:T(8,128)(2,1)}), bf16[128,32,768]{2,1,0:T(8,128)(2,1)}, u32[]{:S(2)}, u32[]{:S(2)}) %all-to-all-start) | async-done | bytes 6291488 | tf_op jit(solution)/shard_map/all_to_all | solution.py:71
  95.6 9.2 %convolution_bitcast_fusion = f32[64,32,1024]{2,1,0:T(8,128)S(1)} fusion(bf16[64,2,32,768]{3,2,1,0:T(8,128)(2,1)} %bitcast.22, bf16[1,768,1024]{2,1,0:T(8,128)(2,1)} %get-tuple-element.12, bf16[1,768,1024]{2,1,0:T(8,128)(2,1)S(1)} %get-tuple-element.11), kind=kOutput, calls=%fused_computation.8 | convolution fusion | flops 6444023808 | bytes 17825792 | tf_op jit(solution)/shard_map/gcsd,cdf->gsf/dot_general | solution.py:82
  104.9 1.5 fusion.1
  106.4 3.9 %convert_bitcast_fusion = bf16[64,2,32,768]{3,0,2,1:T(8,128)(2,1)S(1)} fusion(bf16[64,32,512]{2,1,0:T(8,128)(2,1)S(1)} %fusion.1, bf16[1,768,512]{2,1,0:T(8,128)(2,1)S(1)} %copy-done.10, bf16[1,768,512]{2,1,0:T(8,128)(2,1)S(1)} %copy-done.9), kind=kOutput, calls=%fused_computation.5 | convolution fusion | flops 3227516928 | bytes 9961472 | tf_op jit(solution)/shard_map/gsh,cdh->gcsd/dot_general | solution.py:91
  110.3 6.2 %copy.36 = bf16[64,2,32,768]{3,2,1,0:T(8,128)(2,1)} copy(bf16[64,2,32,768]{3,0,2,1:T(8,128)(2,1)S(1)} %convert_bitcast_fusion) | data formatting | bytes 12582912 | tf_op jit(solution)/shard_map/convert_element_type | solution.py:96
  116.5 5.3 %all-to-all-start.1 = ((bf16[128,32,768]{2,1,0:T(8,128)(2,1)}), bf16[128,32,768]{2,1,0:T(8,128)(2,1)}, u32[]{:S(2)}, u32[]{:S(2)}) async-start(bf16[128,32,768]{2,1,0:T(8,128)(2,1)} %bitcast.71), calls=%async_computation.1 | async-start | bytes 12582912 | tf_op jit(solution)/shard_map/all_to_all | solution.py:97
  123.1 1.7 pad_maximum_fusion.3
  125.2 1.3 reduce-window.8
  126.6 2.8 %copy.41 = bf16[192,8,2,512]{3,1,2,0:T(8,128)(2,1)S(1)} copy(bf16[192,8,2,512]{3,2,1,0:T(2,128)(2,1)} %bitcast.75) | data formatting | bytes 6291456
  131.3 2.2 %broadcast_select_fusion.3 = (bf16[768,320]{0,1:T(8,128)(2,1)}, bf16[768,320]{0,1:T(8,128)(2,1)}) fusion(bf16[768,320]{0,1:T(8,128)(2,1)} %collective-permute-done.2, pred[]{:T(512)S(6)} %eq.204, bf16[768,256]{0,1:T(8,128)(2,1)S(1)} %copy.33, bf16[768,64]{0,1:T(8,128)(2,1)S(1)} %copy-done.18), kind=kLoop, calls=%fused_computation.42 | loop fusion | flops 1474560 | bytes 1966081 | tf_op jit(solution)/shard_map/jit(_where)/select_n | solution.py:16
  133.7 1.8 fusion.11
  135.5 2.2 %convolution_convert_fusion.1 = bf16[512,1536]{1,0:T(8,128)(2,1)} fusion(bf16[512,1536]{1,0:T(8,128)(2,1)S(1)} %copy-done, f32[512,1024]{1,0:T(8,128)S(1)} %fusion.11), kind=kOutput, calls=%fused_computation.12 | convolution fusion | flops 807665664 | bytes 5242880 | tf_op jit(solution)/shard_map/dot_general | solution.py:130
  137.7 3.6 %reshape.211 = bf16[512,2,768]{2,1,0:T(2,128)(2,1)S(1)} reshape(bf16[512,1536]{1,0:T(8,128)(2,1)} %convolution_convert_fusion.1) | data formatting | bytes 3145728 | tf_op jit(solution)/shard_map/reshape | solution.py:131
  141.3 2.2 %fusion.68 = (bf16[512,1,768]{2,1,0:T(2,128)(2,1)S(1)}, bf16[512,1,768]{2,1,0:T(2,128)(2,1)S(1)}) fusion(bf16[512,2,768]{2,1,0:T(2,128)(2,1)S(1)} %reshape.211), kind=kLoop, calls=%fused_computation.129 | loop fusion | bytes 3145728 | tf_op jit(solution)/shard_map/slice | solution.py:133
  147.8 2.7 %select_convert_fusion = bf16[512,64,64]{0,2,1:T(8,128)(2,1)} fusion(f32[512,64]{0,1:T(8,128)S(1)} %broadcast_divide_fusion, s32[64,64]{1,0:T(8,128)S(1)} %copy-done.19, s32[512,64]{0,1:T(8,128)S(1)} %get-tuple-element.27), kind=kLoop, calls=%fused_computation.1 | loop fusion | flops 4194304 | bytes 4472832 | tf_op jit(solution)/shard_map/convert_element_type | solution.py:147
  150.5 2.6 %fusion = bf16[512,64,64]{0,2,1:T(8,128)(2,1)} fusion(f32[512,64]{0,1:T(8,128)S(1)} %broadcast_divide_fusion, s32[64,64]{1,0:T(8,128)S(1)} %copy-done.19, s32[512,64]{0,1:T(8,128)S(1)} %get-tuple-element.27), kind=kLoop, calls=%fused_computation.2 | loop fusion | flops 12582912 | bytes 4472832 | tf_op jit(solution)/shard_map/convert_element_type | solution.py:148
  153.1 44.7 %all-to-all-done.1 = bf16[128,32,768]{2,1,0:T(8,128)(2,1)} async-done(((bf16[128,32,768]{2,1,0:T(8,128)(2,1)}), bf16[128,32,768]{2,1,0:T(8,128)(2,1)}, u32[]{:S(2)}, u32[]{:S(2)}) %all-to-all-start.1) | async-done | bytes 6291488 | tf_op jit(solution)/shard_map/all_to_all | solution.py:97
  197.8 7.2 %fusion.71 = f32[512,768]{1,0:T(8,128)S(1)} fusion(bf16[512,4096]{0,1:T(8,128)(2,1)} %bitcast.74, bf16[4096,768]{1,0:T(8,128)(2,1)} %bitcast.32), kind=kOutput, calls=%fused_computation.132 | convolution fusion | flops 3221225472 | bytes 12058624 | tf_op jit(solution)/shard_map/dot_general | solution.py:150
  205.1 5.8 %fusion.70 = f32[512,768]{1,0:T(8,128)S(1)} fusion(bf16[512,4096]{0,1:T(8,128)(2,1)S(1)} %bitcast.73, bf16[4096,768]{1,0:T(8,128)(2,1)} %bitcast.32), kind=kOutput, calls=%fused_computation.131 | convolution fusion | flops 3221225472 | bytes 12058624 | tf_op jit(solution)/shard_map/dot_general | solution.py:150
  211.0 1.7 add_convert_fusion
  (83 shorter events, 13.7 us)
Async XLA Ops:
  0.0 135.5 %copy-start = (bf16[512,1536]{1,0:T(8,128)(2,1)S(1)}, bf16[512,1536]{1,0:T(8,128)(2,1)}, u32[]{:S(2)}) copy-start(bf16[512,1536]{1,0:T(8,128)(2,1)} %param.16) | copy-start | bytes 4718596
  0.0 3.3 %copy-start.7 = (bf16[512,768]{1,0:T(8,128)(2,1)S(1)}, bf16[512,768]{1,0:T(8,128)(2,1)}, u32[]{:S(2)}) copy-start(bf16[512,768]{1,0:T(8,128)(2,1)} %param.11) | copy-start | bytes 2359300
  8.6 11.1 %copy-start.6 = (bf16[1,512,768]{2,1,0:T(8,128)(2,1)S(1)}, bf16[1,512,768]{2,1,0:T(8,128)(2,1)}, u32[]{:S(2)}) copy-start(bf16[1,512,768]{2,1,0:T(8,128)(2,1)} %param.18) | copy-start | bytes 2359300
  8.6 87.0 %all-to-all-start = ((bf16[128,32,768]{2,1,0:T(8,128)(2,1)}), bf16[128,32,768]{2,1,0:T(8,128)(2,1)}, u32[]{:S(2)}, u32[]{:S(2)}) async-start(bf16[128,32,768]{2,1,0:T(8,128)(2,1)} %bitcast.72), calls=%async_computation | async-start | bytes 12582912 | tf_op jit(solution)/shard_map/all_to_all | solution.py:71
  19.6 6.1 %collective-permute-start.4 = (bf16[768,1024]{1,0:T(8,128)(2,1)}, bf16[768,1024]{1,0:T(8,128)(2,1)}, u32[]{:S(2)}, u32[]{:S(2)}) collective-permute-start(bf16[768,1024]{1,0:T(8,128)(2,1)} %bitcast.23), channel_id=1, source_target_pairs={{0,1},{1,0},{2,3},{3,2},{4,5},{5,4},{6,7},{7,6},{8,9},{9,8},{10,11... | collective-permute-start | bytes 4718600 | tf_op jit(solution)/shard_map/ppermute | solution.py:10
  20.0 4.3 %collective-permute-start.3 = (bf16[768,512]{1,0:T(8,128)(2,1)S(1)}, bf16[768,512]{1,0:T(8,128)(2,1)S(1)}, u32[]{:S(2)}, u32[]{:S(2)}) collective-permute-start(bf16[768,512]{1,0:T(8,128)(2,1)S(1)} %bitcast.77), channel_id=1, source_target_pairs={{0,1},{1,0},{2,3},{3,2},{4,5},{5,4},{6,7},{7,6},{8,9},{9,8},{10,11... | collective-permute-start | bytes 2359304 | tf_op jit(solution)/shard_map/ppermute | solution.py:10
  116.5 5.3 %copy-start.8 = (bf16[512,768]{1,0:T(8,128)(2,1)S(1)}, bf16[512,768]{1,0:T(8,128)(2,1)}, u32[]{:S(2)}) copy-start(bf16[512,768]{1,0:T(8,128)(2,1)} %param.11) | copy-start | bytes 2359300
  116.5 81.4 %all-to-all-start.1 = ((bf16[128,32,768]{2,1,0:T(8,128)(2,1)}), bf16[128,32,768]{2,1,0:T(8,128)(2,1)}, u32[]{:S(2)}, u32[]{:S(2)}) async-start(bf16[128,32,768]{2,1,0:T(8,128)(2,1)} %bitcast.71), calls=%async_computation.1 | async-start | bytes 12582912 | tf_op jit(solution)/shard_map/all_to_all | solution.py:97
  121.8 11.8 %collective-permute-start = (bf16[512,768]{1,0:T(8,128)(2,1)S(1)}, bf16[512,768]{1,0:T(8,128)(2,1)S(1)}, u32[]{:S(2)}, u32[]{:S(2)}) collective-permute-start(bf16[512,768]{1,0:T(8,128)(2,1)S(1)} %copy-done.8), channel_id=1, source_target_pairs={{0,1},{1,0},{2,3},{3,2},{4,5},{5,4},{6,7},{7,6},{8,9},{9,8},{10,11... | collective-permute-start | bytes 2359304 | tf_op jit(solution)/shard_map/ppermute | solution.py:10
  124.8 6.5 %collective-permute-start.2 = (bf16[768,320]{0,1:T(8,128)(2,1)}, bf16[768,320]{0,1:T(8,128)(2,1)}, u32[]{:S(2)}, u32[]{:S(2)}) collective-permute-start(bf16[768,320]{0,1:T(8,128)(2,1)} %pad_maximum_fusion.3), channel_id=1, source_target_pairs={{0,1},{1,0},{2,3},{3,2},{4,5},{5,4},{6,7},{7,6},{8,9},{9,8},{10,11... | collective-permute-start | bytes 1474568 | tf_op jit(solution)/shard_map/ppermute | solution.py:10
  126.6 4.0 %copy-start.28 = (s32[4,1]{0,1:T(1,128)S(1)}, s32[4,1]{0,1:T(1,128)}, u32[]{:S(2)}) copy-start(s32[4,1]{0,1:T(1,128)} %reduce-window.8) | copy-start | bytes 52
  126.6 4.1 %copy-start.27 = (s32[1,4]{1,0:T(1,128)S(1)}, s32[1,4]{1,0:T(1,128)}, u32[]{:S(2)}) copy-start(s32[1,4]{1,0:T(1,128)} %param.20) | copy-start | bytes 52
  126.6 4.8 %copy-start.18 = (bf16[768,64]{0,1:T(8,128)(2,1)S(1)}, bf16[768,64]{0,1:T(8,128)(2,1)}, u32[]{:S(2)}) copy-start(bf16[768,64]{0,1:T(8,128)(2,1)} %param.12) | copy-start | bytes 294916
  143.6 3.8 %copy-start.1 = (bf16[512,1,768]{2,1,0:T(2,128)(2,1)}, bf16[512,1,768]{2,1,0:T(2,128)(2,1)S(1)}, u32[]{:S(2)}) copy-start(bf16[512,1,768]{2,1,0:T(2,128)(2,1)S(1)} %get-tuple-element.13) | copy-start | bytes 2359300
  143.6 3.8 %copy-start.3 = (bf16[512,1,768]{2,1,0:T(2,128)(2,1)}, bf16[512,1,768]{2,1,0:T(2,128)(2,1)S(1)}, u32[]{:S(2)}) copy-start(bf16[512,1,768]{2,1,0:T(2,128)(2,1)S(1)} %get-tuple-element.14) | copy-start | bytes 2359300
  143.6 2.9 %copy-start.15 = (bf16[768,320]{0,1:T(8,128)(2,1)S(1)}, bf16[768,320]{0,1:T(8,128)(2,1)}, u32[]{:S(2)}) copy-start(bf16[768,320]{0,1:T(8,128)(2,1)} %get-tuple-element.19) | copy-start | bytes 1474564
  143.6 3.0 %copy-start.16 = (bf16[768,320]{0,1:T(8,128)(2,1)S(1)}, bf16[768,320]{0,1:T(8,128)(2,1)}, u32[]{:S(2)}) copy-start(bf16[768,320]{0,1:T(8,128)(2,1)} %get-tuple-element.20) | copy-start | bytes 1474564
  144.8 66.2 %collective-permute-start.1 = (bf16[512,768]{1,0:T(8,128)(2,1)}, bf16[512,768]{1,0:T(8,128)(2,1)S(1)}, u32[]{:S(2)}, u32[]{:S(2)}) collective-permute-start(bf16[512,768]{1,0:T(8,128)(2,1)} %select_bitcast_fusion.4), channel_id=1, source_target_pairs={{0,1},{1,0},{2,3},{3,2},{4,5},{5,4},{6,7},{7,6},{8,9},{9,8},{10,11... | collective-permute-start | bytes 2359304 | tf_op jit(solution)/shard_map/ppermute | solution.py:10
  197.8 7.2 %copy-start.5 = (bf16[512,64,64]{0,2,1:T(8,128)(2,1)S(1)}, bf16[512,64,64]{0,2,1:T(8,128)(2,1)}, u32[]{:S(2)}) copy-start(bf16[512,64,64]{0,2,1:T(8,128)(2,1)} %select_convert_fusion) | copy-start | bytes 12582916
  205.1 5.9 %copy-start.2 = (bf16[512,1,768]{2,1,0:T(2,128)(2,1)S(1)}, bf16[512,1,768]{2,1,0:T(2,128)(2,1)}, u32[]{:S(2)}) copy-start(bf16[512,1,768]{2,1,0:T(2,128)(2,1)} %copy-done.1) | copy-start | bytes 2359300
  205.1 5.9 %copy-start.4 = (bf16[512,1,768]{2,1,0:T(2,128)(2,1)S(1)}, bf16[512,1,768]{2,1,0:T(2,128)(2,1)}, u32[]{:S(2)}) copy-start(bf16[512,1,768]{2,1,0:T(2,128)(2,1)} %copy-done.3) | copy-start | bytes 2359300
  205.1 5.9 %copy-start.17 = (bf16[256,768]{1,0:T(8,128)(2,1)S(1)}, bf16[256,768]{1,0:T(8,128)(2,1)}, u32[]{:S(2)}) copy-start(bf16[256,768]{1,0:T(8,128)(2,1)} %param.14) | copy-start | bytes 1179652
  205.1 5.9 %copy-start.25 = (s32[512]{0:T(512)S(1)}, s32[512]{0:T(512)}, u32[]{:S(2)}) copy-start(s32[512]{0:T(512)} %select_reduce_fusion) | copy-start | bytes 6148
  205.1 5.9 %copy-start.26 = (s32[256]{0:T(256)S(1)}, s32[256]{0:T(256)}, u32[]{:S(2)}) copy-start(s32[256]{0:T(256)} %and_select_fusion) | copy-start | bytes 3076
  (12 other events, 16.9 us)

commit v6 on v5

--- a/solution.py
+++ b/solution.py
@@ -57,17 +57,17 @@
     pad_rows = -(-part_rows // 16) * 16
     chunk_count = expert_count * blk_count
     row_iota = jnp.arange(chunk_count * pad_rows, dtype=jnp.int32)
-    row_slot = (row_iota // pad_rows) % blk_count * part_rows + row_iota % pad_rows
+    row_slot = row_iota // (expert_count * pad_rows) * part_rows + row_iota % pad_rows
     row_slot = jnp.where(row_iota % pad_rows < part_rows, row_slot, -2)
     rank_rows = jnp.broadcast_to(
-        rank.T[:, None, :], (expert_count, blk_count * pad_rows, tok_rows)
+        rank.T[None, :, None, :], (blk_count, expert_count, pad_rows, tok_rows)
     ).reshape(chunk_count * pad_rows, tok_rows)
     pick = rank_rows == row_slot[:, None]
 
     send_rows = jnp.dot(
         pick.astype(jnp.bfloat16), normed, preferred_element_type=jnp.float32
     ).astype(jnp.bfloat16)
-    both = ("req", "blk")
+    both = ("blk", "req")
     received = lax.all_to_all(
         send_rows.reshape(chunk_count, pad_rows, feat_local),
         both,
@@ -75,12 +75,12 @@
         concat_axis=0,
         tiled=True,
     )
-    rows_in = received.reshape(req_count, blk_count, pad_rows, feat_local)
+    rows_in = received.reshape(blk_count, req_count, pad_rows, feat_local)
 
     weight_gate_up = gather_blk(expert_gate_up[0], 0, stack=True)
-    weight_down = gather_blk(expert_down[0].T, 0, stack=True)
+    weight_down = gather_blk(expert_down[0], 0, stack=True)
     gate_up = jnp.einsum(
-        "gcsd,cdf->gsf",
+        "cgsd,cdf->gsf",
         rows_in,
         weight_gate_up,
         preferred_element_type=jnp.float32,
@@ -88,12 +88,16 @@
     hidden = (jax.nn.silu(gate_up[..., :hidden_width]) * gate_up[..., hidden_width:]).astype(
         jnp.bfloat16
     )
-    expert_out = jnp.einsum(
-        "gsh,cdh->gcsd",
-        hidden,
-        weight_down,
-        preferred_element_type=jnp.float32,
-    ).astype(jnp.bfloat16)
+    hidden_rows = hidden.reshape(req_count * pad_rows, hidden_width)
+    expert_out = jnp.concatenate(
+        [
+            jnp.dot(hidden_rows, weight_down[c], preferred_element_type=jnp.float32).astype(
+                jnp.bfloat16
+            )
+            for c in range(blk_count)
+        ],
+        axis=0,
+    )
     returned = lax.all_to_all(
         expert_out.reshape(req_count * blk_count, pad_rows, feat_local),
         both,
@@ -136,12 +140,11 @@
 
     chosen = jnp.where(has > 0, jax.nn.sigmoid(logits), 0.0)
     gate = chosen / jnp.sum(chosen, axis=1, keepdims=True)
-    rows_per_expert = blk_count * pad_rows
     rank_cols = jnp.broadcast_to(
-        rank[:, :, None], (tok_rows, expert_count, rows_per_expert)
+        rank[:, None, :, None], (tok_rows, blk_count, expert_count, pad_rows)
     ).reshape(tok_rows, chunk_count * pad_rows)
     gate_cols = jnp.broadcast_to(
-        gate[:, :, None], (tok_rows, expert_count, rows_per_expert)
+        gate[:, None, :, None], (tok_rows, blk_count, expert_count, pad_rows)
     ).reshape(tok_rows, chunk_count * pad_rows)
     weights = jnp.where(rank_cols == row_slot[None, :], gate_cols, 0.0)
     weights_hi = weights.astype(jnp.bfloat16)

time: 213 us -> 231 us (1.085)
  the two profiles are of different devices: /device:TPU:2 before, /device:TPU:19 now
where the time goes in v6:
time: 231 us
  waiting for transfers between devices  135 us (58%)
  matrix products  40.2 us (17%)
  other arithmetic  23 us (10%)
  starting transfers between devices  19.6 us (8%)
  local copies, waits for them, and re-layouts  12.4 us (5%)
    all_to_all x1, waiting for transfers between devices, body(): lax.all_to_all(send_rows.reshape(chunk_count, pad_rows, feat_local), both...  78 us
    all_to_all x1, waiting for transfers between devices, body(): lax.all_to_all(expert_out.reshape(req_count * blk_count, pad_rows, feat_l...  53.9 us
    all_to_all x1, starting transfers between devices, body(): lax.all_to_all(send_rows.reshape(chunk_count, pad_rows, feat_local), both...  11 us
    dot_general x1, matrix products, body(): jnp.einsum('cgsd,cdf->gsf', rows_in, weight_gate_up, preferred_element_ty...  9.69 us
    dot_general x1, matrix products, body(): jnp.dot(weights_lo, back, preferred_element_type=jnp.float32)  7.23 us
    all_to_all x1, starting transfers between devices, body(): lax.all_to_all(expert_out.reshape(req_count * blk_count, pad_rows, feat_l...  7 us
    dot_general x1, matrix products, body(): jnp.dot(weights_hi, back, preferred_element_type=jnp.float32)  5.82 us
    dot_general x1, matrix products, body(): jnp.dot(pick.astype(jnp.bfloat16), normed, preferred_element_type=jnp.flo...  5.33 us
  transfers between devices with their start and end apart: 7, of which 3 were waited for; matrix products, arithmetic and copies ran while one was open for 24% of the time, Pallas kernels for 0%

profile of v6, /device:TPU:19, one launch (start us, length us, event | category | flops | bytes accessed | tf_op | source)
XLA Modules:
  0.0 230.6 jit_solution(695787906015591127)
XLA Ops:
  3.5 5.3 %convolution_convert_fusion = bf16[4096,768]{1,0:T(8,128)(2,1)} fusion(pred[4096,512]{1,0:T(32,128)(4,1)S(1)} %bitcast_compare_fusion, bf16[512,768]{1,0:T(8,128)(2,1)S(1)} %copy-done.7), kind=kOutput, calls=%fused_computation.4 | convolution fusion | flops 3224371200 | bytes 9175040 | tf_op jit(solution)/shard_map/dot_general | solution.py:67
  8.8 11.0 %all-to-all-start = ((bf16[128,32,768]{2,1,0:T(8,128)(2,1)}), bf16[128,32,768]{2,1,0:T(8,128)(2,1)}, u32[]{:S(2)}, u32[]{:S(2)}) async-start(bf16[128,32,768]{2,1,0:T(8,128)(2,1)} %bitcast.66), calls=%async_computation | async-start | bytes 12582912 | tf_op jit(solution)/shard_map/all_to_all | solution.py:71
  20.4 3.0 %collective-permute-done.3 = bf16[768,1024]{1,0:T(8,128)(2,1)} collective-permute-done((bf16[768,1024]{1,0:T(8,128)(2,1)S(1)}, bf16[768,1024]{1,0:T(8,128)(2,1)}, u32[]{:S(2)}, u32[]{:S(2)}) %collective-permute-start.3) | collective-permute-done | bytes 1572896 | tf_op jit(solution)/shard_map/ppermute | solution.py:10
  23.4 3.3 %select_bitcast_fusion.1 = (bf16[1,768,1024]{2,1,0:T(8,128)(2,1)}, bf16[1,768,1024]{2,1,0:T(8,128)(2,1)}) fusion(bf16[768,1024]{1,0:T(8,128)(2,1)} %collective-permute-done.3, pred[]{:T(512)S(6)} %eq.203, bf16[1,768,1024]{2,1,0:T(8,128)(2,1)S(1)} %copy-done.6), kind=kLoop, calls=%fused_computation.18 | loop fusion | flops 1572864 | bytes 6291457 | tf_op jit(solution)/shard_map/stack | solution.py:19
  26.7 78.0 %all-to-all-done = bf16[128,32,768]{2,1,0:T(8,128)(2,1)} async-done(((bf16[128,32,768]{2,1,0:T(8,128)(2,1)}), bf16[128,32,768]{2,1,0:T(8,128)(2,1)}, u32[]{:S(2)}, u32[]{:S(2)}) %all-to-all-start) | async-done | bytes 6291488 | tf_op jit(solution)/shard_map/all_to_all | solution.py:71
  104.7 9.7 %convolution_bitcast_fusion = f32[64,32,1024]{2,1,0:T(8,128)S(1)} fusion(bf16[2,64,32,768]{3,2,1,0:T(8,128)(2,1)} %bitcast.15, bf16[1,768,1024]{2,1,0:T(8,128)(2,1)} %get-tuple-element.12, bf16[1,768,1024]{2,1,0:T(8,128)(2,1)} %get-tuple-element.11), kind=kOutput, calls=%fused_computation.10 | convolution fusion | flops 6444023808 | bytes 17825792 | tf_op jit(solution)/shard_map/cgsd,cdf->gsf/dot_general | solution.py:82
  114.4 1.5 fusion.1
  115.9 1.8 convolution_convert_fusion.1
  117.7 2.9 %convolution_convert_fusion.2 = bf16[2048,768]{1,0:T(8,128)(2,1)S(1)} fusion(bf16[2048,512]{1,0:T(8,128)(2,1)S(1)} %bitcast.72, bf16[512,768]{1,0:T(8,128)(2,1)} %collective-permute-done.4, pred[]{:T(512)S(6)} %eq.203, bf16[1,512,768]{2,1,0:T(8,128)(2,1)S(1)} %copy-done.27), kind=kOutput, calls=%fused_computation.9 | convolution fusion | flops 1612578816 | bytes 6815745 | tf_op jit(solution)/shard_map/dot_general | solution.py:94
  120.7 3.0 %pad_maximum_fusion = bf16[4096,768]{1,0:T(8,128)(2,1)} fusion(bf16[2048,768]{1,0:T(8,128)(2,1)S(1)} %convolution_convert_fusion.1, bf16[2048,768]{1,0:T(8,128)(2,1)S(1)} %convolution_convert_fusion.2), kind=kLoop, calls=%fused_computation.5 | loop fusion | flops 12582912 | bytes 12582912 | tf_op jit(solution)/shard_map/concatenate | solution.py:92
  123.7 7.0 %all-to-all-start.1 = ((bf16[128,32,768]{2,1,0:T(8,128)(2,1)}), bf16[128,32,768]{2,1,0:T(8,128)(2,1)}, u32[]{:S(2)}, u32[]{:S(2)}) async-start(bf16[128,32,768]{2,1,0:T(8,128)(2,1)} %bitcast.65), calls=%async_computation.1 | async-start | bytes 12582912 | tf_op jit(solution)/shard_map/all_to_all | solution.py:101
  132.4 1.7 pad_maximum_fusion.4
  135.5 2.8 %copy.30 = bf16[192,8,2,512]{3,1,2,0:T(8,128)(2,1)S(1)} copy(bf16[192,8,2,512]{3,2,1,0:T(2,128)(2,1)} %bitcast.69) | data formatting | bytes 6291456
  140.3 2.2 broadcast_select_fusion.3
  142.6 1.8 fusion.7
  144.5 2.2 convolution_convert_fusion.3
  146.7 3.6 %reshape.192 = bf16[512,2,768]{2,1,0:T(2,128)(2,1)S(1)} reshape(bf16[512,1536]{1,0:T(8,128)(2,1)} %convolution_convert_fusion.3) | data formatting | bytes 3145728 | tf_op jit(solution)/shard_map/reshape | solution.py:135
  150.3 2.2 fusion.67
  156.7 2.5 %select_convert_fusion = bf16[512,2,64,32]{0,3,2,1:T(8,128)(2,1)} fusion(f32[512,64]{0,1:T(8,128)S(1)} %broadcast_divide_fusion, s32[2,64,32]{2,1,0:T(8,128)S(1)} %copy-done.13, s32[512,64]{0,1:T(8,128)S(1)} %get-tuple-element.25), kind=kLoop, calls=%fused_computation.1 | loop fusion | flops 4194304 | bytes 4472832 | tf_op jit(solution)/shard_map/convert_element_type | solution.py:150
  159.2 2.5 %fusion = bf16[512,2,64,32]{0,3,2,1:T(8,128)(2,1)} fusion(f32[512,64]{0,1:T(8,128)S(1)} %broadcast_divide_fusion, s32[2,64,32]{2,1,0:T(8,128)S(1)} %copy-done.13, s32[512,64]{0,1:T(8,128)S(1)} %get-tuple-element.25), kind=kLoop, calls=%fused_computation.2 | loop fusion | flops 12582912 | bytes 4472832 | tf_op jit(solution)/shard_map/convert_element_type | solution.py:151
  161.7 53.9 %all-to-all-done.1 = bf16[128,32,768]{2,1,0:T(8,128)(2,1)} async-done(((bf16[128,32,768]{2,1,0:T(8,128)(2,1)}), bf16[128,32,768]{2,1,0:T(8,128)(2,1)}, u32[]{:S(2)}, u32[]{:S(2)}) %all-to-all-start.1) | async-done | bytes 6291488 | tf_op jit(solution)/shard_map/all_to_all | solution.py:101
  215.6 7.2 %fusion.70 = f32[512,768]{1,0:T(8,128)S(1)} fusion(bf16[512,4096]{0,1:T(8,128)(2,1)} %bitcast.68, bf16[4096,768]{1,0:T(8,128)(2,1)} %bitcast.25), kind=kOutput, calls=%fused_computation.126 | convolution fusion | flops 3221225472 | bytes 12058624 | tf_op jit(solution)/shard_map/dot_general | solution.py:153
  222.9 5.8 %fusion.69 = f32[512,768]{1,0:T(8,128)S(1)} fusion(bf16[512,4096]{0,1:T(8,128)(2,1)S(1)} %bitcast.67, bf16[4096,768]{1,0:T(8,128)(2,1)} %bitcast.25), kind=kOutput, calls=%fused_computation.125 | convolution fusion | flops 3221225472 | bytes 12058624 | tf_op jit(solution)/shard_map/dot_general | solution.py:153
  228.8 1.7 add_convert_fusion
  (80 shorter events, 13.3 us)
Async XLA Ops:
  0.0 144.5 %copy-start = (bf16[512,1536]{1,0:T(8,128)(2,1)S(1)}, bf16[512,1536]{1,0:T(8,128)(2,1)}, u32[]{:S(2)}) copy-start(bf16[512,1536]{1,0:T(8,128)(2,1)} %param.16) | copy-start | bytes 4718596
  0.0 3.4 %copy-start.7 = (bf16[512,768]{1,0:T(8,128)(2,1)S(1)}, bf16[512,768]{1,0:T(8,128)(2,1)}, u32[]{:S(2)}) copy-start(bf16[512,768]{1,0:T(8,128)(2,1)} %param.11) | copy-start | bytes 2359300
  8.8 11.0 %copy-start.6 = (bf16[1,768,1024]{2,1,0:T(8,128)(2,1)S(1)}, bf16[1,768,1024]{2,1,0:T(8,128)(2,1)}, u32[]{:S(2)}) copy-start(bf16[1,768,1024]{2,1,0:T(8,128)(2,1)} %param.17) | copy-start | bytes 4718596
  8.8 95.9 %all-to-all-start = ((bf16[128,32,768]{2,1,0:T(8,128)(2,1)}), bf16[128,32,768]{2,1,0:T(8,128)(2,1)}, u32[]{:S(2)}, u32[]{:S(2)}) async-start(bf16[128,32,768]{2,1,0:T(8,128)(2,1)} %bitcast.66), calls=%async_computation | async-start | bytes 12582912 | tf_op jit(solution)/shard_map/all_to_all | solution.py:71
  19.8 3.6 %collective-permute-start.3 = (bf16[768,1024]{1,0:T(8,128)(2,1)S(1)}, bf16[768,1024]{1,0:T(8,128)(2,1)}, u32[]{:S(2)}, u32[]{:S(2)}) collective-permute-start(bf16[768,1024]{1,0:T(8,128)(2,1)S(1)} %bitcast.73), channel_id=1, source_target_pairs={{0,1},{1,0},{2,3},{3,2},{4,5},{5,4},{6,7},{7,6},{8,9},{9,8},{10,11... | collective-permute-start | bytes 4718600 | tf_op jit(solution)/shard_map/ppermute | solution.py:10
  20.3 95.6 %collective-permute-start.4 = (bf16[512,768]{1,0:T(8,128)(2,1)}, bf16[512,768]{1,0:T(8,128)(2,1)}, u32[]{:S(2)}, u32[]{:S(2)}) collective-permute-start(bf16[512,768]{1,0:T(8,128)(2,1)} %bitcast.94), channel_id=1, source_target_pairs={{0,1},{1,0},{2,3},{3,2},{4,5},{5,4},{6,7},{7,6},{8,9},{9,8},{10,11... | collective-permute-start | bytes 2359304 | tf_op jit(solution)/shard_map/ppermute | solution.py:10
  123.7 7.0 %copy-start.8 = (bf16[512,768]{1,0:T(8,128)(2,1)S(1)}, bf16[512,768]{1,0:T(8,128)(2,1)}, u32[]{:S(2)}) copy-start(bf16[512,768]{1,0:T(8,128)(2,1)} %param.11) | copy-start | bytes 2359300
  123.7 91.9 %all-to-all-start.1 = ((bf16[128,32,768]{2,1,0:T(8,128)(2,1)}), bf16[128,32,768]{2,1,0:T(8,128)(2,1)}, u32[]{:S(2)}, u32[]{:S(2)}) async-start(bf16[128,32,768]{2,1,0:T(8,128)(2,1)} %bitcast.65), calls=%async_computation.1 | async-start | bytes 12582912 | tf_op jit(solution)/shard_map/all_to_all | solution.py:101
  130.7 11.8 %collective-permute-start = (bf16[512,768]{1,0:T(8,128)(2,1)S(1)}, bf16[512,768]{1,0:T(8,128)(2,1)S(1)}, u32[]{:S(2)}, u32[]{:S(2)}) collective-permute-start(bf16[512,768]{1,0:T(8,128)(2,1)S(1)} %copy-done.8), channel_id=1, source_target_pairs={{0,1},{1,0},{2,3},{3,2},{4,5},{5,4},{6,7},{7,6},{8,9},{9,8},{10,11... | collective-permute-start | bytes 2359304 | tf_op jit(solution)/shard_map/ppermute | solution.py:10
  134.1 6.2 %collective-permute-start.2 = (bf16[768,320]{0,1:T(8,128)(2,1)}, bf16[768,320]{0,1:T(8,128)(2,1)}, u32[]{:S(2)}, u32[]{:S(2)}) collective-permute-start(bf16[768,320]{0,1:T(8,128)(2,1)} %pad_maximum_fusion.4), channel_id=1, source_target_pairs={{0,1},{1,0},{2,3},{3,2},{4,5},{5,4},{6,7},{7,6},{8,9},{9,8},{10,11... | collective-permute-start | bytes 1474568 | tf_op jit(solution)/shard_map/ppermute | solution.py:10
  135.5 3.3 %copy-start.26 = (s32[4,1]{0,1:T(1,128)S(1)}, s32[4,1]{0,1:T(1,128)}, u32[]{:S(2)}) copy-start(s32[4,1]{0,1:T(1,128)} %reduce-window.8) | copy-start | bytes 52
  135.5 3.4 %copy-start.25 = (s32[1,4]{1,0:T(1,128)S(1)}, s32[1,4]{1,0:T(1,128)}, u32[]{:S(2)}) copy-start(s32[1,4]{1,0:T(1,128)} %param.20) | copy-start | bytes 52
  135.5 4.8 %copy-start.17 = (bf16[768,64]{0,1:T(8,128)(2,1)S(1)}, bf16[768,64]{0,1:T(8,128)(2,1)}, u32[]{:S(2)}) copy-start(bf16[768,64]{0,1:T(8,128)(2,1)} %param.12) | copy-start | bytes 294916
  152.6 3.8 %copy-start.1 = (bf16[512,1,768]{2,1,0:T(2,128)(2,1)}, bf16[512,1,768]{2,1,0:T(2,128)(2,1)S(1)}, u32[]{:S(2)}) copy-start(bf16[512,1,768]{2,1,0:T(2,128)(2,1)S(1)} %get-tuple-element.13) | copy-start | bytes 2359300
  152.6 3.8 %copy-start.3 = (bf16[512,1,768]{2,1,0:T(2,128)(2,1)}, bf16[512,1,768]{2,1,0:T(2,128)(2,1)S(1)}, u32[]{:S(2)}) copy-start(bf16[512,1,768]{2,1,0:T(2,128)(2,1)S(1)} %get-tuple-element.14) | copy-start | bytes 2359300
  152.6 2.9 %copy-start.14 = (bf16[768,320]{0,1:T(8,128)(2,1)S(1)}, bf16[768,320]{0,1:T(8,128)(2,1)}, u32[]{:S(2)}) copy-start(bf16[768,320]{0,1:T(8,128)(2,1)} %get-tuple-element.17) | copy-start | bytes 1474564
  152.6 3.0 %copy-start.15 = (bf16[768,320]{0,1:T(8,128)(2,1)S(1)}, bf16[768,320]{0,1:T(8,128)(2,1)}, u32[]{:S(2)}) copy-start(bf16[768,320]{0,1:T(8,128)(2,1)} %get-tuple-element.18) | copy-start | bytes 1474564
  153.8 75.0 %collective-permute-start.1 = (bf16[512,768]{1,0:T(8,128)(2,1)}, bf16[512,768]{1,0:T(8,128)(2,1)S(1)}, u32[]{:S(2)}, u32[]{:S(2)}) collective-permute-start(bf16[512,768]{1,0:T(8,128)(2,1)} %select_bitcast_fusion.2), channel_id=1, source_target_pairs={{0,1},{1,0},{2,3},{3,2},{4,5},{5,4},{6,7},{7,6},{8,9},{9,8},{10,11... | collective-permute-start | bytes 2359304 | tf_op jit(solution)/shard_map/ppermute | solution.py:10
  215.6 7.2 %copy-start.5 = (bf16[512,2,64,32]{0,3,2,1:T(8,128)(2,1)S(1)}, bf16[512,2,64,32]{0,3,2,1:T(8,128)(2,1)}, u32[]{:S(2)}) copy-start(bf16[512,2,64,32]{0,3,2,1:T(8,128)(2,1)} %select_convert_fusion) | copy-start | bytes 12582916
  222.9 5.9 %copy-start.2 = (bf16[512,1,768]{2,1,0:T(2,128)(2,1)S(1)}, bf16[512,1,768]{2,1,0:T(2,128)(2,1)}, u32[]{:S(2)}) copy-start(bf16[512,1,768]{2,1,0:T(2,128)(2,1)} %copy-done.1) | copy-start | bytes 2359300
  222.9 5.9 %copy-start.4 = (bf16[512,1,768]{2,1,0:T(2,128)(2,1)S(1)}, bf16[512,1,768]{2,1,0:T(2,128)(2,1)}, u32[]{:S(2)}) copy-start(bf16[512,1,768]{2,1,0:T(2,128)(2,1)} %copy-done.3) | copy-start | bytes 2359300
  222.9 5.9 %copy-start.16 = (bf16[256,768]{1,0:T(8,128)(2,1)S(1)}, bf16[256,768]{1,0:T(8,128)(2,1)}, u32[]{:S(2)}) copy-start(bf16[256,768]{1,0:T(8,128)(2,1)} %param.14) | copy-start | bytes 1179652
  222.9 5.9 %copy-start.23 = (s32[512]{0:T(512)S(1)}, s32[512]{0:T(512)}, u32[]{:S(2)}) copy-start(s32[512]{0:T(512)} %select_reduce_fusion) | copy-start | bytes 6148
  222.9 5.9 %copy-start.24 = (s32[256]{0:T(256)S(1)}, s32[256]{0:T(256)}, u32[]{:S(2)}) copy-start(s32[256]{0:T(256)} %and_select_fusion) | copy-start | bytes 3076
  (11 other events, 20.3 us)

commit v7 on v5

--- a/solution.py
+++ b/solution.py
@@ -78,7 +78,6 @@
     rows_in = received.reshape(req_count, blk_count, pad_rows, feat_local)
 
     weight_gate_up = gather_blk(expert_gate_up[0], 0, stack=True)
-    weight_down = gather_blk(expert_down[0].T, 0, stack=True)
     gate_up = jnp.einsum(
         "gcsd,cdf->gsf",
         rows_in,
@@ -88,12 +87,17 @@
     hidden = (jax.nn.silu(gate_up[..., :hidden_width]) * gate_up[..., hidden_width:]).astype(
         jnp.bfloat16
     )
-    expert_out = jnp.einsum(
-        "gsh,cdh->gcsd",
-        hidden,
-        weight_down,
-        preferred_element_type=jnp.float32,
-    ).astype(jnp.bfloat16)
+    hidden_rows = hidden.reshape(req_count * pad_rows, hidden_width)
+    weight_down = gather_blk(expert_down[0], 0, stack=True)
+    expert_out = jnp.stack(
+        [
+            jnp.dot(hidden_rows, weight_down[c], preferred_element_type=jnp.float32)
+            .astype(jnp.bfloat16)
+            .reshape(req_count, pad_rows, feat_local)
+            for c in range(blk_count)
+        ],
+        axis=1,
+    )
     returned = lax.all_to_all(
         expert_out.reshape(req_count * blk_count, pad_rows, feat_local),
         both,

time: 213 us -> 212 us (level)
  local copies, waits for them, and re-layouts: 19.3 us -> 12.6 us
    convert_element_type x1 -> x0, local copies, waits for them, and re-layouts: 6.18 us -> none  [body(): expert_out = jnp.einsum('gsh,cdh->gcsd', hidden, weight_down, preferred_e...]
    another operation x1 -> x2, other arithmetic: 1.34 us -> 4.63 us  [the longest x1 3.22 us: body(): jnp.stack([jnp.dot(hidden_rows, weight_down[c], preferred_element_type=jn...]
    all_to_all x1, waiting for transfers between devices: 66.7 us -> 69.2 us  [body(): lax.all_to_all(send_rows.reshape(chunk_count, pad_rows, feat_local), both...]
    another operation x2 -> x1, other arithmetic: 4.5 us -> 3.26 us  [gather_blk(): return jnp.stack([first, second], axis=axis)]
    dot_general x1 -> x2, matrix products: 3.88 us -> 4.79 us  [body(): jnp.dot(hidden_rows, weight_down[c], preferred_element_type=jnp.float32)]
    unnamed x60 -> x57, local copies, waits for them, and re-layouts: 5.1 us -> 4.63 us
  transfers between devices with their start and end apart: 7 -> 7, of which waited for: 3 -> 3; matrix products, arithmetic and copies ran while one was open for 22% -> 27% of each run, Pallas kernels for 0% -> 0%
where the time goes in v7:
time: 212 us; the launch traced here: 211 us
  waiting for transfers between devices  117 us (55%)
  matrix products  40.2 us (19%)
  other arithmetic  23.4 us (11%)
  starting transfers between devices  17.7 us (8%)
  local copies, waits for them, and re-layouts  12.6 us (6%)
    all_to_all x1, waiting for transfers between devices, body(): lax.all_to_all(send_rows.reshape(chunk_count, pad_rows, feat_local), both...  69.2 us
    all_to_all x1, waiting for transfers between devices, body(): lax.all_to_all(expert_out.reshape(req_count * blk_count, pad_rows, feat_l...  44.6 us
    all_to_all x1, starting transfers between devices, body(): lax.all_to_all(send_rows.reshape(chunk_count, pad_rows, feat_local), both...  10.9 us
    dot_general x1, matrix products, body(): jnp.einsum('gcsd,cdf->gsf', rows_in, weight_gate_up, preferred_element_ty...  9.69 us
    dot_general x1, matrix products, body(): jnp.dot(weights_lo, back, preferred_element_type=jnp.float32)  7.23 us
    dot_general x1, matrix products, body(): jnp.dot(weights_hi, back, preferred_element_type=jnp.float32)  5.82 us
    dot_general x1, matrix products, body(): jnp.dot(pick.astype(jnp.bfloat16), normed, preferred_element_type=jnp.flo...  5.33 us
    all_to_all x1, starting transfers between devices, body(): lax.all_to_all(expert_out.reshape(req_count * blk_count, pad_rows, feat_l...  5.27 us
  transfers between devices with their start and end apart: 7, of which 3 were waited for; matrix products, arithmetic and copies ran while one was open for 27% of the time, Pallas kernels for 0%

profile of v7, /device:TPU:2, one launch (start us, length us, event | category | flops | bytes accessed | tf_op | source)
XLA Modules:
  0.0 211.2 jit_solution(5833681599988332770)
XLA Ops:
  3.3 5.3 %convolution_convert_fusion = bf16[4096,768]{1,0:T(8,128)(2,1)} fusion(pred[4096,512]{1,0:T(32,128)(4,1)S(1)} %bitcast_compare_fusion, bf16[512,768]{1,0:T(8,128)(2,1)S(1)} %copy-done.7), kind=kOutput, calls=%fused_computation.4 | convolution fusion | flops 3224371200 | bytes 9175040 | tf_op jit(solution)/shard_map/dot_general | solution.py:67
  8.6 10.9 %all-to-all-start = ((bf16[128,32,768]{2,1,0:T(8,128)(2,1)}), bf16[128,32,768]{2,1,0:T(8,128)(2,1)}, u32[]{:S(2)}, u32[]{:S(2)}) async-start(bf16[128,32,768]{2,1,0:T(8,128)(2,1)} %bitcast.71), calls=%async_computation | async-start | bytes 12582912 | tf_op jit(solution)/shard_map/all_to_all | solution.py:71
  20.2 3.0 %collective-permute-done.3 = bf16[768,1024]{1,0:T(8,128)(2,1)} collective-permute-done((bf16[768,1024]{1,0:T(8,128)(2,1)S(1)}, bf16[768,1024]{1,0:T(8,128)(2,1)}, u32[]{:S(2)}, u32[]{:S(2)}) %collective-permute-start.3) | collective-permute-done | bytes 1572896 | tf_op jit(solution)/shard_map/ppermute | solution.py:10
  23.2 3.3 %select_bitcast_fusion.1 = (bf16[1,768,1024]{2,1,0:T(8,128)(2,1)}, bf16[1,768,1024]{2,1,0:T(8,128)(2,1)}) fusion(bf16[768,1024]{1,0:T(8,128)(2,1)} %collective-permute-done.3, pred[]{:T(512)S(6)} %eq.204, bf16[1,768,1024]{2,1,0:T(8,128)(2,1)S(1)} %copy-done.6), kind=kLoop, calls=%fused_computation.18 | loop fusion | flops 1572864 | bytes 6291457 | tf_op jit(solution)/shard_map/stack | solution.py:19
  26.5 69.2 %all-to-all-done = bf16[128,32,768]{2,1,0:T(8,128)(2,1)} async-done(((bf16[128,32,768]{2,1,0:T(8,128)(2,1)}), bf16[128,32,768]{2,1,0:T(8,128)(2,1)}, u32[]{:S(2)}, u32[]{:S(2)}) %all-to-all-start) | async-done | bytes 6291488 | tf_op jit(solution)/shard_map/all_to_all | solution.py:71
  95.6 9.7 %convolution_bitcast_fusion = f32[64,32,1024]{2,1,0:T(8,128)S(1)} fusion(bf16[64,2,32,768]{3,2,1,0:T(8,128)(2,1)} %bitcast.15, bf16[1,768,1024]{2,1,0:T(8,128)(2,1)} %get-tuple-element.12, bf16[1,768,1024]{2,1,0:T(8,128)(2,1)} %get-tuple-element.11), kind=kOutput, calls=%fused_computation.10 | convolution fusion | flops 6444023808 | bytes 17825792 | tf_op jit(solution)/shard_map/gcsd,cdf->gsf/dot_general | solution.py:81
  105.4 1.5 fusion.1
  106.9 3.0 %convolution_convert_fusion.1 = bf16[2048,768]{1,0:T(8,128)(2,1)S(1)} fusion(bf16[2048,512]{1,0:T(8,128)(2,1)S(1)} %bitcast.78, bf16[512,768]{1,0:T(8,128)(2,1)} %collective-permute-done.4, pred[]{:T(512)S(6)} %eq.204, bf16[1,512,768]{2,1,0:T(8,128)(2,1)S(1)} %copy-done.27), kind=kOutput, calls=%fused_computation.8 | convolution fusion | flops 1612578816 | bytes 6815745 | tf_op jit(solution)/shard_map/dot_general | solution.py:94
  109.8 1.8 convolution_convert_fusion.2
  111.7 3.2 %pad_maximum_fusion = bf16[64,2,32,768]{3,2,1,0:T(8,128)(2,1)} fusion(bf16[64,1,32,768]{3,2,1,0:T(8,128)(2,1)S(1)} %bitcast.76, bf16[64,1,32,768]{3,2,1,0:T(8,128)(2,1)S(1)} %bitcast.77), kind=kLoop, calls=%fused_computation.5 | loop fusion | flops 3145728 | bytes 12582912 | tf_op jit(solution)/shard_map/stack | solution.py:92
  114.9 5.3 %all-to-all-start.1 = ((bf16[128,32,768]{2,1,0:T(8,128)(2,1)}), bf16[128,32,768]{2,1,0:T(8,128)(2,1)}, u32[]{:S(2)}, u32[]{:S(2)}) async-start(bf16[128,32,768]{2,1,0:T(8,128)(2,1)} %bitcast.70), calls=%async_computation.1 | async-start | bytes 12582912 | tf_op jit(solution)/shard_map/all_to_all | solution.py:101
  121.7 1.7 pad_maximum_fusion.4
  125.3 2.8 %copy.35 = bf16[192,8,2,512]{3,1,2,0:T(8,128)(2,1)S(1)} copy(bf16[192,8,2,512]{3,2,1,0:T(2,128)(2,1)} %bitcast.74) | data formatting | bytes 6291456
  130.0 2.2 %broadcast_select_fusion.3 = (bf16[768,320]{0,1:T(8,128)(2,1)}, bf16[768,320]{0,1:T(8,128)(2,1)}) fusion(bf16[768,320]{0,1:T(8,128)(2,1)} %collective-permute-done.2, pred[]{:T(512)S(6)} %eq.204, bf16[768,256]{0,1:T(8,128)(2,1)S(1)} %copy.29, bf16[768,64]{0,1:T(8,128)(2,1)S(1)} %copy-done.16), kind=kLoop, calls=%fused_computation.41 | loop fusion | flops 1474560 | bytes 1966081 | tf_op jit(solution)/shard_map/jit(_where)/select_n | solution.py:16
  132.3 1.8 fusion.7
  134.2 2.2 %convolution_convert_fusion.3 = bf16[512,1536]{1,0:T(8,128)(2,1)} fusion(bf16[512,1536]{1,0:T(8,128)(2,1)S(1)} %copy-done, f32[512,1024]{1,0:T(8,128)S(1)} %fusion.7), kind=kOutput, calls=%fused_computation.14 | convolution fusion | flops 807665664 | bytes 5242880 | tf_op jit(solution)/shard_map/dot_general | solution.py:134
  136.4 3.6 %reshape.214 = bf16[512,2,768]{2,1,0:T(2,128)(2,1)S(1)} reshape(bf16[512,1536]{1,0:T(8,128)(2,1)} %convolution_convert_fusion.3) | data formatting | bytes 3145728 | tf_op jit(solution)/shard_map/reshape | solution.py:135
  140.0 2.2 %fusion.69 = (bf16[512,1,768]{2,1,0:T(2,128)(2,1)S(1)}, bf16[512,1,768]{2,1,0:T(2,128)(2,1)S(1)}) fusion(bf16[512,2,768]{2,1,0:T(2,128)(2,1)S(1)} %reshape.214), kind=kLoop, calls=%fused_computation.129 | loop fusion | bytes 3145728 | tf_op jit(solution)/shard_map/slice | solution.py:137
  146.4 2.7 %select_convert_fusion = bf16[512,64,64]{0,2,1:T(8,128)(2,1)} fusion(f32[512,64]{0,1:T(8,128)S(1)} %broadcast_divide_fusion, s32[64,64]{1,0:T(8,128)S(1)} %copy-done.17, s32[512,64]{0,1:T(8,128)S(1)} %get-tuple-element.25), kind=kLoop, calls=%fused_computation.1 | loop fusion | flops 4194304 | bytes 4472832 | tf_op jit(solution)/shard_map/convert_element_type | solution.py:151
  149.0 2.6 %fusion = bf16[512,64,64]{0,2,1:T(8,128)(2,1)} fusion(f32[512,64]{0,1:T(8,128)S(1)} %broadcast_divide_fusion, s32[64,64]{1,0:T(8,128)S(1)} %copy-done.17, s32[512,64]{0,1:T(8,128)S(1)} %get-tuple-element.25), kind=kLoop, calls=%fused_computation.2 | loop fusion | flops 12582912 | bytes 4472832 | tf_op jit(solution)/shard_map/convert_element_type | solution.py:152
  151.7 44.6 %all-to-all-done.1 = bf16[128,32,768]{2,1,0:T(8,128)(2,1)} async-done(((bf16[128,32,768]{2,1,0:T(8,128)(2,1)}), bf16[128,32,768]{2,1,0:T(8,128)(2,1)}, u32[]{:S(2)}, u32[]{:S(2)}) %all-to-all-start.1) | async-done | bytes 6291488 | tf_op jit(solution)/shard_map/all_to_all | solution.py:101
  196.3 7.2 %fusion.72 = f32[512,768]{1,0:T(8,128)S(1)} fusion(bf16[512,4096]{0,1:T(8,128)(2,1)} %bitcast.73, bf16[4096,768]{1,0:T(8,128)(2,1)} %bitcast.29), kind=kOutput, calls=%fused_computation.132 | convolution fusion | flops 3221225472 | bytes 12058624 | tf_op jit(solution)/shard_map/dot_general | solution.py:154
  203.6 5.8 %fusion.71 = f32[512,768]{1,0:T(8,128)S(1)} fusion(bf16[512,4096]{0,1:T(8,128)(2,1)S(1)} %bitcast.72, bf16[4096,768]{1,0:T(8,128)(2,1)} %bitcast.29), kind=kOutput, calls=%fused_computation.131 | convolution fusion | flops 3221225472 | bytes 12058624 | tf_op jit(solution)/shard_map/dot_general | solution.py:154
  209.5 1.7 add_convert_fusion
  (80 shorter events, 13.3 us)
Async XLA Ops:
  0.0 134.2 %copy-start = (bf16[512,1536]{1,0:T(8,128)(2,1)S(1)}, bf16[512,1536]{1,0:T(8,128)(2,1)}, u32[]{:S(2)}) copy-start(bf16[512,1536]{1,0:T(8,128)(2,1)} %param.16) | copy-start | bytes 4718596
  0.0 3.3 %copy-start.7 = (bf16[512,768]{1,0:T(8,128)(2,1)S(1)}, bf16[512,768]{1,0:T(8,128)(2,1)}, u32[]{:S(2)}) copy-start(bf16[512,768]{1,0:T(8,128)(2,1)} %param.11) | copy-start | bytes 2359300
  8.6 10.9 %copy-start.6 = (bf16[1,768,1024]{2,1,0:T(8,128)(2,1)S(1)}, bf16[1,768,1024]{2,1,0:T(8,128)(2,1)}, u32[]{:S(2)}) copy-start(bf16[1,768,1024]{2,1,0:T(8,128)(2,1)} %param.17) | copy-start | bytes 4718596
  8.6 87.0 %all-to-all-start = ((bf16[128,32,768]{2,1,0:T(8,128)(2,1)}), bf16[128,32,768]{2,1,0:T(8,128)(2,1)}, u32[]{:S(2)}, u32[]{:S(2)}) async-start(bf16[128,32,768]{2,1,0:T(8,128)(2,1)} %bitcast.71), calls=%async_computation | async-start | bytes 12582912 | tf_op jit(solution)/shard_map/all_to_all | solution.py:71
  19.6 3.6 %collective-permute-start.3 = (bf16[768,1024]{1,0:T(8,128)(2,1)S(1)}, bf16[768,1024]{1,0:T(8,128)(2,1)}, u32[]{:S(2)}, u32[]{:S(2)}) collective-permute-start(bf16[768,1024]{1,0:T(8,128)(2,1)S(1)} %bitcast.80), channel_id=1, source_target_pairs={{0,1},{1,0},{2,3},{3,2},{4,5},{5,4},{6,7},{7,6},{8,9},{9,8},{10,11... | collective-permute-start | bytes 4718600 | tf_op jit(solution)/shard_map/ppermute | solution.py:10
  19.8 87.1 %collective-permute-start.4 = (bf16[512,768]{1,0:T(8,128)(2,1)}, bf16[512,768]{1,0:T(8,128)(2,1)}, u32[]{:S(2)}, u32[]{:S(2)}) collective-permute-start(bf16[512,768]{1,0:T(8,128)(2,1)} %bitcast.101), channel_id=1, source_target_pairs={{0,1},{1,0},{2,3},{3,2},{4,5},{5,4},{6,7},{7,6},{8,9},{9,8},{10,11... | collective-permute-start | bytes 2359304 | tf_op jit(solution)/shard_map/ppermute | solution.py:10
  114.9 5.3 %copy-start.8 = (bf16[512,768]{1,0:T(8,128)(2,1)S(1)}, bf16[512,768]{1,0:T(8,128)(2,1)}, u32[]{:S(2)}) copy-start(bf16[512,768]{1,0:T(8,128)(2,1)} %param.11) | copy-start | bytes 2359300
  114.9 81.4 %all-to-all-start.1 = ((bf16[128,32,768]{2,1,0:T(8,128)(2,1)}), bf16[128,32,768]{2,1,0:T(8,128)(2,1)}, u32[]{:S(2)}, u32[]{:S(2)}) async-start(bf16[128,32,768]{2,1,0:T(8,128)(2,1)} %bitcast.70), calls=%async_computation.1 | async-start | bytes 12582912 | tf_op jit(solution)/shard_map/all_to_all | solution.py:101
  120.2 12.0 %collective-permute-start = (bf16[512,768]{1,0:T(8,128)(2,1)S(1)}, bf16[512,768]{1,0:T(8,128)(2,1)S(1)}, u32[]{:S(2)}, u32[]{:S(2)}) collective-permute-start(bf16[512,768]{1,0:T(8,128)(2,1)S(1)} %copy-done.8), channel_id=1, source_target_pairs={{0,1},{1,0},{2,3},{3,2},{4,5},{5,4},{6,7},{7,6},{8,9},{9,8},{10,11... | collective-permute-start | bytes 2359304 | tf_op jit(solution)/shard_map/ppermute | solution.py:10
  123.5 6.6 %collective-permute-start.2 = (bf16[768,320]{0,1:T(8,128)(2,1)}, bf16[768,320]{0,1:T(8,128)(2,1)}, u32[]{:S(2)}, u32[]{:S(2)}) collective-permute-start(bf16[768,320]{0,1:T(8,128)(2,1)} %pad_maximum_fusion.4), channel_id=1, source_target_pairs={{0,1},{1,0},{2,3},{3,2},{4,5},{5,4},{6,7},{7,6},{8,9},{9,8},{10,11... | collective-permute-start | bytes 1474568 | tf_op jit(solution)/shard_map/ppermute | solution.py:10
  125.3 4.0 %copy-start.26 = (s32[4,1]{0,1:T(1,128)S(1)}, s32[4,1]{0,1:T(1,128)}, u32[]{:S(2)}) copy-start(s32[4,1]{0,1:T(1,128)} %reduce-window.8) | copy-start | bytes 52
  125.3 4.1 %copy-start.25 = (s32[1,4]{1,0:T(1,128)S(1)}, s32[1,4]{1,0:T(1,128)}, u32[]{:S(2)}) copy-start(s32[1,4]{1,0:T(1,128)} %param.20) | copy-start | bytes 52
  125.3 4.8 %copy-start.16 = (bf16[768,64]{0,1:T(8,128)(2,1)S(1)}, bf16[768,64]{0,1:T(8,128)(2,1)}, u32[]{:S(2)}) copy-start(bf16[768,64]{0,1:T(8,128)(2,1)} %param.12) | copy-start | bytes 294916
  142.3 3.8 %copy-start.1 = (bf16[512,1,768]{2,1,0:T(2,128)(2,1)}, bf16[512,1,768]{2,1,0:T(2,128)(2,1)S(1)}, u32[]{:S(2)}) copy-start(bf16[512,1,768]{2,1,0:T(2,128)(2,1)S(1)} %get-tuple-element.13) | copy-start | bytes 2359300
  142.3 3.8 %copy-start.3 = (bf16[512,1,768]{2,1,0:T(2,128)(2,1)}, bf16[512,1,768]{2,1,0:T(2,128)(2,1)S(1)}, u32[]{:S(2)}) copy-start(bf16[512,1,768]{2,1,0:T(2,128)(2,1)S(1)} %get-tuple-element.14) | copy-start | bytes 2359300
  142.3 2.9 %copy-start.13 = (bf16[768,320]{0,1:T(8,128)(2,1)S(1)}, bf16[768,320]{0,1:T(8,128)(2,1)}, u32[]{:S(2)}) copy-start(bf16[768,320]{0,1:T(8,128)(2,1)} %get-tuple-element.17) | copy-start | bytes 1474564
  142.3 3.0 %copy-start.14 = (bf16[768,320]{0,1:T(8,128)(2,1)S(1)}, bf16[768,320]{0,1:T(8,128)(2,1)}, u32[]{:S(2)}) copy-start(bf16[768,320]{0,1:T(8,128)(2,1)} %get-tuple-element.18) | copy-start | bytes 1474564
  143.5 65.9 %collective-permute-start.1 = (bf16[512,768]{1,0:T(8,128)(2,1)}, bf16[512,768]{1,0:T(8,128)(2,1)S(1)}, u32[]{:S(2)}, u32[]{:S(2)}) collective-permute-start(bf16[512,768]{1,0:T(8,128)(2,1)} %select_bitcast_fusion.2), channel_id=1, source_target_pairs={{0,1},{1,0},{2,3},{3,2},{4,5},{5,4},{6,7},{7,6},{8,9},{9,8},{10,11... | collective-permute-start | bytes 2359304 | tf_op jit(solution)/shard_map/ppermute | solution.py:10
  196.3 7.2 %copy-start.5 = (bf16[512,64,64]{0,2,1:T(8,128)(2,1)S(1)}, bf16[512,64,64]{0,2,1:T(8,128)(2,1)}, u32[]{:S(2)}) copy-start(bf16[512,64,64]{0,2,1:T(8,128)(2,1)} %select_convert_fusion) | copy-start | bytes 12582916
  203.5 5.9 %copy-start.2 = (bf16[512,1,768]{2,1,0:T(2,128)(2,1)S(1)}, bf16[512,1,768]{2,1,0:T(2,128)(2,1)}, u32[]{:S(2)}) copy-start(bf16[512,1,768]{2,1,0:T(2,128)(2,1)} %copy-done.1) | copy-start | bytes 2359300
  203.5 5.9 %copy-start.4 = (bf16[512,1,768]{2,1,0:T(2,128)(2,1)S(1)}, bf16[512,1,768]{2,1,0:T(2,128)(2,1)}, u32[]{:S(2)}) copy-start(bf16[512,1,768]{2,1,0:T(2,128)(2,1)} %copy-done.3) | copy-start | bytes 2359300
  203.5 5.9 %copy-start.15 = (bf16[256,768]{1,0:T(8,128)(2,1)S(1)}, bf16[256,768]{1,0:T(8,128)(2,1)}, u32[]{:S(2)}) copy-start(bf16[256,768]{1,0:T(8,128)(2,1)} %param.14) | copy-start | bytes 1179652
  203.6 5.9 %copy-start.23 = (s32[512]{0:T(512)S(1)}, s32[512]{0:T(512)}, u32[]{:S(2)}) copy-start(s32[512]{0:T(512)} %select_reduce_fusion) | copy-start | bytes 6148
  203.6 5.9 %copy-start.24 = (s32[256]{0:T(256)S(1)}, s32[256]{0:T(256)}, u32[]{:S(2)}) copy-start(s32[256]{0:T(256)} %and_select_fusion) | copy-start | bytes 3076
  (11 other events, 20.3 us)

commit v8 on v7

--- a/solution.py
+++ b/solution.py
@@ -148,12 +148,8 @@
         gate[:, :, None], (tok_rows, expert_count, rows_per_expert)
     ).reshape(tok_rows, chunk_count * pad_rows)
     weights = jnp.where(rank_cols == row_slot[None, :], gate_cols, 0.0)
-    weights_hi = weights.astype(jnp.bfloat16)
-    weights_lo = (weights - weights_hi.astype(jnp.float32)).astype(jnp.bfloat16)
     back = returned.reshape(chunk_count * pad_rows, feat_local)
-    routed = jnp.dot(weights_hi, back, preferred_element_type=jnp.float32) + jnp.dot(
-        weights_lo, back, preferred_element_type=jnp.float32
-    )
+    routed = jnp.dot(weights.astype(jnp.bfloat16), back, preferred_element_type=jnp.float32)
     return (shared_out + 0.5 * delta + routed).astype(jnp.bfloat16)
 
 

time: 212 us -> 206 us (0.972)
  matrix products: 40.2 us -> 34.3 us
  other arithmetic: 23.4 us -> 20.8 us
    dot_general x2 -> x1, matrix products: 13.1 us -> 7.24 us  [body(): jnp.dot(weights.astype(jnp.bfloat16), back, preferred_element_type=jnp.fl...]
    convert_element_type x2 -> x1, other arithmetic: 5.29 us -> 2.9 us  [body(): weights.astype(jnp.bfloat16)]
    all_to_all x1, waiting for transfers between devices: 44.6 us -> 46.9 us  [body(): lax.all_to_all(expert_out.reshape(req_count * blk_count, pad_rows, feat_l...]
    unnamed x57 -> x55, local copies, waits for them, and re-layouts: 4.63 us -> 4.88 us
  transfers between devices with their start and end apart: 7 -> 7, of which waited for: 3 -> 3; matrix products, arithmetic and copies ran while one was open for 27% -> 23% of each run, Pallas kernels for 0% -> 0%
where the time goes in v8:
time: 206 us; the launch traced here: 205 us
  waiting for transfers between devices  119 us (58%)
  matrix products  34.3 us (17%)
  other arithmetic  20.8 us (10%)
  starting transfers between devices  17.7 us (9%)
  local copies, waits for them, and re-layouts  12.9 us (6%)
    all_to_all x1, waiting for transfers between devices, body(): lax.all_to_all(send_rows.reshape(chunk_count, pad_rows, feat_local), both...  69.2 us
    all_to_all x1, waiting for transfers between devices, body(): lax.all_to_all(expert_out.reshape(req_count * blk_count, pad_rows, feat_l...  46.9 us
    all_to_all x1, starting transfers between devices, body(): lax.all_to_all(send_rows.reshape(chunk_count, pad_rows, feat_local), both...  10.9 us
    dot_general x1, matrix products, body(): jnp.einsum('gcsd,cdf->gsf', rows_in, weight_gate_up, preferred_element_ty...  9.69 us
    dot_general x1, matrix products, body(): jnp.dot(weights.astype(jnp.bfloat16), back, preferred_element_type=jnp.fl...  7.24 us
    dot_general x1, matrix products, body(): jnp.dot(pick.astype(jnp.bfloat16), normed, preferred_element_type=jnp.flo...  5.3 us
    all_to_all x1, starting transfers between devices, body(): lax.all_to_all(expert_out.reshape(req_count * blk_count, pad_rows, feat_l...  5.27 us
    unnamed x55, local copies, waits for them, and re-layouts  4.88 us
  transfers between devices with their start and end apart: 7, of which 3 were waited for; matrix products, arithmetic and copies ran while one was open for 23% of the time, Pallas kernels for 0%

profile of v8, /device:TPU:2, one launch (start us, length us, event | category | flops | bytes accessed | tf_op | source)
XLA Modules:
  0.0 205.2 jit_solution(6928258159742158348)
XLA Ops:
  1.9 1.3 bitcast_compare_fusion
  3.3 5.3 %convolution_convert_fusion = bf16[4096,768]{1,0:T(8,128)(2,1)} fusion(pred[4096,512]{1,0:T(32,128)(4,1)S(1)} %bitcast_compare_fusion, bf16[512,768]{1,0:T(8,128)(2,1)S(1)} %copy-done.6), kind=kOutput, calls=%fused_computation.2 | convolution fusion | flops 3224371200 | bytes 9175040 | tf_op jit(solution)/shard_map/dot_general | solution.py:67
  8.6 10.9 %all-to-all-start = ((bf16[128,32,768]{2,1,0:T(8,128)(2,1)}), bf16[128,32,768]{2,1,0:T(8,128)(2,1)}, u32[]{:S(2)}, u32[]{:S(2)}) async-start(bf16[128,32,768]{2,1,0:T(8,128)(2,1)} %bitcast.68), calls=%async_computation | async-start | bytes 12582912 | tf_op jit(solution)/shard_map/all_to_all | solution.py:71
  20.1 3.0 %collective-permute-done.3 = bf16[768,1024]{1,0:T(8,128)(2,1)} collective-permute-done((bf16[768,1024]{1,0:T(8,128)(2,1)S(1)}, bf16[768,1024]{1,0:T(8,128)(2,1)}, u32[]{:S(2)}, u32[]{:S(2)}) %collective-permute-start.3) | collective-permute-done | bytes 1572896 | tf_op jit(solution)/shard_map/ppermute | solution.py:10
  23.2 3.3 %select_bitcast_fusion.1 = (bf16[1,768,1024]{2,1,0:T(8,128)(2,1)}, bf16[1,768,1024]{2,1,0:T(8,128)(2,1)}) fusion(bf16[768,1024]{1,0:T(8,128)(2,1)} %collective-permute-done.3, pred[]{:T(512)S(6)} %eq.197, bf16[1,768,1024]{2,1,0:T(8,128)(2,1)S(1)} %copy-done.5), kind=kLoop, calls=%fused_computation.16 | loop fusion | flops 1572864 | bytes 6291457 | tf_op jit(solution)/shard_map/stack | solution.py:19
  26.4 69.2 %all-to-all-done = bf16[128,32,768]{2,1,0:T(8,128)(2,1)} async-done(((bf16[128,32,768]{2,1,0:T(8,128)(2,1)}), bf16[128,32,768]{2,1,0:T(8,128)(2,1)}, u32[]{:S(2)}, u32[]{:S(2)}) %all-to-all-start) | async-done | bytes 6291488 | tf_op jit(solution)/shard_map/all_to_all | solution.py:71
  95.6 9.7 %convolution_bitcast_fusion = f32[64,32,1024]{2,1,0:T(8,128)S(1)} fusion(bf16[64,2,32,768]{3,2,1,0:T(8,128)(2,1)} %bitcast.15, bf16[1,768,1024]{2,1,0:T(8,128)(2,1)} %get-tuple-element.12, bf16[1,768,1024]{2,1,0:T(8,128)(2,1)} %get-tuple-element.11), kind=kOutput, calls=%fused_computation.8 | convolution fusion | flops 6444023808 | bytes 17825792 | tf_op jit(solution)/shard_map/gcsd,cdf->gsf/dot_general | solution.py:81
  105.3 1.5 fusion
  106.9 3.0 %convolution_convert_fusion.1 = bf16[2048,768]{1,0:T(8,128)(2,1)S(1)} fusion(bf16[2048,512]{1,0:T(8,128)(2,1)S(1)} %bitcast.74, bf16[512,768]{1,0:T(8,128)(2,1)} %collective-permute-done.4, pred[]{:T(512)S(6)} %eq.197, bf16[1,512,768]{2,1,0:T(8,128)(2,1)S(1)} %copy-done.26), kind=kOutput, calls=%fused_computation.6 | convolution fusion | flops 1612578816 | bytes 6815745 | tf_op jit(solution)/shard_map/dot_general | solution.py:94
  109.8 1.8 convolution_convert_fusion.2
  111.7 3.2 %pad_maximum_fusion = bf16[64,2,32,768]{3,2,1,0:T(8,128)(2,1)} fusion(bf16[64,1,32,768]{3,2,1,0:T(8,128)(2,1)S(1)} %bitcast.72, bf16[64,1,32,768]{3,2,1,0:T(8,128)(2,1)S(1)} %bitcast.73), kind=kLoop, calls=%fused_computation.3 | loop fusion | flops 3145728 | bytes 12582912 | tf_op jit(solution)/shard_map/stack | solution.py:92
  114.9 5.3 %all-to-all-start.1 = ((bf16[128,32,768]{2,1,0:T(8,128)(2,1)}), bf16[128,32,768]{2,1,0:T(8,128)(2,1)}, u32[]{:S(2)}, u32[]{:S(2)}) async-start(bf16[128,32,768]{2,1,0:T(8,128)(2,1)} %bitcast.67), calls=%async_computation.1 | async-start | bytes 12582912 | tf_op jit(solution)/shard_map/all_to_all | solution.py:101
  121.7 1.7 pad_maximum_fusion.4
  123.8 1.4 reduce-window.8
  125.2 2.8 %copy.35 = bf16[192,8,2,512]{3,1,2,0:T(8,128)(2,1)S(1)} copy(bf16[192,8,2,512]{3,2,1,0:T(2,128)(2,1)} %bitcast.70) | data formatting | bytes 6291456
  129.9 2.2 %broadcast_select_fusion.3 = (bf16[768,320]{0,1:T(8,128)(2,1)}, bf16[768,320]{0,1:T(8,128)(2,1)}) fusion(bf16[768,320]{0,1:T(8,128)(2,1)} %collective-permute-done.2, pred[]{:T(512)S(6)} %eq.197, bf16[768,256]{0,1:T(8,128)(2,1)S(1)} %copy.29, bf16[768,64]{0,1:T(8,128)(2,1)S(1)} %copy-done.15), kind=kLoop, calls=%fused_computation.39 | loop fusion | flops 1474560 | bytes 1966081 | tf_op jit(solution)/shard_map/jit(_where)/select_n | solution.py:16
  132.3 1.8 fusion.6
  134.1 2.2 %convolution_convert_fusion.3 = bf16[512,1536]{1,0:T(8,128)(2,1)} fusion(bf16[512,1536]{1,0:T(8,128)(2,1)S(1)} %copy-done, f32[512,1024]{1,0:T(8,128)S(1)} %fusion.6), kind=kOutput, calls=%fused_computation.12 | convolution fusion | flops 807665664 | bytes 5242880 | tf_op jit(solution)/shard_map/dot_general | solution.py:134
  136.3 3.6 %reshape.181 = bf16[512,2,768]{2,1,0:T(2,128)(2,1)S(1)} reshape(bf16[512,1536]{1,0:T(8,128)(2,1)} %convolution_convert_fusion.3) | data formatting | bytes 3145728 | tf_op jit(solution)/shard_map/reshape | solution.py:135
  139.9 2.2 %fusion.68 = (bf16[512,1,768]{2,1,0:T(2,128)(2,1)S(1)}, bf16[512,1,768]{2,1,0:T(2,128)(2,1)S(1)}) fusion(bf16[512,2,768]{2,1,0:T(2,128)(2,1)S(1)} %reshape.181), kind=kLoop, calls=%fused_computation.127 | loop fusion | bytes 3145728 | tf_op jit(solution)/shard_map/slice | solution.py:137
  146.5 2.9 %select_convert_fusion = bf16[512,64,64]{0,2,1:T(8,128)(2,1)} fusion(bf16[512,64]{0,1:T(8,128)(2,1)S(1)} %broadcast_divide_fusion, s32[64,64]{1,0:T(8,128)S(1)} %copy-done.16, s32[512,64]{0,1:T(8,128)S(1)} %get-tuple-element.25), kind=kLoop, calls=%fused_computation.1 | loop fusion | flops 4194304 | bytes 4407296 | tf_op jit(solution)/shard_map/convert_element_type | solution.py:152
  149.4 46.9 %all-to-all-done.1 = bf16[128,32,768]{2,1,0:T(8,128)(2,1)} async-done(((bf16[128,32,768]{2,1,0:T(8,128)(2,1)}), bf16[128,32,768]{2,1,0:T(8,128)(2,1)}, u32[]{:S(2)}, u32[]{:S(2)}) %all-to-all-start.1) | async-done | bytes 6291488 | tf_op jit(solution)/shard_map/all_to_all | solution.py:101
  196.3 7.2 %fusion.70 = f32[512,768]{1,0:T(8,128)S(1)} fusion(bf16[512,4096]{0,1:T(8,128)(2,1)} %bitcast.69, bf16[4096,768]{1,0:T(8,128)(2,1)} %bitcast.29), kind=kOutput, calls=%fused_computation.129 | convolution fusion | flops 3221225472 | bytes 12058624 | tf_op jit(solution)/shard_map/dot_general | solution.py:152
  203.6 1.6 add_convert_fusion
  (76 shorter events, 10.8 us)
Async XLA Ops:
  0.0 134.1 %copy-start = (bf16[512,1536]{1,0:T(8,128)(2,1)S(1)}, bf16[512,1536]{1,0:T(8,128)(2,1)}, u32[]{:S(2)}) copy-start(bf16[512,1536]{1,0:T(8,128)(2,1)} %param.16) | copy-start | bytes 4718596
  0.0 3.3 %copy-start.6 = (bf16[512,768]{1,0:T(8,128)(2,1)S(1)}, bf16[512,768]{1,0:T(8,128)(2,1)}, u32[]{:S(2)}) copy-start(bf16[512,768]{1,0:T(8,128)(2,1)} %param.11) | copy-start | bytes 2359300
  8.6 10.9 %copy-start.5 = (bf16[1,768,1024]{2,1,0:T(8,128)(2,1)S(1)}, bf16[1,768,1024]{2,1,0:T(8,128)(2,1)}, u32[]{:S(2)}) copy-start(bf16[1,768,1024]{2,1,0:T(8,128)(2,1)} %param.17) | copy-start | bytes 4718596
  8.6 87.0 %all-to-all-start = ((bf16[128,32,768]{2,1,0:T(8,128)(2,1)}), bf16[128,32,768]{2,1,0:T(8,128)(2,1)}, u32[]{:S(2)}, u32[]{:S(2)}) async-start(bf16[128,32,768]{2,1,0:T(8,128)(2,1)} %bitcast.68), calls=%async_computation | async-start | bytes 12582912 | tf_op jit(solution)/shard_map/all_to_all | solution.py:71
  19.6 3.6 %collective-permute-start.3 = (bf16[768,1024]{1,0:T(8,128)(2,1)S(1)}, bf16[768,1024]{1,0:T(8,128)(2,1)}, u32[]{:S(2)}, u32[]{:S(2)}) collective-permute-start(bf16[768,1024]{1,0:T(8,128)(2,1)S(1)} %bitcast.76), channel_id=1, source_target_pairs={{0,1},{1,0},{2,3},{3,2},{4,5},{5,4},{6,7},{7,6},{8,9},{9,8},{10,11... | collective-permute-start | bytes 4718600 | tf_op jit(solution)/shard_map/ppermute | solution.py:10
  19.7 87.1 %collective-permute-start.4 = (bf16[512,768]{1,0:T(8,128)(2,1)}, bf16[512,768]{1,0:T(8,128)(2,1)}, u32[]{:S(2)}, u32[]{:S(2)}) collective-permute-start(bf16[512,768]{1,0:T(8,128)(2,1)} %bitcast.97), channel_id=1, source_target_pairs={{0,1},{1,0},{2,3},{3,2},{4,5},{5,4},{6,7},{7,6},{8,9},{9,8},{10,11... | collective-permute-start | bytes 2359304 | tf_op jit(solution)/shard_map/ppermute | solution.py:10
  114.9 5.3 %copy-start.7 = (bf16[512,768]{1,0:T(8,128)(2,1)S(1)}, bf16[512,768]{1,0:T(8,128)(2,1)}, u32[]{:S(2)}) copy-start(bf16[512,768]{1,0:T(8,128)(2,1)} %param.11) | copy-start | bytes 2359300
  114.9 81.4 %all-to-all-start.1 = ((bf16[128,32,768]{2,1,0:T(8,128)(2,1)}), bf16[128,32,768]{2,1,0:T(8,128)(2,1)}, u32[]{:S(2)}, u32[]{:S(2)}) async-start(bf16[128,32,768]{2,1,0:T(8,128)(2,1)} %bitcast.67), calls=%async_computation.1 | async-start | bytes 12582912 | tf_op jit(solution)/shard_map/all_to_all | solution.py:101
  120.2 12.0 %collective-permute-start = (bf16[512,768]{1,0:T(8,128)(2,1)S(1)}, bf16[512,768]{1,0:T(8,128)(2,1)S(1)}, u32[]{:S(2)}, u32[]{:S(2)}) collective-permute-start(bf16[512,768]{1,0:T(8,128)(2,1)S(1)} %copy-done.7), channel_id=1, source_target_pairs={{0,1},{1,0},{2,3},{3,2},{4,5},{5,4},{6,7},{7,6},{8,9},{9,8},{10,11... | collective-permute-start | bytes 2359304 | tf_op jit(solution)/shard_map/ppermute | solution.py:10
  123.4 6.5 %collective-permute-start.2 = (bf16[768,320]{0,1:T(8,128)(2,1)}, bf16[768,320]{0,1:T(8,128)(2,1)}, u32[]{:S(2)}, u32[]{:S(2)}) collective-permute-start(bf16[768,320]{0,1:T(8,128)(2,1)} %pad_maximum_fusion.4), channel_id=1, source_target_pairs={{0,1},{1,0},{2,3},{3,2},{4,5},{5,4},{6,7},{7,6},{8,9},{9,8},{10,11... | collective-permute-start | bytes 1474568 | tf_op jit(solution)/shard_map/ppermute | solution.py:10
  125.2 4.0 %copy-start.25 = (s32[4,1]{0,1:T(1,128)S(1)}, s32[4,1]{0,1:T(1,128)}, u32[]{:S(2)}) copy-start(s32[4,1]{0,1:T(1,128)} %reduce-window.8) | copy-start | bytes 52
  125.2 4.1 %copy-start.24 = (s32[1,4]{1,0:T(1,128)S(1)}, s32[1,4]{1,0:T(1,128)}, u32[]{:S(2)}) copy-start(s32[1,4]{1,0:T(1,128)} %param.20) | copy-start | bytes 52
  125.2 4.7 %copy-start.15 = (bf16[768,64]{0,1:T(8,128)(2,1)S(1)}, bf16[768,64]{0,1:T(8,128)(2,1)}, u32[]{:S(2)}) copy-start(bf16[768,64]{0,1:T(8,128)(2,1)} %param.12) | copy-start | bytes 294916
  142.2 3.8 %copy-start.1 = (bf16[512,1,768]{2,1,0:T(2,128)(2,1)}, bf16[512,1,768]{2,1,0:T(2,128)(2,1)S(1)}, u32[]{:S(2)}) copy-start(bf16[512,1,768]{2,1,0:T(2,128)(2,1)S(1)} %get-tuple-element.13) | copy-start | bytes 2359300
  142.2 3.8 %copy-start.3 = (bf16[512,1,768]{2,1,0:T(2,128)(2,1)}, bf16[512,1,768]{2,1,0:T(2,128)(2,1)S(1)}, u32[]{:S(2)}) copy-start(bf16[512,1,768]{2,1,0:T(2,128)(2,1)S(1)} %get-tuple-element.14) | copy-start | bytes 2359300
  142.2 2.5 %copy-start.11 = (bf16[512,768]{1,0:T(8,128)(2,1)S(1)}, bf16[512,768]{1,0:T(8,128)(2,1)}, u32[]{:S(2)}) copy-start(bf16[512,768]{1,0:T(8,128)(2,1)} %copy-done.10) | copy-start | bytes 2359300
  142.2 2.9 %copy-start.12 = (bf16[768,320]{0,1:T(8,128)(2,1)S(1)}, bf16[768,320]{0,1:T(8,128)(2,1)}, u32[]{:S(2)}) copy-start(bf16[768,320]{0,1:T(8,128)(2,1)} %get-tuple-element.17) | copy-start | bytes 1474564
  142.2 3.0 %copy-start.13 = (bf16[768,320]{0,1:T(8,128)(2,1)S(1)}, bf16[768,320]{0,1:T(8,128)(2,1)}, u32[]{:S(2)}) copy-start(bf16[768,320]{0,1:T(8,128)(2,1)} %get-tuple-element.18) | copy-start | bytes 1474564
  143.3 60.2 %collective-permute-start.1 = (bf16[512,768]{1,0:T(8,128)(2,1)}, bf16[512,768]{1,0:T(8,128)(2,1)S(1)}, u32[]{:S(2)}, u32[]{:S(2)}) collective-permute-start(bf16[512,768]{1,0:T(8,128)(2,1)} %select_bitcast_fusion.2), channel_id=1, source_target_pairs={{0,1},{1,0},{2,3},{3,2},{4,5},{5,4},{6,7},{7,6},{8,9},{9,8},{10,11... | collective-permute-start | bytes 2359304 | tf_op jit(solution)/shard_map/ppermute | solution.py:10
  196.2 7.3 %copy-start.2 = (bf16[512,1,768]{2,1,0:T(2,128)(2,1)S(1)}, bf16[512,1,768]{2,1,0:T(2,128)(2,1)}, u32[]{:S(2)}) copy-start(bf16[512,1,768]{2,1,0:T(2,128)(2,1)} %copy-done.1) | copy-start | bytes 2359300
  196.2 7.3 %copy-start.4 = (bf16[512,1,768]{2,1,0:T(2,128)(2,1)S(1)}, bf16[512,1,768]{2,1,0:T(2,128)(2,1)}, u32[]{:S(2)}) copy-start(bf16[512,1,768]{2,1,0:T(2,128)(2,1)} %copy-done.3) | copy-start | bytes 2359300
  196.2 7.3 %copy-start.14 = (bf16[256,768]{1,0:T(8,128)(2,1)S(1)}, bf16[256,768]{1,0:T(8,128)(2,1)}, u32[]{:S(2)}) copy-start(bf16[256,768]{1,0:T(8,128)(2,1)} %param.14) | copy-start | bytes 1179652
  196.2 7.3 %copy-start.22 = (s32[512]{0:T(512)S(1)}, s32[512]{0:T(512)}, u32[]{:S(2)}) copy-start(s32[512]{0:T(512)} %select_reduce_fusion) | copy-start | bytes 6148
  196.2 7.3 %copy-start.23 = (s32[256]{0:T(256)S(1)}, s32[256]{0:T(256)}, u32[]{:S(2)}) copy-start(s32[256]{0:T(256)} %and_select_fusion) | copy-start | bytes 3076
  (10 other events, 12.8 us)

commit v9 on v8

--- a/solution.py
+++ b/solution.py
@@ -148,9 +148,12 @@
         gate[:, :, None], (tok_rows, expert_count, rows_per_expert)
     ).reshape(tok_rows, chunk_count * pad_rows)
     weights = jnp.where(rank_cols == row_slot[None, :], gate_cols, 0.0)
+    weights, base = lax.optimization_barrier(
+        (weights.astype(jnp.bfloat16), shared_out + 0.5 * delta)
+    )
     back = returned.reshape(chunk_count * pad_rows, feat_local)
-    routed = jnp.dot(weights.astype(jnp.bfloat16), back, preferred_element_type=jnp.float32)
-    return (shared_out + 0.5 * delta + routed).astype(jnp.bfloat16)
+    routed = jnp.dot(weights, back, preferred_element_type=jnp.float32)
+    return (base + routed).astype(jnp.bfloat16)
 
 
 def solution(mesh):

time: 206 us -> 205 us (level)
  waiting for transfers between devices: 119 us -> 123 us
    all_to_all x1, waiting for transfers between devices: 46.9 us -> 50.5 us  [body(): lax.all_to_all(expert_out.reshape(req_count * blk_count, pad_rows, feat_l...]
    unnamed x55 -> x57, local copies, waits for them, and re-layouts: 4.88 us -> 3.48 us
  transfers between devices with their start and end apart: 7 -> 7, of which waited for: 3 -> 3; matrix products, arithmetic and copies ran while one was open for 23% -> 19% of each run, Pallas kernels for 0% -> 0%
where the time goes in v9:
time: 205 us
  waiting for transfers between devices  123 us (60%)
  matrix products  33.1 us (16%)
  other arithmetic  18.9 us (9%)
  starting transfers between devices  17.8 us (9%)
  local copies, waits for them, and re-layouts  11.5 us (6%)
    all_to_all x1, waiting for transfers between devices, body(): lax.all_to_all(send_rows.reshape(chunk_count, pad_rows, feat_local), both...  69.2 us
    all_to_all x1, waiting for transfers between devices, body(): lax.all_to_all(expert_out.reshape(req_count * blk_count, pad_rows, feat_l...  50.5 us
    all_to_all x1, starting transfers between devices, body(): lax.all_to_all(send_rows.reshape(chunk_count, pad_rows, feat_local), both...  10.9 us
    dot_general x1, matrix products, body(): jnp.einsum('gcsd,cdf->gsf', rows_in, weight_gate_up, preferred_element_ty...  9.69 us
    dot_general x1, matrix products, body(): routed = jnp.dot(weights, back, preferred_element_type=jnp.float32)  7.09 us
    dot_general x1, matrix products, body(): jnp.dot(pick.astype(jnp.bfloat16), normed, preferred_element_type=jnp.flo...  5.33 us
    all_to_all x1, starting transfers between devices, body(): lax.all_to_all(expert_out.reshape(req_count * blk_count, pad_rows, feat_l...  5.27 us
    dot_general x2, matrix products, body(): jnp.dot(hidden_rows, weight_down[c], preferred_element_type=jnp.float32)  4.79 us
  transfers between devices with their start and end apart: 7, of which 3 were waited for; matrix products, arithmetic and copies ran while one was open for 19% of the time, Pallas kernels for 0%

profile of v9, /device:TPU:2, one launch (start us, length us, event | category | flops | bytes accessed | tf_op | source)
XLA Modules:
  0.0 204.5 jit_solution(17322673965750572648)
XLA Ops:
  2.0 1.3 bitcast_compare_fusion
  3.3 5.3 %convolution_convert_fusion = bf16[4096,768]{1,0:T(8,128)(2,1)} fusion(pred[4096,512]{1,0:T(32,128)(4,1)S(1)} %bitcast_compare_fusion, bf16[512,768]{1,0:T(8,128)(2,1)S(1)} %copy-done.2), kind=kOutput, calls=%fused_computation.4 | convolution fusion | flops 3224371200 | bytes 9175040 | tf_op jit(solution)/shard_map/dot_general | solution.py:67
  8.7 10.9 %all-to-all-start = ((bf16[128,32,768]{2,1,0:T(8,128)(2,1)}), bf16[128,32,768]{2,1,0:T(8,128)(2,1)}, u32[]{:S(2)}, u32[]{:S(2)}) async-start(bf16[128,32,768]{2,1,0:T(8,128)(2,1)} %bitcast.75), calls=%async_computation | async-start | bytes 12582912 | tf_op jit(solution)/shard_map/all_to_all | solution.py:71
  20.3 3.0 %collective-permute-done.3 = bf16[768,1024]{1,0:T(8,128)(2,1)} collective-permute-done((bf16[768,1024]{1,0:T(8,128)(2,1)S(1)}, bf16[768,1024]{1,0:T(8,128)(2,1)}, u32[]{:S(2)}, u32[]{:S(2)}) %collective-permute-start.3) | collective-permute-done | bytes 1572896 | tf_op jit(solution)/shard_map/ppermute | solution.py:10
  23.3 3.3 %select_bitcast_fusion.1 = (bf16[1,768,1024]{2,1,0:T(8,128)(2,1)}, bf16[1,768,1024]{2,1,0:T(8,128)(2,1)}) fusion(bf16[768,1024]{1,0:T(8,128)(2,1)} %collective-permute-done.3, pred[]{:T(512)S(6)} %eq.216, bf16[1,768,1024]{2,1,0:T(8,128)(2,1)S(1)} %copy-done.1), kind=kLoop, calls=%fused_computation.18 | loop fusion | flops 1572864 | bytes 6291457 | tf_op jit(solution)/shard_map/stack | solution.py:19
  26.6 69.2 %all-to-all-done = bf16[128,32,768]{2,1,0:T(8,128)(2,1)} async-done(((bf16[128,32,768]{2,1,0:T(8,128)(2,1)}), bf16[128,32,768]{2,1,0:T(8,128)(2,1)}, u32[]{:S(2)}, u32[]{:S(2)}) %all-to-all-start) | async-done | bytes 6291488 | tf_op jit(solution)/shard_map/all_to_all | solution.py:71
  95.7 9.7 %convolution_bitcast_fusion = f32[64,32,1024]{2,1,0:T(8,128)S(1)} fusion(bf16[64,2,32,768]{3,2,1,0:T(8,128)(2,1)} %bitcast.16, bf16[1,768,1024]{2,1,0:T(8,128)(2,1)} %get-tuple-element.16, bf16[1,768,1024]{2,1,0:T(8,128)(2,1)} %get-tuple-element.15), kind=kOutput, calls=%fused_computation.10 | convolution fusion | flops 6444023808 | bytes 17825792 | tf_op jit(solution)/shard_map/gcsd,cdf->gsf/dot_general | solution.py:81
  105.5 1.5 fusion.1
  107.0 3.0 %convolution_convert_fusion.1 = bf16[2048,768]{1,0:T(8,128)(2,1)S(1)} fusion(bf16[2048,512]{1,0:T(8,128)(2,1)S(1)} %bitcast.80, bf16[512,768]{1,0:T(8,128)(2,1)} %collective-permute-done.4, pred[]{:T(512)S(6)} %eq.216, bf16[1,512,768]{2,1,0:T(8,128)(2,1)S(1)} %copy-done.25), kind=kOutput, calls=%fused_computation.8 | convolution fusion | flops 1612578816 | bytes 6815745 | tf_op jit(solution)/shard_map/dot_general | solution.py:94
  109.9 1.8 convolution_convert_fusion.2
  111.8 3.2 %pad_maximum_fusion = bf16[64,2,32,768]{3,2,1,0:T(8,128)(2,1)} fusion(bf16[64,1,32,768]{3,2,1,0:T(8,128)(2,1)S(1)} %bitcast.78, bf16[64,1,32,768]{3,2,1,0:T(8,128)(2,1)S(1)} %bitcast.79), kind=kLoop, calls=%fused_computation.5 | loop fusion | flops 3145728 | bytes 12582912 | tf_op jit(solution)/shard_map/stack | solution.py:92
  115.0 5.3 %all-to-all-start.1 = ((bf16[128,32,768]{2,1,0:T(8,128)(2,1)}), bf16[128,32,768]{2,1,0:T(8,128)(2,1)}, u32[]{:S(2)}, u32[]{:S(2)}) async-start(bf16[128,32,768]{2,1,0:T(8,128)(2,1)} %bitcast.74), calls=%async_computation.1 | async-start | bytes 12582912 | tf_op jit(solution)/shard_map/all_to_all | solution.py:101
  120.7 1.2 copy.27
  121.8 1.7 pad_maximum_fusion.4
  124.0 1.3 reduce-window.8
  125.3 2.8 %copy.35 = bf16[192,8,2,512]{3,1,2,0:T(8,128)(2,1)S(1)} copy(bf16[192,8,2,512]{3,2,1,0:T(2,128)(2,1)} %bitcast.76) | data formatting | bytes 6291456
  129.6 1.8 fusion.6
  131.4 2.2 %convolution_convert_fusion.3 = bf16[512,1536]{1,0:T(8,128)(2,1)} fusion(bf16[512,1536]{1,0:T(8,128)(2,1)S(1)} %copy-done, f32[512,1024]{1,0:T(8,128)S(1)} %fusion.6), kind=kOutput, calls=%fused_computation.14 | convolution fusion | flops 807665664 | bytes 5242880 | tf_op jit(solution)/shard_map/dot_general | solution.py:134
  133.6 3.6 %reshape.151 = bf16[512,2,768]{2,1,0:T(2,128)(2,1)S(1)} reshape(bf16[512,1536]{1,0:T(8,128)(2,1)} %convolution_convert_fusion.3) | data formatting | bytes 3145728 | tf_op jit(solution)/shard_map/reshape | solution.py:135
  137.2 2.2 %fusion.59 = (bf16[512,1,768]{2,1,0:T(2,128)(2,1)S(1)}, bf16[512,1,768]{2,1,0:T(2,128)(2,1)S(1)}) fusion(bf16[512,2,768]{2,1,0:T(2,128)(2,1)S(1)} %reshape.151), kind=kLoop, calls=%fused_computation.113 | loop fusion | bytes 3145728 | tf_op jit(solution)/shard_map/slice | solution.py:137
  140.4 1.2 broadcast_select_fusion.3
  142.8 2.4 %fusion = bf16[512,4096]{0,1:T(8,128)(2,1)} fusion(bf16[512,64]{0,1:T(8,128)(2,1)S(1)} %broadcast_divide_fusion, s32[4096]{0:T(1024)S(1)} %fusion.48, s32[512,64]{0,1:T(8,128)S(1)} %get-tuple-element.29), kind=kLoop, calls=%fused_computation.1 | loop fusion | flops 4194304 | bytes 4407296 | tf_op jit(solution)/shard_map/convert_element_type | solution.py:152
  145.9 50.5 %all-to-all-done.1 = bf16[128,32,768]{2,1,0:T(8,128)(2,1)} async-done(((bf16[128,32,768]{2,1,0:T(8,128)(2,1)}), bf16[128,32,768]{2,1,0:T(8,128)(2,1)}, u32[]{:S(2)}, u32[]{:S(2)}) %all-to-all-start.1) | async-done | bytes 6291488 | tf_op jit(solution)/shard_map/all_to_all | solution.py:101
  196.4 7.1 %fusion.61 = f32[512,768]{1,0:T(8,128)S(1)} fusion(bf16[512,4096]{0,1:T(8,128)(2,1)} %fusion, bf16[4096,768]{1,0:T(8,128)(2,1)} %bitcast.30), kind=kOutput, calls=%fused_computation.115 | convolution fusion | flops 3221225472 | bytes 12058624 | tf_op jit(solution)/shard_map/dot_general | solution.py:155
  (78 shorter events, 8.5 us)
Async XLA Ops:
  0.0 131.4 %copy-start = (bf16[512,1536]{1,0:T(8,128)(2,1)S(1)}, bf16[512,1536]{1,0:T(8,128)(2,1)}, u32[]{:S(2)}) copy-start(bf16[512,1536]{1,0:T(8,128)(2,1)} %param.16) | copy-start | bytes 4718596
  0.0 3.3 %copy-start.2 = (bf16[512,768]{1,0:T(8,128)(2,1)S(1)}, bf16[512,768]{1,0:T(8,128)(2,1)}, u32[]{:S(2)}) copy-start(bf16[512,768]{1,0:T(8,128)(2,1)} %param.11) | copy-start | bytes 2359300
  1.0 7.7 %copy-start.10 = (s32[512,1]{0,1:T(1,128)}, s32[512,1]{0,1:T(1,128)S(1)}, u32[]{:S(2)}) copy-start(s32[512,1]{0,1:T(1,128)S(1)} %get-tuple-element.23) | copy-start | bytes 6148
  1.0 7.7 %copy-start.12 = (s32[512,1]{0,1:T(1,128)}, s32[512,1]{0,1:T(1,128)S(1)}, u32[]{:S(2)}) copy-start(s32[512,1]{0,1:T(1,128)S(1)} %get-tuple-element.24) | copy-start | bytes 6148
  1.0 7.7 %copy-start.14 = (s32[512,1]{0,1:T(1,128)}, s32[512,1]{0,1:T(1,128)S(1)}, u32[]{:S(2)}) copy-start(s32[512,1]{0,1:T(1,128)S(1)} %get-tuple-element.25) | copy-start | bytes 6148
  1.0 7.7 %copy-start.16 = (s32[512,1]{0,1:T(1,128)}, s32[512,1]{0,1:T(1,128)S(1)}, u32[]{:S(2)}) copy-start(s32[512,1]{0,1:T(1,128)S(1)} %get-tuple-element.26) | copy-start | bytes 6148
  1.0 7.7 %copy-start.18 = (s32[512,1]{0,1:T(1,128)}, s32[512,1]{0,1:T(1,128)S(1)}, u32[]{:S(2)}) copy-start(s32[512,1]{0,1:T(1,128)S(1)} %get-tuple-element.27) | copy-start | bytes 6148
  1.0 7.7 %copy-start.20 = (s32[512,1]{0,1:T(1,128)}, s32[512,1]{0,1:T(1,128)S(1)}, u32[]{:S(2)}) copy-start(s32[512,1]{0,1:T(1,128)S(1)} %get-tuple-element.28) | copy-start | bytes 6148
  8.7 11.0 %copy-start.1 = (bf16[1,768,1024]{2,1,0:T(8,128)(2,1)S(1)}, bf16[1,768,1024]{2,1,0:T(8,128)(2,1)}, u32[]{:S(2)}) copy-start(bf16[1,768,1024]{2,1,0:T(8,128)(2,1)} %param.17) | copy-start | bytes 4718596
  8.7 87.0 %all-to-all-start = ((bf16[128,32,768]{2,1,0:T(8,128)(2,1)}), bf16[128,32,768]{2,1,0:T(8,128)(2,1)}, u32[]{:S(2)}, u32[]{:S(2)}) async-start(bf16[128,32,768]{2,1,0:T(8,128)(2,1)} %bitcast.75), calls=%async_computation | async-start | bytes 12582912 | tf_op jit(solution)/shard_map/all_to_all | solution.py:71
  19.7 3.6 %collective-permute-start.3 = (bf16[768,1024]{1,0:T(8,128)(2,1)S(1)}, bf16[768,1024]{1,0:T(8,128)(2,1)}, u32[]{:S(2)}, u32[]{:S(2)}) collective-permute-start(bf16[768,1024]{1,0:T(8,128)(2,1)S(1)} %bitcast.82), channel_id=1, source_target_pairs={{0,1},{1,0},{2,3},{3,2},{4,5},{5,4},{6,7},{7,6},{8,9},{9,8},{10,11... | collective-permute-start | bytes 4718600 | tf_op jit(solution)/shard_map/ppermute | solution.py:10
  19.9 87.1 %collective-permute-start.4 = (bf16[512,768]{1,0:T(8,128)(2,1)}, bf16[512,768]{1,0:T(8,128)(2,1)}, u32[]{:S(2)}, u32[]{:S(2)}) collective-permute-start(bf16[512,768]{1,0:T(8,128)(2,1)} %bitcast.103), channel_id=1, source_target_pairs={{0,1},{1,0},{2,3},{3,2},{4,5},{5,4},{6,7},{7,6},{8,9},{9,8},{10,11... | collective-permute-start | bytes 2359304 | tf_op jit(solution)/shard_map/ppermute | solution.py:10
  115.0 5.3 %copy-start.3 = (bf16[512,768]{1,0:T(8,128)(2,1)S(1)}, bf16[512,768]{1,0:T(8,128)(2,1)}, u32[]{:S(2)}) copy-start(bf16[512,768]{1,0:T(8,128)(2,1)} %param.11) | copy-start | bytes 2359300
  115.0 81.4 %all-to-all-start.1 = ((bf16[128,32,768]{2,1,0:T(8,128)(2,1)}), bf16[128,32,768]{2,1,0:T(8,128)(2,1)}, u32[]{:S(2)}, u32[]{:S(2)}) async-start(bf16[128,32,768]{2,1,0:T(8,128)(2,1)} %bitcast.74), calls=%async_computation.1 | async-start | bytes 12582912 | tf_op jit(solution)/shard_map/all_to_all | solution.py:101
  120.3 9.1 %collective-permute-start = (bf16[512,768]{1,0:T(8,128)(2,1)S(1)}, bf16[512,768]{1,0:T(8,128)(2,1)S(1)}, u32[]{:S(2)}, u32[]{:S(2)}) collective-permute-start(bf16[512,768]{1,0:T(8,128)(2,1)S(1)} %copy-done.3), channel_id=1, source_target_pairs={{0,1},{1,0},{2,3},{3,2},{4,5},{5,4},{6,7},{7,6},{8,9},{9,8},{10,11... | collective-permute-start | bytes 2359304 | tf_op jit(solution)/shard_map/ppermute | solution.py:10
  123.6 16.3 %collective-permute-start.1 = (bf16[768,320]{0,1:T(8,128)(2,1)}, bf16[768,320]{0,1:T(8,128)(2,1)}, u32[]{:S(2)}, u32[]{:S(2)}) collective-permute-start(bf16[768,320]{0,1:T(8,128)(2,1)} %pad_maximum_fusion.4), channel_id=1, source_target_pairs={{0,1},{1,0},{2,3},{3,2},{4,5},{5,4},{6,7},{7,6},{8,9},{9,8},{10,11... | collective-permute-start | bytes 1474568 | tf_op jit(solution)/shard_map/ppermute | solution.py:10
  125.3 3.4 %copy-start.24 = (s32[4,1]{0,1:T(1,128)S(1)}, s32[4,1]{0,1:T(1,128)}, u32[]{:S(2)}) copy-start(s32[4,1]{0,1:T(1,128)} %reduce-window.8) | copy-start | bytes 52
  125.3 3.5 %copy-start.23 = (s32[1,4]{1,0:T(1,128)S(1)}, s32[1,4]{1,0:T(1,128)}, u32[]{:S(2)}) copy-start(s32[1,4]{1,0:T(1,128)} %param.20) | copy-start | bytes 52
  139.5 2.1 %copy-start.5 = (bf16[512,768]{1,0:T(8,128)(2,1)S(1)}, bf16[512,768]{1,0:T(8,128)(2,1)}, u32[]{:S(2)}) copy-start(bf16[512,768]{1,0:T(8,128)(2,1)} %copy-done.4) | copy-start | bytes 2359300
  139.5 2.1 %copy-start.7 = (bf16[512,768]{1,0:T(8,128)(2,1)S(1)}, bf16[512,768]{1,0:T(8,128)(2,1)}, u32[]{:S(2)}) copy-start(bf16[512,768]{1,0:T(8,128)(2,1)} %copy-done.6) | copy-start | bytes 2359300
  139.7 5.5 %collective-permute-start.2 = (bf16[512,768]{1,0:T(8,128)(2,1)S(1)}, bf16[512,768]{1,0:T(8,128)(2,1)S(1)}, u32[]{:S(2)}, u32[]{:S(2)}) collective-permute-start(bf16[512,768]{1,0:T(8,128)(2,1)S(1)} %select_bitcast_fusion.2), channel_id=1, source_target_pairs={{0,1},{1,0},{2,3},{3,2},{4,5},{5,4},{6,7},{7,6},{8,9},{9,8},{10,11... | collective-permute-start | bytes 2359304 | tf_op jit(solution)/shard_map/ppermute | solution.py:10
  142.8 2.4 %copy-start.22 = (s32[512]{0:T(512)S(1)}, s32[512]{0:T(512)}, u32[]{:S(2)}) copy-start(s32[512]{0:T(512)} %select_reduce_fusion) | copy-start | bytes 6148
  142.8 2.4 %copy-start.26 = (bf16[256,768]{1,0:T(8,128)(2,1)S(1)}, bf16[256,768]{1,0:T(8,128)(2,1)}, u32[]{:S(2)}) copy-start(bf16[256,768]{1,0:T(8,128)(2,1)} %param.14) | copy-start | bytes 1179652
  142.8 2.4 %copy-start.27 = (s32[256]{0:T(256)S(1)}, s32[256]{0:T(256)}, u32[]{:S(2)}) copy-start(s32[256]{0:T(256)} %and_select_fusion) | copy-start | bytes 3076
  (11 other events, 12.3 us)

commit v10 on v9

--- a/solution.py
+++ b/solution.py
@@ -1,6 +1,7 @@
 import jax
 import jax.numpy as jnp
 from jax import lax
+from jax.experimental.layout import Layout, with_layout_constraint
 from jax.sharding import PartitionSpec as P
 
 RANK = 16
@@ -148,9 +149,8 @@
         gate[:, :, None], (tok_rows, expert_count, rows_per_expert)
     ).reshape(tok_rows, chunk_count * pad_rows)
     weights = jnp.where(rank_cols == row_slot[None, :], gate_cols, 0.0)
-    weights, base = lax.optimization_barrier(
-        (weights.astype(jnp.bfloat16), shared_out + 0.5 * delta)
-    )
+    weights = with_layout_constraint(weights.astype(jnp.bfloat16), Layout(major_to_minor=(0, 1)))
+    weights, base = lax.optimization_barrier((weights, shared_out + 0.5 * delta))
     back = returned.reshape(chunk_count * pad_rows, feat_local)
     routed = jnp.dot(weights, back, preferred_element_type=jnp.float32)
     return (base + routed).astype(jnp.bfloat16)

time: 205 us -> 205 us (level)
  waiting for transfers between devices: 123 us -> 90 us
  local copies, waits for them, and re-layouts: 11.5 us -> 33.2 us
  other arithmetic: 18.9 us -> 28.8 us
    all_to_all x1, waiting for transfers between devices: 50.5 us -> 17.8 us  [body(): lax.all_to_all(expert_out.reshape(req_count * blk_count, pad_rows, feat_l...]
    reshape x0 -> x2, local copies, waits for them, and re-layouts: none -> 15.4 us  [the longest x1 8.97 us: body(): rank_cols = jnp.broadcast_to(rank[:, :, None], (tok_rows, expert_count, r...]
    broadcast_in_dim x0 -> x2, local copies, waits for them, and re-layouts: none -> 6.65 us  [the longest x1 4.32 us: body(): jnp.broadcast_to(rank[:, :, None], (tok_rows, expert_count, rows_per_expe...]
    convert_element_type x1, other arithmetic: 2.38 us -> 8.19 us  [body(): weights.astype(jnp.bfloat16)]
    reshape x1, local copies, waits for them, and re-layouts: 3.63 us -> 0.4 us  [body(): shared_terms.astype(jnp.bfloat16).reshape(tok_rows, blk_count, feat_local)]
    unnamed x57 -> x69, local copies, waits for them, and re-layouts: 3.48 us -> 6.4 us
    dot_general x1, matrix products: 0.62 us -> 2.93 us  [body(): delta = jnp.dot(low, adapter_up, preferred_element_type=jnp.float32)]
  transfers between devices with their start and end apart: 7 -> 7, of which waited for: 3 -> 3; matrix products, arithmetic and copies ran while one was open for 19% -> 34% of each run, Pallas kernels for 0% -> 0%
where the time goes in v10:
time: 205 us
  waiting for transfers between devices  90 us (44%)
  matrix products  34.3 us (17%)
  local copies, waits for them, and re-layouts  33.2 us (16%)
  other arithmetic  28.8 us (14%)
  starting transfers between devices  17.7 us (9%)
    all_to_all x1, waiting for transfers between devices, body(): lax.all_to_all(send_rows.reshape(chunk_count, pad_rows, feat_local), both...  69.2 us
    all_to_all x1, waiting for transfers between devices, body(): lax.all_to_all(expert_out.reshape(req_count * blk_count, pad_rows, feat_l...  17.8 us
    all_to_all x1, starting transfers between devices, body(): lax.all_to_all(send_rows.reshape(chunk_count, pad_rows, feat_local), both...  10.9 us
    dot_general x1, matrix products, body(): jnp.einsum('gcsd,cdf->gsf', rows_in, weight_gate_up, preferred_element_ty...  9.69 us
    reshape x1, local copies, waits for them, and re-layouts, body(): rank_cols = jnp.broadcast_to(rank[:, :, None], (tok_rows, expert_count, r...  8.97 us
    convert_element_type x1, other arithmetic, body(): weights.astype(jnp.bfloat16)  8.19 us
    dot_general x1, matrix products, body(): routed = jnp.dot(weights, back, preferred_element_type=jnp.float32)  7.19 us
    reshape x1, local copies, waits for them, and re-layouts, body(): gate_cols = jnp.broadcast_to(gate[:, :, None], (tok_rows, expert_count, r...  6.43 us
  transfers between devices with their start and end apart: 7, of which 3 were waited for; matrix products, arithmetic and copies ran while one was open for 34% of the time, Pallas kernels for 0%

profile of v10, /device:TPU:2, one launch (start us, length us, event | category | flops | bytes accessed | tf_op | source)
XLA Modules:
  0.0 204.6 jit_solution(7221351077879819147)
XLA Ops:
  3.3 5.3 %convolution_convert_fusion = bf16[4096,768]{1,0:T(8,128)(2,1)} fusion(pred[4096,512]{1,0:T(32,128)(4,1)S(1)} %bitcast_compare_fusion, bf16[512,768]{1,0:T(8,128)(2,1)S(1)} %copy-done.7), kind=kOutput, calls=%fused_computation.2 | convolution fusion | flops 3224371200 | bytes 9175040 | tf_op jit(solution)/shard_map/dot_general | solution.py:68
  8.7 10.9 %all-to-all-start = ((bf16[128,32,768]{2,1,0:T(8,128)(2,1)}), bf16[128,32,768]{2,1,0:T(8,128)(2,1)}, u32[]{:S(2)}, u32[]{:S(2)}) async-start(bf16[128,32,768]{2,1,0:T(8,128)(2,1)} %bitcast.71), calls=%async_computation | async-start | bytes 12582912 | tf_op jit(solution)/shard_map/all_to_all | solution.py:72
  20.2 3.0 %collective-permute-done.3 = bf16[768,1024]{1,0:T(8,128)(2,1)} collective-permute-done((bf16[768,1024]{1,0:T(8,128)(2,1)S(1)}, bf16[768,1024]{1,0:T(8,128)(2,1)}, u32[]{:S(2)}, u32[]{:S(2)}) %collective-permute-start.3) | collective-permute-done | bytes 1572896 | tf_op jit(solution)/shard_map/ppermute | solution.py:11
  23.3 3.2 %select_bitcast_fusion.1 = (bf16[1,768,1024]{2,1,0:T(8,128)(2,1)}, bf16[1,768,1024]{2,1,0:T(8,128)(2,1)}) fusion(bf16[768,1024]{1,0:T(8,128)(2,1)} %collective-permute-done.3, pred[]{:T(512)S(6)} %eq.216, bf16[1,768,1024]{2,1,0:T(8,128)(2,1)S(1)} %copy-done.5), kind=kLoop, calls=%fused_computation.16 | loop fusion | flops 1572864 | bytes 6291457 | tf_op jit(solution)/shard_map/stack | solution.py:20
  26.5 69.2 %all-to-all-done = bf16[128,32,768]{2,1,0:T(8,128)(2,1)} async-done(((bf16[128,32,768]{2,1,0:T(8,128)(2,1)}), bf16[128,32,768]{2,1,0:T(8,128)(2,1)}, u32[]{:S(2)}, u32[]{:S(2)}) %all-to-all-start) | async-done | bytes 6291488 | tf_op jit(solution)/shard_map/all_to_all | solution.py:72
  95.7 9.7 %convolution_bitcast_fusion = f32[64,32,1024]{2,1,0:T(8,128)S(1)} fusion(bf16[64,2,32,768]{3,2,1,0:T(8,128)(2,1)} %bitcast.16, bf16[1,768,1024]{2,1,0:T(8,128)(2,1)} %get-tuple-element.16, bf16[1,768,1024]{2,1,0:T(8,128)(2,1)} %get-tuple-element.15), kind=kOutput, calls=%fused_computation.8 | convolution fusion | flops 6444023808 | bytes 17825792 | tf_op jit(solution)/shard_map/gcsd,cdf->gsf/dot_general | solution.py:82
  105.4 1.5 fusion
  106.9 1.8 convolution_convert_fusion.2
  108.8 3.0 %convolution_convert_fusion.1 = bf16[2048,768]{1,0:T(8,128)(2,1)S(1)} fusion(bf16[2048,512]{1,0:T(8,128)(2,1)S(1)} %bitcast.77, bf16[512,768]{1,0:T(8,128)(2,1)} %collective-permute-done.4, pred[]{:T(512)S(6)} %eq.216, bf16[1,512,768]{2,1,0:T(8,128)(2,1)S(1)} %copy-done.31), kind=kOutput, calls=%fused_computation.6 | convolution fusion | flops 1612578816 | bytes 6815745 | tf_op jit(solution)/shard_map/dot_general | solution.py:95
  111.7 3.2 %pad_maximum_fusion = bf16[64,2,32,768]{3,2,1,0:T(8,128)(2,1)} fusion(bf16[64,1,32,768]{3,2,1,0:T(8,128)(2,1)S(1)} %bitcast.75, bf16[64,1,32,768]{3,2,1,0:T(8,128)(2,1)S(1)} %bitcast.74), kind=kLoop, calls=%fused_computation.3 | loop fusion | flops 3145728 | bytes 12582912 | tf_op jit(solution)/shard_map/stack | solution.py:93
  114.9 5.3 %all-to-all-start.1 = ((bf16[128,32,768]{2,1,0:T(8,128)(2,1)}), bf16[128,32,768]{2,1,0:T(8,128)(2,1)}, u32[]{:S(2)}, u32[]{:S(2)}) async-start(bf16[128,32,768]{2,1,0:T(8,128)(2,1)} %bitcast.69), calls=%async_computation.1 | async-start | bytes 12582912 | tf_op jit(solution)/shard_map/all_to_all | solution.py:102
  121.8 1.7 pad_maximum_fusion.4
  123.9 4.4 %copy.41 = bf16[192,8,2,512]{3,1,2,0:T(8,128)(2,1)} copy(bf16[192,8,2,512]{3,2,1,0:T(2,128)(2,1)} %bitcast.72) | data formatting | bytes 6291456
  132.2 2.3 %broadcast_select_fusion.3 = (bf16[768,320]{0,1:T(8,128)(2,1)}, bf16[768,320]{0,1:T(8,128)(2,1)}) fusion(bf16[768,320]{0,1:T(8,128)(2,1)} %collective-permute-done.1, pred[]{:T(512)S(6)} %eq.216, bf16[768,256]{0,1:T(8,128)(2,1)S(1)} %copy.32, bf16[768,64]{0,1:T(8,128)(2,1)} %param.12), kind=kLoop, calls=%fused_computation.40 | loop fusion | flops 1474560 | bytes 1966081 | tf_op jit(solution)/shard_map/jit(_where)/select_n | solution.py:17
  134.6 1.8 fusion.5
  137.9 2.2 %fusion.58 = (bf16[512,1,768]{2,1,0:T(2,128)(2,1)S(1)}, bf16[512,1,768]{2,1,0:T(2,128)(2,1)S(1)}) fusion(bf16[512,2,768]{2,1,0:T(2,128)(2,1)S(1)} %reshape.151), kind=kLoop, calls=%fused_computation.111 | loop fusion | bytes 3145728 | tf_op jit(solution)/shard_map/slice | solution.py:138
  144.3 4.3 %broadcast_in_dim.39 = s32[512,64,64]{0,2,1:T(8,128)} broadcast(s32[512,64]{0,1:T(8,128)S(1)} %get-tuple-element.29), dimensions={0,1} | broadcast | bytes 8519680 | tf_op jit(solution)/shard_map/broadcast_in_dim | solution.py:145
  148.6 9.0 %copy.31 = s32[512,4096]{1,0:T(8,128)} copy(s32[512,4096]{0,1:T(8,128)} %bitcast.68) | data formatting | bytes 16777216 | tf_op jit(solution)/shard_map/reshape | solution.py:147
  158.6 2.3 %broadcast_in_dim.43 = bf16[512,64,64]{0,2,1:T(8,128)(2,1)} broadcast(bf16[512,64]{0,1:T(8,128)(2,1)S(1)} %broadcast_divide_fusion), dimensions={0,1} | broadcast | bytes 4259840 | tf_op jit(solution)/shard_map/broadcast_in_dim | solution.py:148
  160.9 6.4 %copy.33 = bf16[512,4096]{1,0:T(8,128)(2,1)} copy(bf16[512,4096]{0,1:T(8,128)(2,1)} %bitcast.70) | data formatting | bytes 8388608 | tf_op jit(solution)/shard_map/reshape | solution.py:150
  167.4 8.2 %select_convert_fusion = bf16[512,4096]{1,0:T(8,128)(2,1)} fusion(bf16[512,4096]{1,0:T(8,128)(2,1)} %copy.33, s32[512,4096]{1,0:T(8,128)} %copy.31, s32[4096]{0:T(1024)S(1)} %fusion.47), kind=kLoop, calls=%fused_computation.1 | loop fusion | flops 4194304 | bytes 16793600 | tf_op jit(solution)/shard_map/convert_element_type | solution.py:152
  175.6 2.9 %multiply_add_fusion = f32[512,768]{1,0:T(8,128)} fusion(bf16[512,768]{1,0:T(8,128)(2,1)} %collective-permute-done.2, pred[]{:T(512)S(6)} %eq.216, bf16[512,1,768]{2,1,0:T(2,128)(2,1)S(1)} %copy-done.3, bf16[512,1,768]{2,1,0:T(2,128)(2,1)S(1)} %get-tuple-element.17, bf16[256,768]{1,0:T(8,128)(2,1)S(1)} %copy-done.32, f32[512,320]{0,1:T(8,128)S(1)} %copy-done.17, ...), kind=kOutput, calls=%fused_computation.17 | convolution fusion | flops 203554816 | bytes 6163457 | tf_op jit(solution)/shard_map/dot_general | solution.py:128
  178.5 17.8 %all-to-all-done.1 = bf16[128,32,768]{2,1,0:T(8,128)(2,1)} async-done(((bf16[128,32,768]{2,1,0:T(8,128)(2,1)}), bf16[128,32,768]{2,1,0:T(8,128)(2,1)}, u32[]{:S(2)}, u32[]{:S(2)}) %all-to-all-start.1) | async-done | bytes 6291488 | tf_op jit(solution)/shard_map/all_to_all | solution.py:102
  196.3 7.2 %fusion.60 = f32[512,768]{1,0:T(8,128)S(1)} fusion(bf16[512,4096]{1,0:T(8,128)(2,1)} %select_convert_fusion, bf16[4096,768]{1,0:T(8,128)(2,1)} %bitcast.30), kind=kOutput, calls=%fused_computation.113 | convolution fusion | flops 3221225472 | bytes 12058624 | tf_op jit(solution)/shard_map/dot_general | solution.py:155
  (94 shorter events, 17.3 us)
Async XLA Ops:
  0.0 136.5 %copy-start = (bf16[512,1536]{1,0:T(8,128)(2,1)S(1)}, bf16[512,1536]{1,0:T(8,128)(2,1)}, u32[]{:S(2)}) copy-start(bf16[512,1536]{1,0:T(8,128)(2,1)} %param.16) | copy-start | bytes 4718596
  0.0 3.3 %copy-start.7 = (bf16[512,768]{1,0:T(8,128)(2,1)S(1)}, bf16[512,768]{1,0:T(8,128)(2,1)}, u32[]{:S(2)}) copy-start(bf16[512,768]{1,0:T(8,128)(2,1)} %param.11) | copy-start | bytes 2359300
  1.0 7.6 %copy-start.18 = (s32[512,1]{0,1:T(1,128)}, s32[512,1]{0,1:T(1,128)S(1)}, u32[]{:S(2)}) copy-start(s32[512,1]{0,1:T(1,128)S(1)} %get-tuple-element.23) | copy-start | bytes 6148
  1.0 7.6 %copy-start.20 = (s32[512,1]{0,1:T(1,128)}, s32[512,1]{0,1:T(1,128)S(1)}, u32[]{:S(2)}) copy-start(s32[512,1]{0,1:T(1,128)S(1)} %get-tuple-element.24) | copy-start | bytes 6148
  1.0 7.6 %copy-start.22 = (s32[512,1]{0,1:T(1,128)}, s32[512,1]{0,1:T(1,128)S(1)}, u32[]{:S(2)}) copy-start(s32[512,1]{0,1:T(1,128)S(1)} %get-tuple-element.25) | copy-start | bytes 6148
  1.0 7.6 %copy-start.24 = (s32[512,1]{0,1:T(1,128)}, s32[512,1]{0,1:T(1,128)S(1)}, u32[]{:S(2)}) copy-start(s32[512,1]{0,1:T(1,128)S(1)} %get-tuple-element.26) | copy-start | bytes 6148
  1.0 7.6 %copy-start.26 = (s32[512,1]{0,1:T(1,128)}, s32[512,1]{0,1:T(1,128)S(1)}, u32[]{:S(2)}) copy-start(s32[512,1]{0,1:T(1,128)S(1)} %get-tuple-element.27) | copy-start | bytes 6148
  1.0 7.6 %copy-start.28 = (s32[512,1]{0,1:T(1,128)}, s32[512,1]{0,1:T(1,128)S(1)}, u32[]{:S(2)}) copy-start(s32[512,1]{0,1:T(1,128)S(1)} %get-tuple-element.28) | copy-start | bytes 6148
  8.7 11.0 %copy-start.5 = (bf16[1,768,1024]{2,1,0:T(8,128)(2,1)S(1)}, bf16[1,768,1024]{2,1,0:T(8,128)(2,1)}, u32[]{:S(2)}) copy-start(bf16[1,768,1024]{2,1,0:T(8,128)(2,1)} %param.17) | copy-start | bytes 4718596
  8.7 87.0 %all-to-all-start = ((bf16[128,32,768]{2,1,0:T(8,128)(2,1)}), bf16[128,32,768]{2,1,0:T(8,128)(2,1)}, u32[]{:S(2)}, u32[]{:S(2)}) async-start(bf16[128,32,768]{2,1,0:T(8,128)(2,1)} %bitcast.71), calls=%async_computation | async-start | bytes 12582912 | tf_op jit(solution)/shard_map/all_to_all | solution.py:72
  19.6 3.6 %collective-permute-start.3 = (bf16[768,1024]{1,0:T(8,128)(2,1)S(1)}, bf16[768,1024]{1,0:T(8,128)(2,1)}, u32[]{:S(2)}, u32[]{:S(2)}) collective-permute-start(bf16[768,1024]{1,0:T(8,128)(2,1)S(1)} %bitcast.78), channel_id=1, source_target_pairs={{0,1},{1,0},{2,3},{3,2},{4,5},{5,4},{6,7},{7,6},{8,9},{9,8},{10,11... | collective-permute-start | bytes 4718600 | tf_op jit(solution)/shard_map/ppermute | solution.py:11
  19.8 87.1 %collective-permute-start.4 = (bf16[512,768]{1,0:T(8,128)(2,1)}, bf16[512,768]{1,0:T(8,128)(2,1)}, u32[]{:S(2)}, u32[]{:S(2)}) collective-permute-start(bf16[512,768]{1,0:T(8,128)(2,1)} %bitcast.99), channel_id=1, source_target_pairs={{0,1},{1,0},{2,3},{3,2},{4,5},{5,4},{6,7},{7,6},{8,9},{9,8},{10,11... | collective-permute-start | bytes 2359304 | tf_op jit(solution)/shard_map/ppermute | solution.py:11
  114.9 5.3 %copy-start.8 = (bf16[512,768]{1,0:T(8,128)(2,1)S(1)}, bf16[512,768]{1,0:T(8,128)(2,1)}, u32[]{:S(2)}) copy-start(bf16[512,768]{1,0:T(8,128)(2,1)} %param.11) | copy-start | bytes 2359300
  114.9 81.4 %all-to-all-start.1 = ((bf16[128,32,768]{2,1,0:T(8,128)(2,1)}), bf16[128,32,768]{2,1,0:T(8,128)(2,1)}, u32[]{:S(2)}, u32[]{:S(2)}) async-start(bf16[128,32,768]{2,1,0:T(8,128)(2,1)} %bitcast.69), calls=%async_computation.1 | async-start | bytes 12582912 | tf_op jit(solution)/shard_map/all_to_all | solution.py:102
  120.2 14.3 %collective-permute-start = (bf16[512,768]{1,0:T(8,128)(2,1)S(1)}, bf16[512,768]{1,0:T(8,128)(2,1)S(1)}, u32[]{:S(2)}, u32[]{:S(2)}) collective-permute-start(bf16[512,768]{1,0:T(8,128)(2,1)S(1)} %copy-done.8), channel_id=1, source_target_pairs={{0,1},{1,0},{2,3},{3,2},{4,5},{5,4},{6,7},{7,6},{8,9},{9,8},{10,11... | collective-permute-start | bytes 2359304 | tf_op jit(solution)/shard_map/ppermute | solution.py:11
  123.5 8.7 %collective-permute-start.1 = (bf16[768,320]{0,1:T(8,128)(2,1)}, bf16[768,320]{0,1:T(8,128)(2,1)}, u32[]{:S(2)}, u32[]{:S(2)}) collective-permute-start(bf16[768,320]{0,1:T(8,128)(2,1)} %pad_maximum_fusion.4), channel_id=1, source_target_pairs={{0,1},{1,0},{2,3},{3,2},{4,5},{5,4},{6,7},{7,6},{8,9},{9,8},{10,11... | collective-permute-start | bytes 1474568 | tf_op jit(solution)/shard_map/ppermute | solution.py:11
  141.3 34.3 %collective-permute-start.2 = (bf16[512,768]{1,0:T(8,128)(2,1)}, bf16[512,768]{1,0:T(8,128)(2,1)}, u32[]{:S(2)}, u32[]{:S(2)}) collective-permute-start(bf16[512,768]{1,0:T(8,128)(2,1)} %select_bitcast_fusion.2), channel_id=1, source_target_pairs={{0,1},{1,0},{2,3},{3,2},{4,5},{5,4},{6,7},{7,6},{8,9},{9,8},{10,11... | collective-permute-start | bytes 2359304 | tf_op jit(solution)/shard_map/ppermute | solution.py:11
  167.3 8.2 %copy-start.3 = (bf16[512,1,768]{2,1,0:T(2,128)(2,1)S(1)}, bf16[512,1,768]{2,1,0:T(2,128)(2,1)}, u32[]{:S(2)}) copy-start(bf16[512,1,768]{2,1,0:T(2,128)(2,1)} %copy-done.2) | copy-start | bytes 2359300
  167.3 8.2 %copy-start.17 = (f32[512,320]{0,1:T(8,128)S(1)}, f32[512,320]{0,1:T(8,128)}, u32[]{:S(2)}) copy-start(f32[512,320]{0,1:T(8,128)} %copy-done.16) | copy-start | bytes 1966084
  167.3 8.2 %copy-start.30 = (s32[512]{0:T(512)S(1)}, s32[512]{0:T(512)}, u32[]{:S(2)}) copy-start(s32[512]{0:T(512)} %select_reduce_fusion) | copy-start | bytes 6148
  167.3 8.2 %copy-start.32 = (bf16[256,768]{1,0:T(8,128)(2,1)S(1)}, bf16[256,768]{1,0:T(8,128)(2,1)}, u32[]{:S(2)}) copy-start(bf16[256,768]{1,0:T(8,128)(2,1)} %param.14) | copy-start | bytes 1179652
  167.3 8.2 %copy-start.33 = (s32[256]{0:T(256)S(1)}, s32[256]{0:T(256)}, u32[]{:S(2)}) copy-start(s32[256]{0:T(256)} %and_select_fusion) | copy-start | bytes 3076
  196.3 7.2 %copy-start.6 = (f32[512,768]{1,0:T(8,128)S(1)}, f32[512,768]{1,0:T(8,128)}, u32[]{:S(2)}) copy-start(f32[512,768]{1,0:T(8,128)} %multiply_add_fusion) | copy-start | bytes 4718596
  196.3 8.2 %copy-start.1 = (bf16[512,1536]{1,0:T(8,128)(2,1)S(1)}, bf16[512,1536]{1,0:T(8,128)(2,1)}, u32[]{:S(2)}) copy-start(bf16[512,1536]{1,0:T(8,128)(2,1)} %param.16) | copy-start | bytes 4718596
  (17 other events, 26.8 us)

commit v11 on v9

--- a/solution.py
+++ b/solution.py
@@ -78,12 +78,15 @@
     rows_in = received.reshape(req_count, blk_count, pad_rows, feat_local)
 
     weight_gate_up = gather_blk(expert_gate_up[0], 0, stack=True)
-    gate_up = jnp.einsum(
-        "gcsd,cdf->gsf",
-        rows_in,
-        weight_gate_up,
-        preferred_element_type=jnp.float32,
-    )
+    rows_flat = rows_in.reshape(req_count, blk_count * pad_rows, feat_local)
+    gate_up = sum(
+        jnp.dot(
+            rows_flat[:, c * pad_rows : (c + 1) * pad_rows].reshape(req_count * pad_rows, feat_local),
+            weight_gate_up[c],
+            preferred_element_type=jnp.float32,
+        )
+        for c in range(blk_count)
+    ).reshape(req_count, pad_rows, 2 * hidden_width)
     hidden = (jax.nn.silu(gate_up[..., :hidden_width]) * gate_up[..., hidden_width:]).astype(
         jnp.bfloat16
     )

time: 205 us -> 207 us (level)
  local copies, waits for them, and re-layouts: 11.5 us -> 16.6 us
    all_to_all x1, waiting for transfers between devices: 69.2 us -> 75.5 us  [body(): lax.all_to_all(send_rows.reshape(chunk_count, pad_rows, feat_local), both...]
    slice x0 -> x1, local copies, waits for them, and re-layouts: none -> 3.48 us  [body(): rows_flat[:, c * pad_rows:(c + 1) * pad_rows]]
    another operation x2 -> x1, other arithmetic: 4.59 us -> 1.33 us  [the longest x1 3.26 us: gather_blk(): return jnp.stack([first, second], axis=axis)]
    all_to_all x1, waiting for transfers between devices: 50.5 us -> 47.3 us  [body(): lax.all_to_all(expert_out.reshape(req_count * blk_count, pad_rows, feat_l...]
    ppermute x5, waiting for transfers between devices: 3.04 us -> 0.01 us  [partner(): return lax.ppermute(x, 'blk', [(0, 1), (1, 0)])]
    unnamed x57 -> x53, local copies, waits for them, and re-layouts: 3.48 us -> 5.11 us
    dot_general x1 -> x2, matrix products: 9.69 us -> 8.3 us  [body(): jnp.dot(rows_flat[:, c * pad_rows:(c + 1) * pad_rows].reshape(req_count *...]
  transfers between devices with their start and end apart: 7 -> 7, of which waited for: 3 -> 2; matrix products, arithmetic and copies ran while one was open for 19% -> 19% of each run, Pallas kernels for 0% -> 0%
where the time goes in v11:
time: 207 us; the launch traced here: 206 us
  waiting for transfers between devices  123 us (59%)
  matrix products  31.7 us (15%)
  starting transfers between devices  17.8 us (9%)
  other arithmetic  17.1 us (8%)
  local copies, waits for them, and re-layouts  16.6 us (8%)
    all_to_all x1, waiting for transfers between devices, body(): lax.all_to_all(send_rows.reshape(chunk_count, pad_rows, feat_local), both...  75.5 us
    all_to_all x1, waiting for transfers between devices, body(): lax.all_to_all(expert_out.reshape(req_count * blk_count, pad_rows, feat_l...  47.3 us
    all_to_all x1, starting transfers between devices, body(): lax.all_to_all(send_rows.reshape(chunk_count, pad_rows, feat_local), both...  10.9 us
    dot_general x2, matrix products, body(): jnp.dot(rows_flat[:, c * pad_rows:(c + 1) * pad_rows].reshape(req_count *...  8.3 us
    dot_general x1, matrix products, body(): routed = jnp.dot(weights, back, preferred_element_type=jnp.float32)  7.09 us
    dot_general x1, matrix products, body(): jnp.dot(pick.astype(jnp.bfloat16), normed, preferred_element_type=jnp.flo...  5.3 us
    all_to_all x1, starting transfers between devices, body(): lax.all_to_all(expert_out.reshape(req_count * blk_count, pad_rows, feat_l...  5.28 us
    unnamed x53, local copies, waits for them, and re-layouts  5.11 us
  transfers between devices with their start and end apart: 7, of which 2 were waited for; matrix products, arithmetic and copies ran while one was open for 19% of the time, Pallas kernels for 0%

profile of v11, /device:TPU:2, one launch (start us, length us, event | category | flops | bytes accessed | tf_op | source)
XLA Modules:
  0.0 206.4 jit_solution(7177875011335151297)
XLA Ops:
  2.0 1.3 bitcast_compare_fusion
  3.3 5.3 %convolution_convert_fusion = bf16[4096,768]{1,0:T(8,128)(2,1)} fusion(pred[4096,512]{1,0:T(32,128)(4,1)S(1)} %bitcast_compare_fusion, bf16[512,768]{1,0:T(8,128)(2,1)S(1)} %copy-done.2), kind=kOutput, calls=%fused_computation.4 | convolution fusion | flops 3224371200 | bytes 9175040 | tf_op jit(solution)/shard_map/dot_general | solution.py:67
  8.7 10.9 %all-to-all-start = ((bf16[128,32,768]{2,1,0:T(8,128)(2,1)}), bf16[128,32,768]{2,1,0:T(8,128)(2,1)}, u32[]{:S(2)}, u32[]{:S(2)}) async-start(bf16[128,32,768]{2,1,0:T(8,128)(2,1)} %bitcast.76), calls=%async_computation | async-start | bytes 12582912 | tf_op jit(solution)/shard_map/all_to_all | solution.py:71
  20.2 75.5 %all-to-all-done = bf16[128,32,768]{2,1,0:T(8,128)(2,1)} async-done(((bf16[128,32,768]{2,1,0:T(8,128)(2,1)}), bf16[128,32,768]{2,1,0:T(8,128)(2,1)}, u32[]{:S(2)}, u32[]{:S(2)}) %all-to-all-start) | async-done | bytes 6291488 | tf_op jit(solution)/shard_map/all_to_all | solution.py:71
  95.7 3.5 %fusion.63 = (bf16[64,32,768]{2,1,0:T(8,128)(2,1)S(1)}, bf16[64,32,768]{2,1,0:T(8,128)(2,1)S(1)}) fusion(bf16[64,64,768]{2,1,0:T(8,128)(2,1)} %bitcast.16), kind=kLoop, calls=%fused_computation.114 | loop fusion | bytes 12582912 | tf_op jit(solution)/shard_map/slice | solution.py:84
  99.2 4.8 %fusion.2 = f32[2048,1024]{1,0:T(8,128)S(1)} fusion(bf16[2048,768]{1,0:T(8,128)(2,1)S(1)} %bitcast.80, bf16[768,1024]{1,0:T(8,128)(2,1)} %collective-permute-done.3, pred[]{:T(512)S(6)} %eq.216, bf16[1,768,1024]{2,1,0:T(8,128)(2,1)S(1)} %copy-done.22), kind=kOutput, calls=%fused_computation.14 | convolution fusion | flops 3222011904 | bytes 14680065 | tf_op jit(solution)/shard_map/dot_general | solution.py:83
  104.1 3.4 %convolution_add_fusion = f32[2048,1024]{1,0:T(8,128)S(1)} fusion(f32[2048,1024]{1,0:T(8,128)S(1)} %fusion.2, bf16[2048,768]{1,0:T(8,128)(2,1)S(1)} %bitcast.79, bf16[768,1024]{1,0:T(8,128)(2,1)} %collective-permute-done.3, pred[]{:T(512)S(6)} %eq.216, bf16[1,768,1024]{2,1,0:T(8,128)(2,1)S(1)} %copy-done.22), kind=kOutput, calls=%fused_computation.8 | convolution fusion | flops 3224109056 | bytes 23068672 | tf_op jit(solution)/shard_map/dot_general | solution.py:83
  107.5 1.4 fusion.1
  108.9 2.9 %convolution_convert_fusion.1 = bf16[2048,768]{1,0:T(8,128)(2,1)S(1)} fusion(bf16[2048,512]{1,0:T(8,128)(2,1)S(1)} %bitcast.83, bf16[512,768]{1,0:T(8,128)(2,1)} %collective-permute-done.4, pred[]{:T(512)S(6)} %eq.216, bf16[1,512,768]{2,1,0:T(8,128)(2,1)S(1)} %copy-done.23), kind=kOutput, calls=%fused_computation.9 | convolution fusion | flops 1612578816 | bytes 6815745 | tf_op jit(solution)/shard_map/dot_general | solution.py:97
  111.9 1.8 convolution_convert_fusion.2
  113.7 3.2 %pad_maximum_fusion = bf16[64,2,32,768]{3,2,1,0:T(8,128)(2,1)} fusion(bf16[64,1,32,768]{3,2,1,0:T(8,128)(2,1)S(1)} %bitcast.81, bf16[64,1,32,768]{3,2,1,0:T(8,128)(2,1)S(1)} %bitcast.82), kind=kLoop, calls=%fused_computation.5 | loop fusion | flops 3145728 | bytes 12582912 | tf_op jit(solution)/shard_map/stack | solution.py:95
  116.9 5.3 %all-to-all-start.1 = ((bf16[128,32,768]{2,1,0:T(8,128)(2,1)}), bf16[128,32,768]{2,1,0:T(8,128)(2,1)}, u32[]{:S(2)}, u32[]{:S(2)}) async-start(bf16[128,32,768]{2,1,0:T(8,128)(2,1)} %bitcast.74), calls=%async_computation.1 | async-start | bytes 12582912 | tf_op jit(solution)/shard_map/all_to_all | solution.py:104
  123.8 1.7 pad_maximum_fusion.4
  125.9 4.4 %copy.34 = bf16[192,8,2,512]{3,1,2,0:T(8,128)(2,1)} copy(bf16[192,8,2,512]{3,2,1,0:T(2,128)(2,1)} %bitcast.77) | data formatting | bytes 6291456
  130.3 1.3 reduce-window.8
  133.2 1.3 select_reduce_fusion
  134.7 1.8 fusion.9
  136.5 2.2 %convolution_convert_fusion.3 = bf16[512,1536]{1,0:T(8,128)(2,1)} fusion(bf16[512,1536]{1,0:T(8,128)(2,1)S(1)} %copy-done, f32[512,1024]{1,0:T(8,128)S(1)} %fusion.9), kind=kOutput, calls=%fused_computation.11 | convolution fusion | flops 807665664 | bytes 5242880 | tf_op jit(solution)/shard_map/dot_general | solution.py:137
  138.7 3.6 %reshape.157 = bf16[512,2,768]{2,1,0:T(2,128)(2,1)S(1)} reshape(bf16[512,1536]{1,0:T(8,128)(2,1)} %convolution_convert_fusion.3) | data formatting | bytes 3145728 | tf_op jit(solution)/shard_map/reshape | solution.py:138
  142.3 2.2 %fusion.64 = (bf16[512,1,768]{2,1,0:T(2,128)(2,1)S(1)}, bf16[512,1,768]{2,1,0:T(2,128)(2,1)S(1)}) fusion(bf16[512,2,768]{2,1,0:T(2,128)(2,1)S(1)} %reshape.157), kind=kLoop, calls=%fused_computation.115 | loop fusion | bytes 3145728 | tf_op jit(solution)/shard_map/slice | solution.py:140
  145.4 1.2 broadcast_select_fusion.3
  147.9 2.4 %fusion = bf16[512,4096]{0,1:T(8,128)(2,1)} fusion(bf16[512,64]{0,1:T(8,128)(2,1)S(1)} %broadcast_divide_fusion, s32[4096]{0:T(1024)S(1)} %fusion.51, s32[512,64]{0,1:T(8,128)S(1)} %get-tuple-element.29), kind=kLoop, calls=%fused_computation.1 | loop fusion | flops 4194304 | bytes 4407296 | tf_op jit(solution)/shard_map/convert_element_type | solution.py:155
  150.9 47.3 %all-to-all-done.1 = bf16[128,32,768]{2,1,0:T(8,128)(2,1)} async-done(((bf16[128,32,768]{2,1,0:T(8,128)(2,1)}), bf16[128,32,768]{2,1,0:T(8,128)(2,1)}, u32[]{:S(2)}, u32[]{:S(2)}) %all-to-all-start.1) | async-done | bytes 6291488 | tf_op jit(solution)/shard_map/all_to_all | solution.py:104
  198.3 7.1 %fusion.66 = f32[512,768]{1,0:T(8,128)S(1)} fusion(bf16[512,4096]{0,1:T(8,128)(2,1)} %fusion, bf16[4096,768]{1,0:T(8,128)(2,1)} %bitcast.28), kind=kOutput, calls=%fused_computation.117 | convolution fusion | flops 3221225472 | bytes 12058624 | tf_op jit(solution)/shard_map/dot_general | solution.py:158
  (75 shorter events, 9.9 us)
Async XLA Ops:
  0.0 136.5 %copy-start = (bf16[512,1536]{1,0:T(8,128)(2,1)S(1)}, bf16[512,1536]{1,0:T(8,128)(2,1)}, u32[]{:S(2)}) copy-start(bf16[512,1536]{1,0:T(8,128)(2,1)} %param.16) | copy-start | bytes 4718596
  0.0 3.3 %copy-start.2 = (bf16[512,768]{1,0:T(8,128)(2,1)S(1)}, bf16[512,768]{1,0:T(8,128)(2,1)}, u32[]{:S(2)}) copy-start(bf16[512,768]{1,0:T(8,128)(2,1)} %param.11) | copy-start | bytes 2359300
  1.0 7.7 %copy-start.9 = (s32[512,1]{0,1:T(1,128)}, s32[512,1]{0,1:T(1,128)S(1)}, u32[]{:S(2)}) copy-start(s32[512,1]{0,1:T(1,128)S(1)} %get-tuple-element.23) | copy-start | bytes 6148
  1.0 7.7 %copy-start.11 = (s32[512,1]{0,1:T(1,128)}, s32[512,1]{0,1:T(1,128)S(1)}, u32[]{:S(2)}) copy-start(s32[512,1]{0,1:T(1,128)S(1)} %get-tuple-element.24) | copy-start | bytes 6148
  1.0 7.6 %copy-start.13 = (s32[512,1]{0,1:T(1,128)}, s32[512,1]{0,1:T(1,128)S(1)}, u32[]{:S(2)}) copy-start(s32[512,1]{0,1:T(1,128)S(1)} %get-tuple-element.25) | copy-start | bytes 6148
  1.0 7.6 %copy-start.15 = (s32[512,1]{0,1:T(1,128)}, s32[512,1]{0,1:T(1,128)S(1)}, u32[]{:S(2)}) copy-start(s32[512,1]{0,1:T(1,128)S(1)} %get-tuple-element.26) | copy-start | bytes 6148
  1.0 7.6 %copy-start.17 = (s32[512,1]{0,1:T(1,128)}, s32[512,1]{0,1:T(1,128)S(1)}, u32[]{:S(2)}) copy-start(s32[512,1]{0,1:T(1,128)S(1)} %get-tuple-element.27) | copy-start | bytes 6148
  1.0 7.6 %copy-start.19 = (s32[512,1]{0,1:T(1,128)}, s32[512,1]{0,1:T(1,128)S(1)}, u32[]{:S(2)}) copy-start(s32[512,1]{0,1:T(1,128)S(1)} %get-tuple-element.28) | copy-start | bytes 6148
  8.7 11.2 %copy-start.23 = (bf16[1,512,768]{2,1,0:T(8,128)(2,1)S(1)}, bf16[1,512,768]{2,1,0:T(8,128)(2,1)}, u32[]{:S(2)}) copy-start(bf16[1,512,768]{2,1,0:T(8,128)(2,1)} %param.18) | copy-start | bytes 2359300
  8.7 87.0 %all-to-all-start = ((bf16[128,32,768]{2,1,0:T(8,128)(2,1)}), bf16[128,32,768]{2,1,0:T(8,128)(2,1)}, u32[]{:S(2)}, u32[]{:S(2)}) async-start(bf16[128,32,768]{2,1,0:T(8,128)(2,1)} %bitcast.76), calls=%async_computation | async-start | bytes 12582912 | tf_op jit(solution)/shard_map/all_to_all | solution.py:71
  19.6 79.6 %collective-permute-start.3 = (bf16[768,1024]{1,0:T(8,128)(2,1)}, bf16[768,1024]{1,0:T(8,128)(2,1)}, u32[]{:S(2)}, u32[]{:S(2)}) collective-permute-start(bf16[768,1024]{1,0:T(8,128)(2,1)} %bitcast.105), channel_id=1, source_target_pairs={{0,1},{1,0},{2,3},{3,2},{4,5},{5,4},{6,7},{7,6},{8,9},{9,8},{10,11... | collective-permute-start | bytes 4718600 | tf_op jit(solution)/shard_map/ppermute | solution.py:10
  19.8 89.1 %collective-permute-start.4 = (bf16[512,768]{1,0:T(8,128)(2,1)S(1)}, bf16[512,768]{1,0:T(8,128)(2,1)}, u32[]{:S(2)}, u32[]{:S(2)}) collective-permute-start(bf16[512,768]{1,0:T(8,128)(2,1)S(1)} %bitcast.106), channel_id=1, source_target_pairs={{0,1},{1,0},{2,3},{3,2},{4,5},{5,4},{6,7},{7,6},{8,9},{9,8},{10,11... | collective-permute-start | bytes 2359304 | tf_op jit(solution)/shard_map/ppermute | solution.py:10
  95.7 3.5 %copy-start.22 = (bf16[1,768,1024]{2,1,0:T(8,128)(2,1)S(1)}, bf16[1,768,1024]{2,1,0:T(8,128)(2,1)}, u32[]{:S(2)}) copy-start(bf16[1,768,1024]{2,1,0:T(8,128)(2,1)} %param.17) | copy-start | bytes 4718596
  116.9 81.4 %all-to-all-start.1 = ((bf16[128,32,768]{2,1,0:T(8,128)(2,1)}), bf16[128,32,768]{2,1,0:T(8,128)(2,1)}, u32[]{:S(2)}, u32[]{:S(2)}) async-start(bf16[128,32,768]{2,1,0:T(8,128)(2,1)} %bitcast.74), calls=%async_computation.1 | async-start | bytes 12582912 | tf_op jit(solution)/shard_map/all_to_all | solution.py:104
  122.2 12.3 %collective-permute-start = (bf16[512,768]{1,0:T(8,128)(2,1)S(1)}, bf16[512,768]{1,0:T(8,128)(2,1)S(1)}, u32[]{:S(2)}, u32[]{:S(2)}) collective-permute-start(bf16[512,768]{1,0:T(8,128)(2,1)S(1)} %copy-done.2), channel_id=1, source_target_pairs={{0,1},{1,0},{2,3},{3,2},{4,5},{5,4},{6,7},{7,6},{8,9},{9,8},{10,11... | collective-permute-start | bytes 2359304 | tf_op jit(solution)/shard_map/ppermute | solution.py:10
  125.5 19.5 %collective-permute-start.1 = (bf16[768,320]{0,1:T(8,128)(2,1)}, bf16[768,320]{0,1:T(8,128)(2,1)}, u32[]{:S(2)}, u32[]{:S(2)}) collective-permute-start(bf16[768,320]{0,1:T(8,128)(2,1)} %pad_maximum_fusion.4), channel_id=1, source_target_pairs={{0,1},{1,0},{2,3},{3,2},{4,5},{5,4},{6,7},{7,6},{8,9},{9,8},{10,11... | collective-permute-start | bytes 1474568 | tf_op jit(solution)/shard_map/ppermute | solution.py:10
  131.6 3.0 %copy-start.1 = (bf16[192,8,2,512]{3,1,2,0:T(8,128)(2,1)S(1)}, bf16[192,8,2,512]{3,1,2,0:T(8,128)(2,1)}, u32[]{:S(2)}) copy-start(bf16[192,8,2,512]{3,1,2,0:T(8,128)(2,1)} %copy.34) | copy-start | bytes 9437188
  134.6 1.8 copy-start.3
  144.6 2.1 %copy-start.4 = (bf16[512,768]{1,0:T(8,128)(2,1)S(1)}, bf16[512,768]{1,0:T(8,128)(2,1)}, u32[]{:S(2)}) copy-start(bf16[512,768]{1,0:T(8,128)(2,1)} %copy-done.3) | copy-start | bytes 2359300
  144.6 2.1 %copy-start.6 = (bf16[512,768]{1,0:T(8,128)(2,1)S(1)}, bf16[512,768]{1,0:T(8,128)(2,1)}, u32[]{:S(2)}) copy-start(bf16[512,768]{1,0:T(8,128)(2,1)} %copy-done.5) | copy-start | bytes 2359300
  144.8 5.5 %collective-permute-start.2 = (bf16[512,768]{1,0:T(8,128)(2,1)S(1)}, bf16[512,768]{1,0:T(8,128)(2,1)S(1)}, u32[]{:S(2)}, u32[]{:S(2)}) collective-permute-start(bf16[512,768]{1,0:T(8,128)(2,1)S(1)} %select_bitcast_fusion), channel_id=1, source_target_pairs={{0,1},{1,0},{2,3},{3,2},{4,5},{5,4},{6,7},{7,6},{8,9},{9,8},{10,11... | collective-permute-start | bytes 2359304 | tf_op jit(solution)/shard_map/ppermute | solution.py:10
  147.9 2.4 %copy-start.21 = (s32[512]{0:T(512)S(1)}, s32[512]{0:T(512)}, u32[]{:S(2)}) copy-start(s32[512]{0:T(512)} %select_reduce_fusion) | copy-start | bytes 6148
  147.9 2.4 %copy-start.24 = (bf16[256,768]{1,0:T(8,128)(2,1)S(1)}, bf16[256,768]{1,0:T(8,128)(2,1)}, u32[]{:S(2)}) copy-start(bf16[256,768]{1,0:T(8,128)(2,1)} %param.14) | copy-start | bytes 1179652
  147.9 2.4 %copy-start.25 = (s32[256]{0:T(256)S(1)}, s32[256]{0:T(256)}, u32[]{:S(2)}) copy-start(s32[256]{0:T(256)} %and_select_fusion) | copy-start | bytes 3076
  (9 other events, 8.9 us)

commit v12 on v9

--- a/solution.py
+++ b/solution.py
@@ -62,6 +62,11 @@
     rank_rows = jnp.broadcast_to(
         rank.T[:, None, :], (expert_count, blk_count * pad_rows, tok_rows)
     ).reshape(chunk_count * pad_rows, tok_rows)
+    weight_gate_up = gather_blk(expert_gate_up[0], 0, stack=True)
+    weight_down = gather_blk(expert_down[0], 0, stack=True)
+    weight_gate_up, weight_down, rank_rows = lax.optimization_barrier(
+        (weight_gate_up, weight_down, rank_rows)
+    )
     pick = rank_rows == row_slot[:, None]
 
     send_rows = jnp.dot(
@@ -77,7 +82,7 @@
     )
     rows_in = received.reshape(req_count, blk_count, pad_rows, feat_local)
 
-    weight_gate_up = gather_blk(expert_gate_up[0], 0, stack=True)
+
     gate_up = jnp.einsum(
         "gcsd,cdf->gsf",
         rows_in,
@@ -88,7 +93,6 @@
         jnp.bfloat16
     )
     hidden_rows = hidden.reshape(req_count * pad_rows, hidden_width)
-    weight_down = gather_blk(expert_down[0], 0, stack=True)
     expert_out = jnp.stack(
         [
             jnp.dot(hidden_rows, weight_down[c], preferred_element_type=jnp.float32)

time: 205 us -> 206 us (level)
  blocking collectives: 0 us -> 85.3 us
  waiting for transfers between devices: 123 us -> 52.4 us
  starting transfers between devices: 17.8 us -> 7.64 us
  matrix products: 33.1 us -> 28.7 us
  local copies, waits for them, and re-layouts: 11.5 us -> 15.5 us
  other arithmetic: 18.9 us -> 15.4 us
    all_to_all x0 -> x1, blocking collectives: none -> 85.3 us  [body(): lax.all_to_all(send_rows.reshape(chunk_count, pad_rows, feat_local), both...]
    all_to_all x1 -> x0, waiting for transfers between devices: 69.2 us -> none  [body(): lax.all_to_all(send_rows.reshape(chunk_count, pad_rows, feat_local), both...]
    all_to_all x1 -> x0, starting transfers between devices: 10.9 us -> none  [body(): lax.all_to_all(send_rows.reshape(chunk_count, pad_rows, feat_local), both...]
    unnamed x57 -> x55, local copies, waits for them, and re-layouts: 3.48 us -> 6.4 us
    dot_general x1, matrix products: 9.69 us -> 7.22 us  [body(): jnp.einsum('gcsd,cdf->gsf', rows_in, weight_gate_up, preferred_element_ty...]
  transfers between devices with their start and end apart: 7 -> 6, of which waited for: 3 -> 2; matrix products, arithmetic and copies ran while one was open for 19% -> 14% of each run, Pallas kernels for 0% -> 0%
where the time goes in v12:
time: 206 us; the launch traced here: 205 us
  blocking collectives  85.3 us (41%)
  waiting for transfers between devices  52.4 us (25%)
  matrix products  28.7 us (14%)
  local copies, waits for them, and re-layouts  15.5 us (8%)
  other arithmetic  15.4 us (7%)
  starting transfers between devices  7.64 us (4%)
    all_to_all x1, blocking collectives, body(): lax.all_to_all(send_rows.reshape(chunk_count, pad_rows, feat_local), both...  85.3 us
    all_to_all x1, waiting for transfers between devices, body(): lax.all_to_all(expert_out.reshape(req_count * blk_count, pad_rows, feat_l...  50 us
    dot_general x1, matrix products, body(): jnp.einsum('gcsd,cdf->gsf', rows_in, weight_gate_up, preferred_element_ty...  7.22 us
    dot_general x1, matrix products, body(): routed = jnp.dot(weights, back, preferred_element_type=jnp.float32)  7.09 us
    unnamed x55, local copies, waits for them, and re-layouts  6.4 us
    all_to_all x1, starting transfers between devices, body(): lax.all_to_all(expert_out.reshape(req_count * blk_count, pad_rows, feat_l...  6.12 us
    dot_general x1, matrix products, body(): jnp.dot(pick.astype(jnp.bfloat16), normed, preferred_element_type=jnp.flo...  4.57 us
  transfers between devices with their start and end apart: 6, of which 2 were waited for; matrix products, arithmetic and copies ran while one was open for 14% of the time, Pallas kernels for 0%

profile of v12, /device:TPU:2, one launch (start us, length us, event | category | flops | bytes accessed | tf_op | source)
XLA Modules:
  0.0 205.4 jit_solution(10173045679086986951)
XLA Ops:
  2.5 2.4 %collective-permute-done.1 = bf16[512,768]{1,0:T(8,128)(2,1)} collective-permute-done((bf16[512,768]{1,0:T(8,128)(2,1)}, bf16[512,768]{1,0:T(8,128)(2,1)}, u32[]{:S(2)}, u32[]{:S(2)}) %collective-permute-start.1) | collective-permute-done | bytes 786464 | tf_op jit(solution)/shard_map/ppermute | solution.py:10
  4.9 1.5 select_bitcast_fusion.4
  6.6 1.2 copy-done.2
  8.4 1.1 broadcast_in_dim.42
  9.5 4.6 %fusion.3 = bf16[4096,768]{1,0:T(8,128)(2,1)S(1)} fusion(bf16[512,768]{1,0:T(8,128)(2,1)S(1)} %copy-done.3, s32[4096,512]{1,0:T(8,128)S(1)} %bitcast.77, s32[4096]{0:T(1024)S(1)} %fusion.53), kind=kOutput, calls=%fused_computation.5 | convolution fusion | flops 3226468352 | bytes 15482880 | tf_op jit(solution)/shard_map/dot_general | solution.py:72
  14.1 85.3 %all_to_all.10 = bf16[128,32,768]{2,1,0:T(8,128)(2,1)S(1)} all-to-all(bf16[128,32,768]{2,1,0:T(8,128)(2,1)S(1)} %bitcast.79), channel_id=1, replica_groups=mesh['req'=64,'blk'=2] {'req','blk'}, dimensions={0} | all-to-all | bytes 12582912 | tf_op jit(solution)/shard_map/all_to_all | solution.py:76
  99.3 7.2 %convolution_bitcast_fusion = f32[64,32,1024]{2,1,0:T(8,128)S(1)} fusion(bf16[64,2,32,768]{3,2,1,0:T(8,128)(2,1)S(1)} %bitcast.78, bf16[2,768,1024]{2,1,0:T(8,128)(2,1)S(1)} %pad_maximum_fusion.1), kind=kOutput, calls=%fused_computation.12 | convolution fusion | flops 6442450944 | bytes 17825792 | tf_op jit(solution)/shard_map/gcsd,cdf->gsf/dot_general | solution.py:86
  106.5 1.5 fusion.6
  108.0 1.8 convolution_convert_fusion
  109.8 1.8 convolution_convert_fusion.1
  111.6 3.2 %pad_maximum_fusion = bf16[64,2,32,768]{3,2,1,0:T(8,128)(2,1)} fusion(bf16[64,1,32,768]{3,2,1,0:T(8,128)(2,1)S(1)} %bitcast.82, bf16[64,1,32,768]{3,2,1,0:T(8,128)(2,1)S(1)} %bitcast.83), kind=kLoop, calls=%fused_computation.6 | loop fusion | flops 3145728 | bytes 12582912 | tf_op jit(solution)/shard_map/stack | solution.py:96
  114.9 6.1 %all-to-all-start.1 = ((bf16[128,32,768]{2,1,0:T(8,128)(2,1)}), bf16[128,32,768]{2,1,0:T(8,128)(2,1)}, u32[]{:S(2)}, u32[]{:S(2)}) async-start(bf16[128,32,768]{2,1,0:T(8,128)(2,1)} %bitcast.76), calls=%async_computation.1 | async-start | bytes 12582912 | tf_op jit(solution)/shard_map/all_to_all | solution.py:105
  121.6 4.4 %copy.35 = bf16[192,8,2,512]{3,1,2,0:T(8,128)(2,1)} copy(bf16[192,8,2,512]{3,2,1,0:T(2,128)(2,1)} %bitcast.80) | data formatting | bytes 6291456
  127.3 1.2 copy.27
  128.5 1.9 pad_maximum_fusion.6
  130.9 1.8 fusion.11
  132.7 2.2 %convolution_convert_fusion.2 = bf16[512,1536]{1,0:T(8,128)(2,1)} fusion(bf16[512,1536]{1,0:T(8,128)(2,1)S(1)} %copy-done, f32[512,1024]{1,0:T(8,128)S(1)} %fusion.11), kind=kOutput, calls=%fused_computation.15 | convolution fusion | flops 807665664 | bytes 5242880 | tf_op jit(solution)/shard_map/dot_general | solution.py:138
  134.9 3.6 %reshape.151 = bf16[512,2,768]{2,1,0:T(2,128)(2,1)S(1)} reshape(bf16[512,1536]{1,0:T(8,128)(2,1)} %convolution_convert_fusion.2) | data formatting | bytes 3145728 | tf_op jit(solution)/shard_map/reshape | solution.py:139
  138.5 2.2 %fusion.61 = (bf16[512,1,768]{2,1,0:T(2,128)(2,1)S(1)}, bf16[512,1,768]{2,1,0:T(2,128)(2,1)S(1)}) fusion(bf16[512,2,768]{2,1,0:T(2,128)(2,1)S(1)} %reshape.151), kind=kLoop, calls=%fused_computation.114 | loop fusion | bytes 3145728 | tf_op jit(solution)/shard_map/slice | solution.py:141
  141.7 1.2 broadcast_select_fusion.3
  144.1 2.4 %fusion = bf16[512,4096]{0,1:T(8,128)(2,1)} fusion(bf16[512,64]{0,1:T(8,128)(2,1)S(1)} %broadcast_divide_fusion, s32[4096]{0:T(1024)S(1)} %fusion.53, s32[512,64]{0,1:T(8,128)S(1)} %get-tuple-element.37), kind=kLoop, calls=%fused_computation.1 | loop fusion | flops 4194304 | bytes 4407296 | tf_op jit(solution)/shard_map/convert_element_type | solution.py:156
  147.2 50.0 %all-to-all-done.1 = bf16[128,32,768]{2,1,0:T(8,128)(2,1)} async-done(((bf16[128,32,768]{2,1,0:T(8,128)(2,1)}), bf16[128,32,768]{2,1,0:T(8,128)(2,1)}, u32[]{:S(2)}, u32[]{:S(2)}) %all-to-all-start.1) | async-done | bytes 6291488 | tf_op jit(solution)/shard_map/all_to_all | solution.py:105
  197.2 7.1 %fusion.63 = f32[512,768]{1,0:T(8,128)S(1)} fusion(bf16[512,4096]{0,1:T(8,128)(2,1)} %fusion, bf16[4096,768]{1,0:T(8,128)(2,1)} %bitcast.34), kind=kOutput, calls=%fused_computation.116 | convolution fusion | flops 3221225472 | bytes 12058624 | tf_op jit(solution)/shard_map/dot_general | solution.py:159
  204.3 1.1 add_convert_fusion
  (78 shorter events, 8.2 us)
Async XLA Ops:
  0.0 132.7 %copy-start = (bf16[512,1536]{1,0:T(8,128)(2,1)S(1)}, bf16[512,1536]{1,0:T(8,128)(2,1)}, u32[]{:S(2)}) copy-start(bf16[512,1536]{1,0:T(8,128)(2,1)} %param.16) | copy-start | bytes 4718596
  0.0 6.6 %collective-permute-start = (bf16[768,1024]{1,0:T(8,128)(2,1)}, bf16[768,1024]{1,0:T(8,128)(2,1)S(1)}, u32[]{:S(2)}, u32[]{:S(2)}) collective-permute-start(bf16[768,1024]{1,0:T(8,128)(2,1)} %bitcast.86), channel_id=1, source_target_pairs={{0,1},{1,0},{2,3},{3,2},{4,5},{5,4},{6,7},{7,6},{8,9},{9,8},{10,11... | collective-permute-start | bytes 4718600 | tf_op jit(solution)/shard_map/ppermute | solution.py:10
  0.0 4.9 %collective-permute-start.1 = (bf16[512,768]{1,0:T(8,128)(2,1)}, bf16[512,768]{1,0:T(8,128)(2,1)}, u32[]{:S(2)}, u32[]{:S(2)}) collective-permute-start(bf16[512,768]{1,0:T(8,128)(2,1)} %bitcast.87), channel_id=1, source_target_pairs={{0,1},{1,0},{2,3},{3,2},{4,5},{5,4},{6,7},{7,6},{8,9},{9,8},{10,11... | collective-permute-start | bytes 2359304 | tf_op jit(solution)/shard_map/ppermute | solution.py:10
  1.5 4.9 %copy-start.10 = (s32[512,1]{0,1:T(1,128)}, s32[512,1]{0,1:T(1,128)S(1)}, u32[]{:S(2)}) copy-start(s32[512,1]{0,1:T(1,128)S(1)} %get-tuple-element.31) | copy-start | bytes 6148
  1.5 4.9 %copy-start.12 = (s32[512,1]{0,1:T(1,128)}, s32[512,1]{0,1:T(1,128)S(1)}, u32[]{:S(2)}) copy-start(s32[512,1]{0,1:T(1,128)S(1)} %get-tuple-element.32) | copy-start | bytes 6148
  1.5 4.9 %copy-start.14 = (s32[512,1]{0,1:T(1,128)}, s32[512,1]{0,1:T(1,128)S(1)}, u32[]{:S(2)}) copy-start(s32[512,1]{0,1:T(1,128)S(1)} %get-tuple-element.33) | copy-start | bytes 6148
  1.5 4.9 %copy-start.16 = (s32[512,1]{0,1:T(1,128)}, s32[512,1]{0,1:T(1,128)S(1)}, u32[]{:S(2)}) copy-start(s32[512,1]{0,1:T(1,128)S(1)} %get-tuple-element.34) | copy-start | bytes 6148
  1.5 4.9 %copy-start.18 = (s32[512,1]{0,1:T(1,128)}, s32[512,1]{0,1:T(1,128)S(1)}, u32[]{:S(2)}) copy-start(s32[512,1]{0,1:T(1,128)S(1)} %get-tuple-element.35) | copy-start | bytes 6148
  1.5 4.9 %copy-start.20 = (s32[512,1]{0,1:T(1,128)}, s32[512,1]{0,1:T(1,128)S(1)}, u32[]{:S(2)}) copy-start(s32[512,1]{0,1:T(1,128)S(1)} %get-tuple-element.36) | copy-start | bytes 6148
  6.4 1.4 copy-start.2
  114.9 6.6 %copy-start.25 = (s32[1,4]{1,0:T(1,128)S(1)}, s32[1,4]{1,0:T(1,128)}, u32[]{:S(2)}) copy-start(s32[1,4]{1,0:T(1,128)} %param.19) | copy-start | bytes 52
  114.9 82.3 %all-to-all-start.1 = ((bf16[128,32,768]{2,1,0:T(8,128)(2,1)}), bf16[128,32,768]{2,1,0:T(8,128)(2,1)}, u32[]{:S(2)}, u32[]{:S(2)}) async-start(bf16[128,32,768]{2,1,0:T(8,128)(2,1)} %bitcast.76), calls=%async_computation.1 | async-start | bytes 12582912 | tf_op jit(solution)/shard_map/all_to_all | solution.py:105
  121.0 9.8 %collective-permute-start.2 = (bf16[512,768]{1,0:T(8,128)(2,1)S(1)}, bf16[512,768]{1,0:T(8,128)(2,1)S(1)}, u32[]{:S(2)}, u32[]{:S(2)}) collective-permute-start(bf16[512,768]{1,0:T(8,128)(2,1)S(1)} %copy-done.3), channel_id=1, source_target_pairs={{0,1},{1,0},{2,3},{3,2},{4,5},{5,4},{6,7},{7,6},{8,9},{9,8},{10,11... | collective-permute-start | bytes 2359304 | tf_op jit(solution)/shard_map/ppermute | solution.py:10
  121.6 5.1 %copy-start.23 = (s32[1,4]{1,0:T(1,128)S(1)}, s32[1,4]{1,0:T(1,128)}, u32[]{:S(2)}) copy-start(s32[1,4]{1,0:T(1,128)} %param.20) | copy-start | bytes 52
  128.5 2.4 %copy-start.1 = (bf16[192,8,2,512]{3,1,2,0:T(8,128)(2,1)S(1)}, bf16[192,8,2,512]{3,1,2,0:T(8,128)(2,1)}, u32[]{:S(2)}) copy-start(bf16[192,8,2,512]{3,1,2,0:T(8,128)(2,1)} %copy.35) | copy-start | bytes 9437188
  130.4 10.8 %collective-permute-start.3 = (bf16[768,320]{0,1:T(8,128)(2,1)}, bf16[768,320]{0,1:T(8,128)(2,1)}, u32[]{:S(2)}, u32[]{:S(2)}) collective-permute-start(bf16[768,320]{0,1:T(8,128)(2,1)} %pad_maximum_fusion.6), channel_id=1, source_target_pairs={{0,1},{1,0},{2,3},{3,2},{4,5},{5,4},{6,7},{7,6},{8,9},{9,8},{10,11... | collective-permute-start | bytes 1474568 | tf_op jit(solution)/shard_map/ppermute | solution.py:10
  130.9 1.8 copy-start.4
  130.9 1.8 copy-start.6
  140.8 2.1 %copy-start.5 = (bf16[512,768]{1,0:T(8,128)(2,1)S(1)}, bf16[512,768]{1,0:T(8,128)(2,1)}, u32[]{:S(2)}) copy-start(bf16[512,768]{1,0:T(8,128)(2,1)} %copy-done.4) | copy-start | bytes 2359300
  140.8 2.1 %copy-start.7 = (bf16[512,768]{1,0:T(8,128)(2,1)S(1)}, bf16[512,768]{1,0:T(8,128)(2,1)}, u32[]{:S(2)}) copy-start(bf16[512,768]{1,0:T(8,128)(2,1)} %copy-done.6) | copy-start | bytes 2359300
  141.0 5.5 %collective-permute-start.4 = (bf16[512,768]{1,0:T(8,128)(2,1)S(1)}, bf16[512,768]{1,0:T(8,128)(2,1)S(1)}, u32[]{:S(2)}, u32[]{:S(2)}) collective-permute-start(bf16[512,768]{1,0:T(8,128)(2,1)S(1)} %select_bitcast_fusion.2), channel_id=1, source_target_pairs={{0,1},{1,0},{2,3},{3,2},{4,5},{5,4},{6,7},{7,6},{8,9},{9,8},{10,11... | collective-permute-start | bytes 2359304 | tf_op jit(solution)/shard_map/ppermute | solution.py:10
  144.1 2.4 %copy-start.22 = (s32[512]{0:T(512)S(1)}, s32[512]{0:T(512)}, u32[]{:S(2)}) copy-start(s32[512]{0:T(512)} %select_reduce_fusion) | copy-start | bytes 6148
  144.1 2.4 %copy-start.24 = (bf16[256,768]{1,0:T(8,128)(2,1)S(1)}, bf16[256,768]{1,0:T(8,128)(2,1)}, u32[]{:S(2)}) copy-start(bf16[256,768]{1,0:T(8,128)(2,1)} %param.14) | copy-start | bytes 1179652
  144.1 2.4 %copy-start.26 = (s32[256]{0:T(256)S(1)}, s32[256]{0:T(256)}, u32[]{:S(2)}) copy-start(s32[256]{0:T(256)} %and_select_fusion) | copy-start | bytes 3076
  (9 other events, 8.2 us)
